TPU v7x, 32 devices: a whole 2x2x4 slice. The times are simulated.
32 devices in a mesh: energy: 8 (over z, x), dom: 4 (over y, core).
Axes of the slice: x: 2, y: 2, z: 4, core: 2. Of those that a mesh axis runs over, the one named last changes fastest.
Arguments:
- hamiltonian: float32 [4, 256, 256], P('dom'), may hold values from -0.005 to 2.4, as said below
- coupling: float32 [4, 256, 256], P('dom'), may hold values from -0.0025 to 1.05
- deform: float32 [4, 256], P('dom'), may hold values from 0.4 to 1
- green_prev: bfloat16 [8, 4, 2, 256, 256], P('energy', 'dom'), may hold values from -0.78 to 0.78
- energy_grid: float32 [8], replicated, may hold values from -0.03 to 0.03
- slot_energy: int32 [8], replicated, may hold values from 0 to 7, each once
- phonon_offsets: int32 [2, 8], replicated, may hold values from 1 to 3
Outputs:
- green_new: float32 [8, 4, 2, 256, 256], P('energy', 'dom')
Inputs may be any that keep to these rules, and one draw needn't show every extreme that they name: `slot_energy`: each energy point stands in exactly one slot. `hamiltonian`: each block is symmetric.
All inputs are finite; a program needn't handle non-finite values.
Results may differ from a plain program's by a relative error of at most 0.0003.
Values may be sent and summed in bfloat16 or wider, within the bound.
No kernel may reach another device: no remote copies, remote signals or barrier semaphores. Data moves between devices by JAX's collectives and lax.ppermute only.
A program may use at most 64 MiB of HBM per device.

v0:
```python
import jax
import jax.numpy as jnp
from jax import lax
from jax.sharding import PartitionSpec as P

BW = 32


emission_weight = 1.3
absorb_weight = 0.3
couple_scale = 0.04
broaden = 0.02
lead_gamma = 0.1
lead_scale = 0.1


def passed_along(array, axis, by):
    peers = lax.axis_size(axis)
    pairs = [(i, i + by) for i in range(peers) if 0 <= i + by < peers]
    return lax.ppermute(array, axis, pairs)


def symmetric(matrix):
    return 0.5 * (matrix + jnp.swapaxes(matrix, -1, -2))


def invert_pair(block_re, block_im):
    orbitals = block_re.shape[-1]
    eye_mat = jnp.eye(orbitals, dtype=block_re.dtype)
    first_factor = jnp.linalg.cholesky(block_re)
    solved_ratio = jax.scipy.linalg.cho_solve((first_factor, True), block_im)
    merged = symmetric(block_re + jnp.dot(block_im, solved_ratio, precision=lax.Precision.HIGHEST))
    second_factor = jnp.linalg.cholesky(merged)
    inv_re = jax.scipy.linalg.cho_solve((second_factor, True), eye_mat)
    inv_im = jnp.dot(solved_ratio, inv_re, precision=lax.Precision.HIGHEST)
    return (inv_re, inv_im)


def forward_sweep(block_re, block_im, coupling, start_re, start_im):

    def advance(state_pair, slab_data):
        left_re, left_im = state_pair
        own_re, own_im, link_block = slab_data
        inv_re, inv_im = invert_pair(own_re + left_re, own_im + left_im)
        next_re = -symmetric(
            jnp.dot(
                link_block.T,
                jnp.dot(inv_re, link_block, precision=lax.Precision.HIGHEST),
                precision=lax.Precision.HIGHEST,
            )
        )
        next_im = symmetric(
            jnp.dot(
                link_block.T,
                jnp.dot(inv_im, link_block, precision=lax.Precision.HIGHEST),
                precision=lax.Precision.HIGHEST,
            )
        )
        return ((next_re, next_im), (left_re, left_im))

    final_pair, slab_terms = lax.scan(advance, (start_re, start_im), (block_re, block_im, coupling))
    return (slab_terms, final_pair)


def backward_sweep(block_re, block_im, coupling, start_re, start_im):

    def retreat(state_pair, slab_data):
        after_re, after_im = state_pair
        own_re, own_im, link_block = slab_data
        right_re = -symmetric(
            jnp.dot(
                link_block,
                jnp.dot(after_re, link_block.T, precision=lax.Precision.HIGHEST),
                precision=lax.Precision.HIGHEST,
            )
        )
        right_im = symmetric(
            jnp.dot(
                link_block,
                jnp.dot(after_im, link_block.T, precision=lax.Precision.HIGHEST),
                precision=lax.Precision.HIGHEST,
            )
        )
        inv_re, inv_im = invert_pair(own_re + right_re, own_im + right_im)
        return ((inv_re, inv_im), (right_re, right_im))

    final_pair, slab_terms = lax.scan(
        retreat, (start_re, start_im), (block_re, block_im, coupling), reverse=True
    )
    return (slab_terms, final_pair)


def slab_blocks(hamiltonian, coupling, deform, fetched, energy, first_mask, last_mask):
    orbitals = hamiltonian.shape[-1]
    positions = jnp.arange(orbitals)
    distance = jnp.abs(positions[:, None] - positions[None, :]).astype(hamiltonian.dtype)
    profile = jnp.where(distance <= BW, jnp.exp(-2.0 * distance / BW), 0.0)
    weight = couple_scale * deform[:, :, None] * deform[:, None, :] * profile
    mixed_part = symmetric(fetched)
    sigma_re = weight * mixed_part[:, 0]
    sigma_im = weight * mixed_part[:, 1]
    eye_mat = jnp.eye(orbitals, dtype=hamiltonian.dtype)
    lead_term = lead_scale * jnp.matmul(
        jnp.swapaxes(coupling, 1, 2), coupling, precision=lax.Precision.HIGHEST
    )
    block_re = hamiltonian - energy * eye_mat + sigma_re
    block_im = (
        broaden * eye_mat
        - sigma_im
        + first_mask[:, None, None] * lead_gamma * eye_mat
        + last_mask[:, None, None] * lead_term
    )
    return (block_re, block_im)


def partner_levels(energy_level, phonon_offsets, level_count):
    lower_level = energy_level - phonon_offsets[0, energy_level]
    upper_level = energy_level + phonon_offsets[1, energy_level]
    lower_level = jnp.where(lower_level >= 0, lower_level, -1)
    upper_level = jnp.where(upper_level < level_count, upper_level, -1)
    return (lower_level, upper_level)


def body(hamiltonian, coupling, deform, green_prev, energy_grid, slot_energy, phonon_offsets):
    slab_count = hamiltonian.shape[0]
    orbitals = hamiltonian.shape[-1]
    level_count = slot_energy.shape[0]
    dom_count = lax.axis_size("dom")
    dom_index = lax.axis_index("dom")
    own_slot = lax.axis_index("energy")
    energy_level = slot_energy[own_slot]
    energy = energy_grid[energy_level]
    lower_level, upper_level = partner_levels(energy_level, phonon_offsets, level_count)
    weights = emission_weight * (slot_energy == lower_level).astype(jnp.float32) + absorb_weight * (
        slot_energy == upper_level
    ).astype(jnp.float32)
    fetched = jnp.einsum(
        "n,nsabc->sabc",
        weights,
        lax.all_gather(green_prev, "energy", axis=0, tiled=True).astype(jnp.float32),
        precision=lax.Precision.HIGHEST,
    )
    global_index = dom_index * slab_count + jnp.arange(slab_count)
    first_mask = (global_index == 0).astype(jnp.float32)
    last_mask = (global_index == slab_count * dom_count - 1).astype(jnp.float32)
    block_re, block_im = slab_blocks(
        hamiltonian, coupling, deform, fetched, energy, first_mask, last_mask
    )
    zero_block = jnp.zeros((orbitals, orbitals), jnp.float32)
    zero_terms = jnp.zeros((slab_count, orbitals, orbitals), jnp.float32)

    def left_step(active, incoming, held):

        def left_compute():
            terms, outgoing = forward_sweep(block_re, block_im, coupling, incoming[0], incoming[1])
            return (outgoing[0], outgoing[1], terms[0], terms[1])

        def left_keep():
            return held

        return lax.cond(active, left_compute, left_keep)

    def right_step(active, incoming, held):

        def right_compute():
            terms, outgoing = backward_sweep(block_re, block_im, coupling, incoming[0], incoming[1])
            return (outgoing[0], outgoing[1], terms[0], terms[1])

        def right_keep():
            return held

        return lax.cond(active, right_compute, right_keep)

    start_held = (zero_block, zero_block, zero_terms, zero_terms)
    start_in = (zero_block, zero_block)

    def joint_turn(link_turn, carry):
        in_left, held_left, in_right, held_right = carry
        held_left = left_step(link_turn == dom_index, in_left, held_left)
        held_right = right_step(link_turn == dom_count - 1 - dom_index, in_right, held_right)
        in_left = passed_along((held_left[0], held_left[1]), "dom", 1)
        in_right = passed_along((held_right[0], held_right[1]), "dom", -1)
        return (in_left, held_left, in_right, held_right)

    left_in, left_held, right_in, right_held = lax.fori_loop(
        0, dom_count - 1, joint_turn, (start_in, start_held, start_in, start_held)
    )
    left_held = left_step(dom_index == dom_count - 1, left_in, left_held)
    right_held = right_step(dom_index == 0, right_in, right_held)
    inv_re, inv_im = jax.vmap(invert_pair)(
        block_re + left_held[2] + right_held[2], block_im + left_held[3] + right_held[3]
    )
    return jnp.stack([-inv_re, -inv_im], axis=1)[None]


def solution(mesh):
    in_specs = (
        P("dom", None, None),
        P("dom", None, None),
        P("dom", None),
        P("energy", "dom", None, None, None),
        P(),
        P(),
        P(),
    )
    out_specs = P("energy", "dom", None, None, None)
    return jax.shard_map(body, mesh=mesh, in_specs=in_specs, out_specs=out_specs, check_vma=False)
```

profile of v0, /device:TPU:0, one launch (start us, length us, event | category | flops | bytes accessed | tf_op | source)
XLA Modules:
  0.0 820.9 jit_solution(6180285481837184304)
XLA Ops:
  17.2 44.3 %all-gather.2.cloned.1.call-done = bf16[8,1,2,256,256]{4,3,2,1,0:T(8,128)(2,1)} async-done(((bf16[1,1,2,256,256]{4,3,2,1,0:T(8,128)(2,1)}), bf16[8,1,2,256,256]{4,3,2,1,0:T(8,128)(2,1)}) %all-gather.2.cloned.1.call-update) | async-done | bytes 2097168 | tf_op jit(solution)/shard_map/all_gather | solution.py:140
  72.1 605.4 %while.61 = (s32[]{:T(128)}, f32[256,256]{0,1:T(8,128)}, f32[256,256]{0,1:T(8,128)}, f32[256,256]{0,1:T(8,128)}, f32[256,256]{0,1:T(8,128)}, /*index=5*/f32[1,25...) while((s32[]{:T(128)}, f32[256,256]{0,1:T(8,128)}, ...), condition=%wide.region_9.12_spmd, body=%wide.region_0.11_spmd.sunk | while | flops 3829662720 | bytes 55584188 | solution.py:185
  72.6 132.2 %conditional.8 = ((f32[256,256]{0,1:T(8,128)}, f32[256,256]{0,1:T(8,128)}, f32[1,256,256]{2,1,0:T(8,128)S(1)}, f32[1,256,256]{2,1,0:T(8,128)S(1)})) conditional(s32[]{:T(128)} %convert_element_type.80, (f32[256,256]{0,1:T(8,128)}, f32[256,256]{0,1:T(8,128)}, f32[1,256,256]{2,1,0:T(8,128)S(1)}, f32[1,256,256]{2,1,0:T(8,128)S(1)}) %tuple.200, ...), branch_computations={%region_1.1_spmd, %region_2.8_spmd} | conditional | flops 1914864128 | bytes 28447246 | solution.py:161
  74.2 11.7 %cholesky.339 = f32[128,128]{1,0:T(8,128)S(1)} custom-call(f32[128,128]{1,0:T(8,128)S(1)} %copy.50), custom_call_target="Cholesky" | custom-call | tf_op jit(solution)/shard_map/while/body/eval_jaxpr/cond/branch_1_fun/while/body/eval_jaxpr/jit(cholesky)/cholesky | solution.py:30
  86.0 9.8 %custom-call.40 = f32[1,128,128]{1,2,0:T(8,128)S(1)} custom-call(f32[1,128,128]{2,1,0:T(8,128)S(1)} %get-tuple-element.807), custom_call_target="InvertDiagBlocksLowerTriangular" | custom-call | tf_op jit(solution)/shard_map/while/body/eval_jaxpr/cond/branch_1_fun/while/body/eval_jaxpr/jit(cholesky)/cholesky | solution.py:30
  96.5 11.7 %cholesky.356 = f32[128,128]{1,0:T(8,128)S(1)} custom-call(f32[128,128]{1,0:T(8,128)S(1)} %copy.52), custom_call_target="Cholesky" | custom-call | tf_op jit(solution)/shard_map/while/body/eval_jaxpr/cond/branch_1_fun/while/body/eval_jaxpr/jit(cholesky)/cholesky | solution.py:30
  114.2 19.8 %custom-call.41 = f32[2,128,128]{1,2,0:T(8,128)S(1)} custom-call(f32[2,128,128]{2,1,0:T(8,128)S(1)} %get-tuple-element.646), custom_call_target="InvertDiagBlocksLowerTriangular" | custom-call | tf_op jit(solution)/shard_map/while/body/eval_jaxpr/cond/branch_1_fun/while/body/eval_jaxpr/jit(_cho_solve)/triangular_solve | solution.py:31
  137.8 11.7 %cholesky.373 = f32[128,128]{1,0:T(8,128)S(1)} custom-call(f32[128,128]{1,0:T(8,128)S(1)} %cholesky.540), custom_call_target="Cholesky" | custom-call | tf_op jit(solution)/shard_map/while/body/eval_jaxpr/cond/branch_1_fun/while/body/eval_jaxpr/jit(cholesky)/cholesky | solution.py:33
  159.9 11.9 %cholesky.390 = f32[128,128]{1,0:T(8,128)S(1)} custom-call(f32[128,128]{1,0:T(8,128)S(1)} %convolution_subtract_fusion.4), custom_call_target="Cholesky" | custom-call | tf_op jit(solution)/shard_map/while/body/eval_jaxpr/cond/branch_1_fun/while/body/eval_jaxpr/jit(cholesky)/cholesky | solution.py:33
  178.8 19.7 %custom-call.43 = f32[2,128,128]{1,2,0:T(8,128)S(1)} custom-call(f32[2,128,128]{2,1,0:T(8,128)S(1)} %get-tuple-element.647), custom_call_target="InvertDiagBlocksLowerTriangular" | custom-call | tf_op jit(solution)/shard_map/while/body/eval_jaxpr/cond/branch_1_fun/while/body/eval_jaxpr/jit(_cho_solve)/triangular_solve | solution.py:34
  225.5 17.1 %conditional.8 = ((f32[256,256]{0,1:T(8,128)}, f32[256,256]{0,1:T(8,128)}, f32[1,256,256]{2,1,0:T(8,128)S(1)}, f32[1,256,256]{2,1,0:T(8,128)S(1)})) conditional(s32[]{:T(128)} %convert_element_type.80, (f32[256,256]{0,1:T(8,128)}, f32[256,256]{0,1:T(8,128)}, f32[1,256,256]{2,1,0:T(8,128)S(1)}, f32[1,256,256]{2,1,0:T(8,128)S(1)}) %tuple.200, ...), branch_computations={%region_1.1_spmd, %region_2.8_spmd} | conditional | flops 1914864128 | bytes 28447246 | solution.py:161
  242.6 118.7 %collective-permute-start = (f32[256,256]{0,1:T(8,128)}, f32[256,256]{0,1:T(8,128)}, u32[]{:S(2)}, u32[]{:S(2)}) collective-permute-start(f32[256,256]{0,1:T(8,128)} %get-tuple-element.1270), channel_id=1, source_target_pairs={{0,1},{1,2},{2,3},{4,5},{5,6},{6,7},{8,9},{9,10},{10,11},{12,13},{... | collective-permute-start | bytes 786440 | tf_op jit(solution)/shard_map/while/body/eval_jaxpr/ppermute | solution.py:20
  375.1 17.2 %conditional.8 = ((f32[256,256]{0,1:T(8,128)}, f32[256,256]{0,1:T(8,128)}, f32[1,256,256]{2,1,0:T(8,128)S(1)}, f32[1,256,256]{2,1,0:T(8,128)S(1)})) conditional(s32[]{:T(128)} %convert_element_type.80, (f32[256,256]{0,1:T(8,128)}, f32[256,256]{0,1:T(8,128)}, f32[1,256,256]{2,1,0:T(8,128)S(1)}, f32[1,256,256]{2,1,0:T(8,128)S(1)}) %tuple.200, ...), branch_computations={%region_1.1_spmd, %region_2.8_spmd} | conditional | flops 1914864128 | bytes 28447246 | solution.py:161
  392.4 30.9 %collective-permute-start = (f32[256,256]{0,1:T(8,128)}, f32[256,256]{0,1:T(8,128)}, u32[]{:S(2)}, u32[]{:S(2)}) collective-permute-start(f32[256,256]{0,1:T(8,128)} %get-tuple-element.1270), channel_id=1, source_target_pairs={{0,1},{1,2},{2,3},{4,5},{5,6},{6,7},{8,9},{9,10},{10,11},{12,13},{... | collective-permute-start | bytes 786440 | tf_op jit(solution)/shard_map/while/body/eval_jaxpr/ppermute | solution.py:20
  423.2 116.9 %collective-permute-start.1 = (f32[256,256]{0,1:T(8,128)}, f32[256,256]{0,1:T(8,128)}, u32[]{:S(2)}, u32[]{:S(2)}) collective-permute-start(f32[256,256]{0,1:T(8,128)} %get-tuple-element.1271), channel_id=1, source_target_pairs={{0,1},{1,2},{2,3},{4,5},{5,6},{6,7},{8,9},{9,10},{10,11},{12,13},{... | collective-permute-start | bytes 786440 | tf_op jit(solution)/shard_map/while/body/eval_jaxpr/ppermute | solution.py:20
  544.1 129.0 %collective-permute-done.2 = f32[256,256]{1,0:T(8,128)S(1)} collective-permute-done((f32[256,256]{1,0:T(8,128)}, f32[256,256]{1,0:T(8,128)S(1)}, u32[]{:S(2)}, u32[]{:S(2)}) %collective-permute-start.2) | collective-permute-done | bytes 262176 | tf_op jit(solution)/shard_map/while/body/eval_jaxpr/ppermute | solution.py:20
  687.2 11.7 %custom-call.48 = f32[1,128,128]{2,1,0:T(8,128)S(1)} custom-call(f32[1,128,128]{2,1,0:T(8,128)S(1)} %copy.81), custom_call_target="Cholesky" | custom-call | tf_op jit(solution)/shard_map/vmap(jit(cholesky))/cholesky | solution.py:30
  699.0 9.8 %custom-call.49 = f32[1,1,128,128]{2,3,1,0:T(8,128)S(1)} custom-call(f32[1,1,128,128]{3,2,1,0:T(8,128)S(1)} %get-tuple-element.845), custom_call_target="InvertDiagBlocksLowerTriangular" | custom-call | tf_op jit(solution)/shard_map/vmap(jit(cholesky))/cholesky | solution.py:30
  709.4 11.7 %custom-call.50 = f32[1,128,128]{2,1,0:T(8,128)S(1)} custom-call(f32[1,128,128]{2,1,0:T(8,128)S(1)} %copy.83), custom_call_target="Cholesky" | custom-call | tf_op jit(solution)/shard_map/vmap(jit(cholesky))/cholesky | solution.py:30
  728.0 19.8 %custom-call.52 = f32[1,2,128,128]{2,3,1,0:T(8,128)S(1)} custom-call(f32[1,2,128,128]{3,2,1,0:T(8,128)S(1)} %bitcast.499), custom_call_target="InvertDiagBlocksLowerTriangular" | custom-call | tf_op jit(solution)/shard_map/vmap(jit(_cho_solve))/triangular_solve/custom-call.8 | solution.py:31
  750.4 11.7 %custom-call.53 = f32[1,128,128]{2,1,0:T(8,128)S(1)} custom-call(f32[1,128,128]{2,1,0:T(8,128)S(1)} %cholesky.552), custom_call_target="Cholesky" | custom-call | tf_op jit(solution)/shard_map/vmap(jit(cholesky))/cholesky | solution.py:33
  762.2 9.8 %custom-call.54 = f32[1,1,128,128]{2,3,1,0:T(8,128)S(1)} custom-call(f32[1,1,128,128]{3,2,1,0:T(8,128)S(1)} %get-tuple-element.841), custom_call_target="InvertDiagBlocksLowerTriangular" | custom-call | tf_op jit(solution)/shard_map/vmap(jit(cholesky))/cholesky | solution.py:33
  772.5 11.7 %custom-call.55 = f32[1,128,128]{2,1,0:T(8,128)S(1)} custom-call(f32[1,128,128]{2,1,0:T(8,128)S(1)} %fusion.115), custom_call_target="Cholesky" | custom-call | tf_op jit(solution)/shard_map/vmap(jit(cholesky))/cholesky | solution.py:33
  791.2 19.7 %custom-call.57 = f32[1,2,128,128]{2,3,1,0:T(8,128)S(1)} custom-call(f32[1,2,128,128]{3,2,1,0:T(8,128)S(1)} %bitcast.498), custom_call_target="InvertDiagBlocksLowerTriangular" | custom-call | tf_op jit(solution)/shard_map/vmap(jit(_cho_solve))/triangular_solve/custom-call.8 | solution.py:34
  (216 shorter events, 130.7 us)
Async XLA Ops:
  6.5 55.0 %all-gather.2.cloned.1.call-start = ((), (), s32[]{:S(2)}) async-start(), calls=%async_computation | async-start | bytes 2359296 | tf_op jit(solution)/shard_map/all_gather | solution.py:140
  61.5 4.6 copy-start.11
  61.5 4.6 copy-start.12
  65.7 1.4 copy-start
  66.9 2.3 copy-start.5
  73.8 36.4 %copy-start.1 = (f32[256,256]{1,0:T(8,128)}, f32[256,256]{1,0:T(8,128)S(1)}, u32[]{:S(2)}) copy-start(f32[256,256]{1,0:T(8,128)S(1)} %copy.64) | copy-start | bytes 786436 | tf_op jit(solution)/shard_map/while/body/eval_jaxpr/cond
  135.1 2.3 copy-start.3
  201.7 2.8 copy-start.2
  201.7 2.8 copy-start.4
  204.9 13.9 %collective-permute-start = (f32[256,256]{0,1:T(8,128)}, f32[256,256]{0,1:T(8,128)}, u32[]{:S(2)}, u32[]{:S(2)}) collective-permute-start(f32[256,256]{0,1:T(8,128)} %get-tuple-element.1270), channel_id=1, source_target_pairs={{0,1},{1,2},{2,3},{4,5},{5,6},{6,7},{8,9},{9,10},{10,11},{12,13},{... | collective-permute-start | bytes 786440 | tf_op jit(solution)/shard_map/while/body/eval_jaxpr/ppermute | solution.py:20
  206.9 11.9 %collective-permute-start.1 = (f32[256,256]{0,1:T(8,128)}, f32[256,256]{0,1:T(8,128)}, u32[]{:S(2)}, u32[]{:S(2)}) collective-permute-start(f32[256,256]{0,1:T(8,128)} %get-tuple-element.1271), channel_id=1, source_target_pairs={{0,1},{1,2},{2,3},{4,5},{5,6},{6,7},{8,9},{9,10},{10,11},{12,13},{... | collective-permute-start | bytes 786440 | tf_op jit(solution)/shard_map/while/body/eval_jaxpr/ppermute | solution.py:20
  216.1 3.6 collective-permute-start.2
  217.4 4.1 collective-permute-start.3
  242.6 124.5 %collective-permute-start = (f32[256,256]{0,1:T(8,128)}, f32[256,256]{0,1:T(8,128)}, u32[]{:S(2)}, u32[]{:S(2)}) collective-permute-start(f32[256,256]{0,1:T(8,128)} %get-tuple-element.1270), channel_id=1, source_target_pairs={{0,1},{1,2},{2,3},{4,5},{5,6},{6,7},{8,9},{9,10},{10,11},{12,13},{... | collective-permute-start | bytes 786440 | tf_op jit(solution)/shard_map/while/body/eval_jaxpr/ppermute | solution.py:20
  361.3 5.9 collective-permute-start.1
  364.5 8.7 %collective-permute-start.2 = (f32[256,256]{1,0:T(8,128)}, f32[256,256]{1,0:T(8,128)S(1)}, u32[]{:S(2)}, u32[]{:S(2)}) collective-permute-start(f32[256,256]{1,0:T(8,128)} %get-tuple-element.1276), channel_id=1, source_target_pairs={{1,0},{2,1},{3,2},{5,4},{6,5},{7,6},{9,8},{10,9},{11,10},{13,12},{... | collective-permute-start | bytes 786440 | tf_op jit(solution)/shard_map/while/body/eval_jaxpr/ppermute | solution.py:20
  365.8 9.1 %collective-permute-start.3 = (f32[256,256]{1,0:T(8,128)S(1)}, f32[256,256]{1,0:T(8,128)S(1)}, u32[]{:S(2)}, u32[]{:S(2)}) collective-permute-start(f32[256,256]{1,0:T(8,128)S(1)} %get-tuple-element.1277), channel_id=1, source_target_pairs={{1,0},{2,1},{3,2},{5,4},{6,5},{7,6},{9,8},{10,9},{11,10},{13,12},{... | collective-permute-start | bytes 786440 | tf_op jit(solution)/shard_map/while/body/eval_jaxpr/ppermute | solution.py:20
  392.4 151.7 %collective-permute-start = (f32[256,256]{0,1:T(8,128)}, f32[256,256]{0,1:T(8,128)}, u32[]{:S(2)}, u32[]{:S(2)}) collective-permute-start(f32[256,256]{0,1:T(8,128)} %get-tuple-element.1270), channel_id=1, source_target_pairs={{0,1},{1,2},{2,3},{4,5},{5,6},{6,7},{8,9},{9,10},{10,11},{12,13},{... | collective-permute-start | bytes 786440 | tf_op jit(solution)/shard_map/while/body/eval_jaxpr/ppermute | solution.py:20
  423.2 120.8 %collective-permute-start.1 = (f32[256,256]{0,1:T(8,128)}, f32[256,256]{0,1:T(8,128)}, u32[]{:S(2)}, u32[]{:S(2)}) collective-permute-start(f32[256,256]{0,1:T(8,128)} %get-tuple-element.1271), channel_id=1, source_target_pairs={{0,1},{1,2},{2,3},{4,5},{5,6},{6,7},{8,9},{9,10},{10,11},{12,13},{... | collective-permute-start | bytes 786440 | tf_op jit(solution)/shard_map/while/body/eval_jaxpr/ppermute | solution.py:20
  541.5 131.7 %collective-permute-start.2 = (f32[256,256]{1,0:T(8,128)}, f32[256,256]{1,0:T(8,128)S(1)}, u32[]{:S(2)}, u32[]{:S(2)}) collective-permute-start(f32[256,256]{1,0:T(8,128)} %get-tuple-element.1276), channel_id=1, source_target_pairs={{1,0},{2,1},{3,2},{5,4},{6,5},{7,6},{9,8},{10,9},{11,10},{13,12},{... | collective-permute-start | bytes 786440 | tf_op jit(solution)/shard_map/while/body/eval_jaxpr/ppermute | solution.py:20
  542.8 132.1 %collective-permute-start.3 = (f32[256,256]{1,0:T(8,128)S(1)}, f32[256,256]{1,0:T(8,128)S(1)}, u32[]{:S(2)}, u32[]{:S(2)}) collective-permute-start(f32[256,256]{1,0:T(8,128)S(1)} %get-tuple-element.1277), channel_id=1, source_target_pairs={{1,0},{2,1},{3,2},{5,4},{6,5},{7,6},{9,8},{10,9},{11,10},{13,12},{... | collective-permute-start | bytes 786440 | tf_op jit(solution)/shard_map/while/body/eval_jaxpr/ppermute | solution.py:20
  677.6 9.2 %copy-start.6 = (f32[1,256,256]{2,1,0:T(8,128)S(1)}, f32[1,256,256]{2,1,0:T(8,128)}, u32[]{:S(2)}) copy-start(f32[1,256,256]{2,1,0:T(8,128)} %copy-done.5) | copy-start | bytes 786436
  677.6 9.2 %copy-start.10 = (f32[1,256,256]{2,1,0:T(8,128)S(1)}, f32[1,256,256]{2,1,0:T(8,128)}, u32[]{:S(2)}) copy-start(f32[1,256,256]{2,1,0:T(8,128)} %copy-done.9) | copy-start | bytes 786436
  750.2 60.7 %copy-start.7 = (f32[1,256,256]{2,1,0:T(8,128)S(1)}, f32[1,256,256]{2,1,0:T(8,128)}, u32[]{:S(2)}) copy-start(f32[1,256,256]{2,1,0:T(8,128)} %fusion.129) | copy-start | bytes 786436
  (1 other events, 0.7 us)
Sparse Core Ops, SparseCore 0:
  9.5 51.9 all-gather.1
where the time goes:
time: 831 us; the launch traced here: 821 us
  starting transfers between devices  280 us (34%)
  other arithmetic  222 us (27%)
  waiting for transfers between devices  186 us (22%)
  loops' own time  62.3 us (7%)
  local copies, waits for them, and re-layouts  29.2 us (4%)
  between operations  21.2 us (3%)
  matrix products  19.2 us (2%)
    ppermute x12, starting transfers between devices, passed_along(): return lax.ppermute(array, axis, pairs)  280 us
    ppermute x12, waiting for transfers between devices, passed_along(): return lax.ppermute(array, axis, pairs)  141 us
    another operation x14, other arithmetic, invert_pair(): second_factor = jnp.linalg.cholesky(merged)  69.5 us
    another operation x13, other arithmetic, invert_pair(): first_factor = jnp.linalg.cholesky(block_re)  68.7 us
    all_gather x1, waiting for transfers between devices, body(): lax.all_gather(green_prev, 'energy', axis=0, tiled=True).astype(jnp.float32)  44.3 us
    another operation x6, other arithmetic, invert_pair(): solved_ratio = jax.scipy.linalg.cho_solve((first_factor, True), block_im)  39.8 us
    another operation x4, other arithmetic, invert_pair(): inv_re = jax.scipy.linalg.cho_solve((second_factor, True), eye_mat)  39.4 us
    another operation x4, loops' own time, left_step(): return lax.cond(active, left_compute, left_keep)  37.7 us
  transfers between devices with their start and end apart: 13, of which 7 were waited for; matrix products, arithmetic and copies ran while one was open for 1% of the time, Pallas kernels for 0%

commit v1 on v0

v1 whole, which is shorter than its diff:
```python
import jax
import jax.numpy as jnp
from jax import lax
from jax.sharding import PartitionSpec as P

BW = 32


emission_weight = 1.3
absorb_weight = 0.3
couple_scale = 0.04
broaden = 0.02
lead_gamma = 0.1
lead_scale = 0.1

HI = lax.Precision.HIGHEST


def symmetric(matrix):
    return 0.5 * (matrix + jnp.swapaxes(matrix, -1, -2))


def invert_pair(block_re, block_im):
    orbitals = block_re.shape[-1]
    eye_mat = jnp.eye(orbitals, dtype=block_re.dtype)
    first_factor = jnp.linalg.cholesky(block_re)
    solved_ratio = jax.scipy.linalg.cho_solve((first_factor, True), block_im)
    merged = symmetric(block_re + jnp.dot(block_im, solved_ratio, precision=HI))
    second_factor = jnp.linalg.cholesky(merged)
    inv_re = jax.scipy.linalg.cho_solve((second_factor, True), eye_mat)
    inv_im = jnp.dot(solved_ratio, inv_re, precision=HI)
    return (inv_re, inv_im)


def slab_blocks(hamiltonian, coupling, deform, fetched, energy, first_mask, last_mask):
    orbitals = hamiltonian.shape[-1]
    positions = jnp.arange(orbitals)
    distance = jnp.abs(positions[:, None] - positions[None, :]).astype(hamiltonian.dtype)
    profile = jnp.where(distance <= BW, jnp.exp(-2.0 * distance / BW), 0.0)
    weight = couple_scale * deform[:, :, None] * deform[:, None, :] * profile
    mixed_part = symmetric(fetched)
    sigma_re = weight * mixed_part[:, 0]
    sigma_im = weight * mixed_part[:, 1]
    eye_mat = jnp.eye(orbitals, dtype=hamiltonian.dtype)
    lead_term = lead_scale * jnp.matmul(jnp.swapaxes(coupling, 1, 2), coupling, precision=HI)
    block_re = hamiltonian - energy * eye_mat + sigma_re
    block_im = (
        broaden * eye_mat
        - sigma_im
        + first_mask[:, None, None] * lead_gamma * eye_mat
        + last_mask[:, None, None] * lead_term
    )
    return (block_re, block_im)


def partner_levels(energy_level, phonon_offsets, level_count):
    lower_level = energy_level - phonon_offsets[0, energy_level]
    upper_level = energy_level + phonon_offsets[1, energy_level]
    lower_level = jnp.where(lower_level >= 0, lower_level, -1)
    upper_level = jnp.where(upper_level < level_count, upper_level, -1)
    return (lower_level, upper_level)


def body(hamiltonian, coupling, deform, green_prev, energy_grid, slot_energy, phonon_offsets):
    local_slabs = hamiltonian.shape[0]
    level_count = slot_energy.shape[0]
    dom_count = lax.axis_size("dom")
    dom_index = lax.axis_index("dom")
    slab_total = local_slabs * dom_count
    own_slot = lax.axis_index("energy")
    energy_level = slot_energy[own_slot]
    energy = energy_grid[energy_level]
    lower_level, upper_level = partner_levels(energy_level, phonon_offsets, level_count)
    weights = emission_weight * (slot_energy == lower_level).astype(jnp.float32) + absorb_weight * (
        slot_energy == upper_level
    ).astype(jnp.float32)
    fetched = jnp.einsum(
        "n,nsabc->sabc",
        weights,
        lax.all_gather(green_prev, "energy", axis=0, tiled=True).astype(jnp.float32),
        precision=HI,
    )
    global_index = dom_index * local_slabs + jnp.arange(local_slabs)
    first_mask = (global_index == 0).astype(jnp.float32)
    last_mask = (global_index == slab_total - 1).astype(jnp.float32)
    block_re, block_im = slab_blocks(
        hamiltonian, coupling, deform, fetched, energy, first_mask, last_mask
    )
    gathered = lax.all_gather(
        jnp.stack([block_re, block_im, coupling]), "dom", axis=1, tiled=True
    )
    all_re, all_im, all_link = gathered[0], gathered[1], gathered[2]
    orbitals = hamiltonian.shape[-1]
    zero_block = jnp.zeros((orbitals, orbitals), jnp.float32)

    outputs = []
    for local in range(local_slabs):
        own = dom_index * local_slabs + local

        def chain_step(step, carry):
            left_re, left_im, right_re, right_im = carry
            is_left = step < own
            slab = jnp.where(is_left, step, slab_total - 1 - step + own)
            acc_re = jnp.where(is_left, left_re, right_re)
            acc_im = jnp.where(is_left, left_im, right_im)
            inv_re, inv_im = invert_pair(all_re[slab] + acc_re, all_im[slab] + acc_im)
            link_index = jnp.where(is_left, step, jnp.maximum(slab - 1, 0))
            link_block = all_link[link_index]
            link_block = jnp.where(is_left, link_block, link_block.T)
            next_re = -symmetric(
                jnp.dot(link_block.T, jnp.dot(inv_re, link_block, precision=HI), precision=HI)
            )
            next_im = symmetric(
                jnp.dot(link_block.T, jnp.dot(inv_im, link_block, precision=HI), precision=HI)
            )
            left_re = jnp.where(is_left, next_re, left_re)
            left_im = jnp.where(is_left, next_im, left_im)
            right_re = jnp.where(is_left, right_re, next_re)
            right_im = jnp.where(is_left, right_im, next_im)
            return (left_re, left_im, right_re, right_im)

        left_re, left_im, right_re, right_im = lax.fori_loop(
            0, slab_total - 1, chain_step, (zero_block, zero_block, zero_block, zero_block)
        )
        inv_re, inv_im = invert_pair(
            block_re[local] + left_re + right_re, block_im[local] + left_im + right_im
        )
        outputs.append(jnp.stack([-inv_re, -inv_im]))
    return jnp.stack(outputs)[None]


def solution(mesh):
    in_specs = (
        P("dom", None, None),
        P("dom", None, None),
        P("dom", None),
        P("energy", "dom", None, None, None),
        P(),
        P(),
        P(),
    )
    out_specs = P("energy", "dom", None, None, None)
    return jax.shard_map(body, mesh=mesh, in_specs=in_specs, out_specs=out_specs, check_vma=False)
```

time: 831 us -> 662 us (0.80)
  starting transfers between devices: 280 us -> 0.04 us
  other arithmetic: 222 us -> 443 us
  waiting for transfers between devices: 186 us -> 72.2 us
  loops' own time: 62.3 us -> 39.1 us
  local copies, waits for them, and re-layouts: 29.2 us -> 49.9 us
  matrix products: 19.2 us -> 31.1 us
    ppermute x12 -> x0, starting transfers between devices: 280 us -> none  [passed_along(): return lax.ppermute(array, axis, pairs)]
    ppermute x12 -> x0, waiting for transfers between devices: 141 us -> none  [passed_along(): return lax.ppermute(array, axis, pairs)]
    another operation x14 -> x28, other arithmetic: 69.5 us -> 139 us  [invert_pair(): second_factor = jnp.linalg.cholesky(merged)]
    another operation x13 -> x24, other arithmetic: 68.7 us -> 136 us  [invert_pair(): first_factor = jnp.linalg.cholesky(block_re)]
    another operation x4 -> x8, other arithmetic: 39.4 us -> 78.8 us  [invert_pair(): inv_re = jax.scipy.linalg.cho_solve((second_factor, True), eye_mat)]
    another operation x6 -> x12, other arithmetic: 39.8 us -> 79 us  [invert_pair(): solved_ratio = jax.scipy.linalg.cho_solve((first_factor, True), block_im)]
    all_gather x0 -> x1, waiting for transfers between devices: none -> 26.4 us  [body(): lax.all_gather(jnp.stack([block_re, block_im, coupling]), 'dom', axis=1,...]
    another operation x9 -> x1, loops' own time: 61.9 us -> 38.6 us  [body(): lax.fori_loop(0, slab_total - 1, chain_step, (zero_block, zero_block, zer...]
  transfers between devices with their start and end apart: 13 -> 2, of which waited for: 7 -> 2; matrix products, arithmetic and copies ran while one was open for 1% -> 1% of each run, Pallas kernels for 0% -> 0%
where the time goes in v1:
time: 662 us; the launch traced here: 657 us
  other arithmetic  443 us (67%)
  waiting for transfers between devices  72.2 us (11%)
  local copies, waits for them, and re-layouts  49.9 us (8%)
  loops' own time  39.1 us (6%)
  matrix products  31.1 us (5%)
  between operations  21.3 us (3%)
    another operation x28, other arithmetic, invert_pair(): second_factor = jnp.linalg.cholesky(merged)  139 us
    another operation x24, other arithmetic, invert_pair(): first_factor = jnp.linalg.cholesky(block_re)  136 us
    another operation x12, other arithmetic, invert_pair(): solved_ratio = jax.scipy.linalg.cho_solve((first_factor, True), block_im)  79 us
    another operation x8, other arithmetic, invert_pair(): inv_re = jax.scipy.linalg.cho_solve((second_factor, True), eye_mat)  78.8 us
    all_gather x1, waiting for transfers between devices, body(): lax.all_gather(green_prev, 'energy', axis=0, tiled=True).astype(jnp.float32)  45.1 us
    another operation x1, loops' own time, body(): lax.fori_loop(0, slab_total - 1, chain_step, (zero_block, zero_block, zer...  38.6 us
    all_gather x1, waiting for transfers between devices, body(): lax.all_gather(jnp.stack([block_re, block_im, coupling]), 'dom', axis=1,...  26.4 us
    another operation x36, local copies, waits for them, and re-layouts, invert_pair(): solved_ratio = jax.scipy.linalg.cho_solve((first_factor, True), block_im)  15.8 us
  transfers between devices with their start and end apart: 2, of which 2 were waited for; matrix products, arithmetic and copies ran while one was open for 1% of the time, Pallas kernels for 0%

profile of v1, /device:TPU:0, one launch (start us, length us, event | category | flops | bytes accessed | tf_op | source)
XLA Modules:
  0.0 657.1 jit_solution(8612224804350294474)
XLA Ops:
  16.4 45.1 %all-gather.3.cloned.1.call-done = bf16[8,1,2,256,256]{4,3,2,1,0:T(8,128)(2,1)} async-done(((bf16[1,1,2,256,256]{4,3,2,1,0:T(8,128)(2,1)}), bf16[8,1,2,256,256]{4,3,2,1,0:T(8,128)(2,1)}) %all-gather.3.cloned.1.call-update) | async-done | bytes 2097168 | tf_op jit(solution)/shard_map/all_gather | solution.py:80
  69.4 26.4 %all-gather.5.cloned.1.call-done = f32[3,4,256,256]{3,2,1,0:T(8,128)} async-done(((f32[3,1,256,256]{3,2,1,0:T(8,128)}), f32[3,4,256,256]{3,2,1,0:T(8,128)}) %all-gather.5.cloned.1.call-update) | async-done | bytes 3145744 | tf_op jit(solution)/shard_map/all_gather | solution.py:89
  99.3 421.5 %while.34 = (s32[]{:T(128)}, f32[256,256]{0,1:T(8,128)S(1)}, f32[256,256]{0,1:T(8,128)S(1)}, f32[256,256]{0,1:T(8,128)S(1)}, f32[256,256]{0,1:T(8,128)S(1)}, /*i...) while((s32[]{:T(128)}, f32[256,256]{0,1:T(8,128)S(1)}, ...), condition=%wide.region_5.8_spmd.clone, body=%wide.region_0.0_spmd.clone.sunk | while | flops 1915847168 | bytes 36311808 | solution.py:122
  121.7 11.7 %cholesky.671 = f32[128,128]{1,0:T(8,128)S(1)} custom-call(f32[128,128]{1,0:T(8,128)S(1)} %cholesky.670), custom_call_target="Cholesky" | custom-call | tf_op jit(solution)/shard_map/while/body/eval_jaxpr/jit(cholesky)/cholesky | solution.py:26
  143.8 11.7 %cholesky.673 = f32[128,128]{1,0:T(8,128)S(1)} custom-call(f32[128,128]{1,0:T(8,128)S(1)} %convolution_subtract_fusion.18), custom_call_target="Cholesky" | custom-call | tf_op jit(solution)/shard_map/while/body/eval_jaxpr/jit(cholesky)/cholesky | solution.py:26
  161.3 19.7 %custom-call.36 = f32[2,128,128]{1,2,0:T(8,128)S(1)} custom-call(f32[2,128,128]{2,1,0:T(8,128)S(1)} %get-tuple-element.604), custom_call_target="InvertDiagBlocksLowerTriangular" | custom-call | tf_op jit(solution)/shard_map/while/body/eval_jaxpr/jit(_cho_solve)/triangular_solve | solution.py:27
  186.2 11.7 %cholesky.676 = f32[128,128]{1,0:T(8,128)S(1)} custom-call(f32[128,128]{1,0:T(8,128)S(1)} %cholesky.675), custom_call_target="Cholesky" | custom-call | tf_op jit(solution)/shard_map/while/body/eval_jaxpr/jit(cholesky)/cholesky | solution.py:29
  208.3 11.7 %cholesky.678 = f32[128,128]{1,0:T(8,128)S(1)} custom-call(f32[128,128]{1,0:T(8,128)S(1)} %convolution_subtract_fusion.21), custom_call_target="Cholesky" | custom-call | tf_op jit(solution)/shard_map/while/body/eval_jaxpr/jit(cholesky)/cholesky | solution.py:29
  226.4 19.7 %custom-call.38 = f32[2,128,128]{1,2,0:T(8,128)S(1)} custom-call(f32[2,128,128]{2,1,0:T(8,128)S(1)} %get-tuple-element.611), custom_call_target="InvertDiagBlocksLowerTriangular" | custom-call | tf_op jit(solution)/shard_map/while/body/eval_jaxpr/jit(_cho_solve)/triangular_solve | solution.py:30
  252.1 11.7 %cholesky.671 = f32[128,128]{1,0:T(8,128)S(1)} custom-call(f32[128,128]{1,0:T(8,128)S(1)} %cholesky.670), custom_call_target="Cholesky" | custom-call | tf_op jit(solution)/shard_map/while/body/eval_jaxpr/jit(cholesky)/cholesky | solution.py:26
  274.2 11.7 %cholesky.673 = f32[128,128]{1,0:T(8,128)S(1)} custom-call(f32[128,128]{1,0:T(8,128)S(1)} %convolution_subtract_fusion.18), custom_call_target="Cholesky" | custom-call | tf_op jit(solution)/shard_map/while/body/eval_jaxpr/jit(cholesky)/cholesky | solution.py:26
  291.8 19.7 %custom-call.36 = f32[2,128,128]{1,2,0:T(8,128)S(1)} custom-call(f32[2,128,128]{2,1,0:T(8,128)S(1)} %get-tuple-element.604), custom_call_target="InvertDiagBlocksLowerTriangular" | custom-call | tf_op jit(solution)/shard_map/while/body/eval_jaxpr/jit(_cho_solve)/triangular_solve | solution.py:27
  316.7 11.7 %cholesky.676 = f32[128,128]{1,0:T(8,128)S(1)} custom-call(f32[128,128]{1,0:T(8,128)S(1)} %cholesky.675), custom_call_target="Cholesky" | custom-call | tf_op jit(solution)/shard_map/while/body/eval_jaxpr/jit(cholesky)/cholesky | solution.py:29
  338.7 11.7 %cholesky.678 = f32[128,128]{1,0:T(8,128)S(1)} custom-call(f32[128,128]{1,0:T(8,128)S(1)} %convolution_subtract_fusion.21), custom_call_target="Cholesky" | custom-call | tf_op jit(solution)/shard_map/while/body/eval_jaxpr/jit(cholesky)/cholesky | solution.py:29
  356.9 19.7 %custom-call.38 = f32[2,128,128]{1,2,0:T(8,128)S(1)} custom-call(f32[2,128,128]{2,1,0:T(8,128)S(1)} %get-tuple-element.611), custom_call_target="InvertDiagBlocksLowerTriangular" | custom-call | tf_op jit(solution)/shard_map/while/body/eval_jaxpr/jit(_cho_solve)/triangular_solve | solution.py:30
  404.7 11.7 %cholesky.673 = f32[128,128]{1,0:T(8,128)S(1)} custom-call(f32[128,128]{1,0:T(8,128)S(1)} %convolution_subtract_fusion.18), custom_call_target="Cholesky" | custom-call | tf_op jit(solution)/shard_map/while/body/eval_jaxpr/jit(cholesky)/cholesky | solution.py:26
  422.2 19.7 %custom-call.36 = f32[2,128,128]{1,2,0:T(8,128)S(1)} custom-call(f32[2,128,128]{2,1,0:T(8,128)S(1)} %get-tuple-element.604), custom_call_target="InvertDiagBlocksLowerTriangular" | custom-call | tf_op jit(solution)/shard_map/while/body/eval_jaxpr/jit(_cho_solve)/triangular_solve | solution.py:27
  469.2 11.7 %cholesky.678 = f32[128,128]{1,0:T(8,128)S(1)} custom-call(f32[128,128]{1,0:T(8,128)S(1)} %convolution_subtract_fusion.21), custom_call_target="Cholesky" | custom-call | tf_op jit(solution)/shard_map/while/body/eval_jaxpr/jit(cholesky)/cholesky | solution.py:29
  487.3 19.7 %custom-call.38 = f32[2,128,128]{1,2,0:T(8,128)S(1)} custom-call(f32[2,128,128]{2,1,0:T(8,128)S(1)} %get-tuple-element.611), custom_call_target="InvertDiagBlocksLowerTriangular" | custom-call | tf_op jit(solution)/shard_map/while/body/eval_jaxpr/jit(_cho_solve)/triangular_solve | solution.py:30
  523.2 11.7 %cholesky.282 = f32[128,128]{1,0:T(8,128)S(1)} custom-call(f32[128,128]{1,0:T(8,128)S(1)} %copy.43), custom_call_target="Cholesky" | custom-call | tf_op jit(solution)/shard_map/jit(cholesky)/cholesky | solution.py:26
  545.5 11.7 %cholesky.299 = f32[128,128]{1,0:T(8,128)S(1)} custom-call(f32[128,128]{1,0:T(8,128)S(1)} %copy.45), custom_call_target="Cholesky" | custom-call | tf_op jit(solution)/shard_map/jit(cholesky)/cholesky | solution.py:26
  563.7 19.9 %custom-call.28 = f32[2,128,128]{1,2,0:T(8,128)S(1)} custom-call(f32[2,128,128]{2,1,0:T(8,128)S(1)} %get-tuple-element.292), custom_call_target="InvertDiagBlocksLowerTriangular" | custom-call | tf_op jit(solution)/shard_map/jit(_cho_solve)/triangular_solve | solution.py:27
  608.6 11.9 %cholesky.333 = f32[128,128]{1,0:T(8,128)S(1)} custom-call(f32[128,128]{1,0:T(8,128)S(1)} %convolution_subtract_fusion.10), custom_call_target="Cholesky" | custom-call | tf_op jit(solution)/shard_map/jit(cholesky)/cholesky | solution.py:29
  627.3 19.7 %custom-call.30 = f32[2,128,128]{1,2,0:T(8,128)S(1)} custom-call(f32[2,128,128]{2,1,0:T(8,128)S(1)} %get-tuple-element.293), custom_call_target="InvertDiagBlocksLowerTriangular" | custom-call | tf_op jit(solution)/shard_map/jit(_cho_solve)/triangular_solve | solution.py:30
  (336 shorter events, 246.3 us)
Async XLA Ops:
  6.5 55.0 %all-gather.3.cloned.1.call-start = ((), (), s32[]{:S(2)}) async-start(), calls=%async_computation | async-start | bytes 2359296 | tf_op jit(solution)/shard_map/all_gather | solution.py:80
  7.3 88.5 %all-gather.5.cloned.1.call-start = ((), (), s32[]{:S(2)}) async-start(), calls=%async_computation.1 | async-start | bytes 3932160 | tf_op jit(solution)/shard_map/all_gather | solution.py:89
  61.5 4.6 copy-start.3
  61.5 4.6 copy-start.7
  65.7 1.3 copy-start.6
  67.6 1.0 copy-start.4
  120.1 60.9 %copy-start = (f32[4,256,256]{2,1,0:T(8,128)}, f32[4,256,256]{2,1,0:T(8,128)S(1)}, u32[]{:S(2)}) copy-start(f32[4,256,256]{2,1,0:T(8,128)S(1)} %get-tuple-element.711) | copy-start | bytes 3145732 | tf_op jit(solution)/shard_map/while
  249.4 1.2 copy-start.1
  250.6 60.9 %copy-start = (f32[4,256,256]{2,1,0:T(8,128)}, f32[4,256,256]{2,1,0:T(8,128)S(1)}, u32[]{:S(2)}) copy-start(f32[4,256,256]{2,1,0:T(8,128)S(1)} %get-tuple-element.711) | copy-start | bytes 3145732 | tf_op jit(solution)/shard_map/while
  379.9 1.2 copy-start.1
  381.1 60.9 %copy-start = (f32[4,256,256]{2,1,0:T(8,128)}, f32[4,256,256]{2,1,0:T(8,128)S(1)}, u32[]{:S(2)}) copy-start(f32[4,256,256]{2,1,0:T(8,128)S(1)} %get-tuple-element.711) | copy-start | bytes 3145732 | tf_op jit(solution)/shard_map/while
  510.3 1.2 copy-start.1
  523.1 60.8 %copy-start.5 = (f32[256,256]{1,0:T(8,128)S(1)}, f32[256,256]{1,0:T(8,128)}, u32[]{:S(2)}) copy-start(f32[256,256]{1,0:T(8,128)} %copy-done.4) | copy-start | bytes 786436
  586.3 60.7 %copy-start.2 = (f32[256,256]{1,0:T(8,128)S(1)}, f32[256,256]{1,0:T(8,128)}, u32[]{:S(2)}) copy-start(f32[256,256]{1,0:T(8,128)} %fusion.52) | copy-start | bytes 786436
Sparse Core Ops, SparseCore 0:
  9.5 51.9 all-gather.2
  68.7 27.0 all-gather.4

commit v2 on v1

--- a/solution.py
+++ b/solution.py
@@ -24,11 +24,15 @@
     orbitals = block_re.shape[-1]
     eye_mat = jnp.eye(orbitals, dtype=block_re.dtype)
     first_factor = jnp.linalg.cholesky(block_re)
-    solved_ratio = jax.scipy.linalg.cho_solve((first_factor, True), block_im)
-    merged = symmetric(block_re + jnp.dot(block_im, solved_ratio, precision=HI))
+    solved = lax.linalg.triangular_solve(
+        first_factor, jnp.concatenate([block_im, eye_mat], axis=1), left_side=True, lower=True
+    )
+    ratio_half, first_inverse = solved[:, :orbitals], solved[:, orbitals:]
+    merged = symmetric(block_re + jnp.dot(ratio_half.T, ratio_half, precision=HI))
     second_factor = jnp.linalg.cholesky(merged)
-    inv_re = jax.scipy.linalg.cho_solve((second_factor, True), eye_mat)
-    inv_im = jnp.dot(solved_ratio, inv_re, precision=HI)
+    second_inverse = lax.linalg.triangular_solve(second_factor, eye_mat, left_side=True, lower=True)
+    inv_re = jnp.dot(second_inverse.T, second_inverse, precision=HI)
+    inv_im = jnp.dot(first_inverse.T, jnp.dot(ratio_half, inv_re, precision=HI), precision=HI)
     return (inv_re, inv_im)
 
 
@@ -98,12 +102,15 @@
         own = dom_index * local_slabs + local
 
         def chain_step(step, carry):
-            left_re, left_im, right_re, right_im = carry
+            left_re, left_im, right_re, right_im, out_re, out_im = carry
             is_left = step < own
+            is_final = step == slab_total - 1
             slab = jnp.where(is_left, step, slab_total - 1 - step + own)
-            acc_re = jnp.where(is_left, left_re, right_re)
-            acc_im = jnp.where(is_left, left_im, right_im)
-            inv_re, inv_im = invert_pair(all_re[slab] + acc_re, all_im[slab] + acc_im)
+            use_left = jnp.logical_or(is_left, is_final)
+            use_right = jnp.logical_not(is_left)
+            in_re = all_re[slab] + jnp.where(use_left, left_re, 0.0) + jnp.where(use_right, right_re, 0.0)
+            in_im = all_im[slab] + jnp.where(use_left, left_im, 0.0) + jnp.where(use_right, right_im, 0.0)
+            inv_re, inv_im = invert_pair(in_re, in_im)
             link_index = jnp.where(is_left, step, jnp.maximum(slab - 1, 0))
             link_block = all_link[link_index]
             link_block = jnp.where(is_left, link_block, link_block.T)
@@ -115,17 +122,13 @@
             )
             left_re = jnp.where(is_left, next_re, left_re)
             left_im = jnp.where(is_left, next_im, left_im)
-            right_re = jnp.where(is_left, right_re, next_re)
-            right_im = jnp.where(is_left, right_im, next_im)
-            return (left_re, left_im, right_re, right_im)
+            keep_right = jnp.logical_or(is_left, is_final)
+            right_re = jnp.where(keep_right, right_re, next_re)
+            right_im = jnp.where(keep_right, right_im, next_im)
+            return (left_re, left_im, right_re, right_im, inv_re, inv_im)
 
-        left_re, left_im, right_re, right_im = lax.fori_loop(
-            0, slab_total - 1, chain_step, (zero_block, zero_block, zero_block, zero_block)
-        )
-        inv_re, inv_im = invert_pair(
-            block_re[local] + left_re + right_re, block_im[local] + left_im + right_im
-        )
-        outputs.append(jnp.stack([-inv_re, -inv_im]))
+        carry = lax.fori_loop(0, slab_total, chain_step, (zero_block,) * 6)
+        outputs.append(jnp.stack([-carry[4], -carry[5]]))
     return jnp.stack(outputs)[None]
 
 

time: 662 us -> 658 us (level)
    another operation x48 -> x24, matrix products: 14.1 us -> 9.55 us  [the longest x12 5.69 us: invert_pair(): lax.linalg.triangular_solve(first_factor, jnp.concatenate([block_im, eye_...]
    another operation x60 -> x84, local copies, waits for them, and re-layouts: 31.1 us -> 32.8 us  [the longest x36 15.8 us: invert_pair(): solved_ratio = jax.scipy.linalg.cho_solve((first_factor, True), block_im)]
where the time goes in v2:
time: 658 us; the launch traced here: 654 us
  other arithmetic  439 us (67%)
  waiting for transfers between devices  73 us (11%)
  local copies, waits for them, and re-layouts  56.2 us (9%)
  loops' own time  34.1 us (5%)
  matrix products  33.1 us (5%)
  between operations  18.4 us (3%)
    another operation x28, other arithmetic, invert_pair(): second_factor = jnp.linalg.cholesky(merged)  138 us
    another operation x24, other arithmetic, invert_pair(): first_factor = jnp.linalg.cholesky(block_re)  136 us
    another operation x12, other arithmetic, invert_pair(): lax.linalg.triangular_solve(first_factor, jnp.concatenate([block_im, eye_...  78.8 us
    another operation x8, other arithmetic, invert_pair(): lax.linalg.triangular_solve(second_factor, eye_mat, left_side=True, lower...  78.8 us
    all_gather x1, waiting for transfers between devices, body(): lax.all_gather(green_prev, 'energy', axis=0, tiled=True).astype(jnp.float32)  45.1 us
    another operation x1, loops' own time, body(): carry = lax.fori_loop(0, slab_total, chain_step, (zero_block,) * 6)  33.4 us
    another operation x80, local copies, waits for them, and re-layouts  32.5 us
    all_gather x1, waiting for transfers between devices, body(): lax.all_gather(jnp.stack([block_re, block_im, coupling]), 'dom', axis=1,...  27.1 us
  transfers between devices with their start and end apart: 2, of which 2 were waited for; matrix products, arithmetic and copies ran while one was open for 1% of the time, Pallas kernels for 0%

profile of v2, /device:TPU:0, one launch (start us, length us, event | category | flops | bytes accessed | tf_op | source)
XLA Modules:
  0.0 653.7 jit_solution(13339425417884684590)
XLA Ops:
  16.4 45.1 %all-gather.3.cloned.1.call-done = bf16[8,1,2,256,256]{4,3,2,1,0:T(8,128)(2,1)} async-done(((bf16[1,1,2,256,256]{4,3,2,1,0:T(8,128)(2,1)}), bf16[8,1,2,256,256]{4,3,2,1,0:T(8,128)(2,1)}) %all-gather.3.cloned.1.call-update) | async-done | bytes 2097168 | tf_op jit(solution)/shard_map/all_gather | solution.py:84
  68.6 27.1 %all-gather.5.cloned.1.call-done = f32[3,4,256,256]{3,2,1,0:T(8,128)} async-done(((f32[3,1,256,256]{3,2,1,0:T(8,128)}), f32[3,4,256,256]{3,2,1,0:T(8,128)}) %all-gather.5.cloned.1.call-update) | async-done | bytes 3145744 | tf_op jit(solution)/shard_map/all_gather | solution.py:93
  99.1 545.4 %while.39 = (s32[]{:T(128)}, f32[256,256]{0,1:T(8,128)S(1)}, f32[256,256]{0,1:T(8,128)S(1)}, f32[256,256]{0,1:T(8,128)S(1)}, f32[256,256]{0,1:T(8,128)S(1)}, /*i...) while((s32[]{:T(128)}, f32[256,256]{0,1:T(8,128)S(1)}, ...), condition=%wide.region_5.7_spmd.clone.clone, body=%wide.region_0.6_spmd.clone.sunk.clone | while | flops 2167931392 | bytes 40997700 | solution.py:130
  122.1 11.7 %cholesky.459 = f32[128,128]{1,0:T(8,128)S(1)} custom-call(f32[128,128]{1,0:T(8,128)S(1)} %cholesky.458), custom_call_target="Cholesky" | custom-call | tf_op jit(solution)/shard_map/while/body/eval_jaxpr/jit(cholesky)/cholesky | solution.py:26
  144.2 11.7 %cholesky.461 = f32[128,128]{1,0:T(8,128)S(1)} custom-call(f32[128,128]{1,0:T(8,128)S(1)} %convolution_subtract_fusion.12), custom_call_target="Cholesky" | custom-call | tf_op jit(solution)/shard_map/while/body/eval_jaxpr/jit(cholesky)/cholesky | solution.py:26
  162.5 19.7 %custom-call.48 = f32[2,128,128]{1,2,0:T(8,128)S(1)} custom-call(f32[2,128,128]{2,1,0:T(8,128)S(1)} %get-tuple-element.591), custom_call_target="InvertDiagBlocksLowerTriangular" | custom-call | tf_op jit(solution)/shard_map/while/body/eval_jaxpr/triangular_solve | solution.py:27
  186.0 11.7 %cholesky.464 = f32[128,128]{1,0:T(8,128)S(1)} custom-call(f32[128,128]{1,0:T(8,128)S(1)} %cholesky.463), custom_call_target="Cholesky" | custom-call | tf_op jit(solution)/shard_map/while/body/eval_jaxpr/jit(cholesky)/cholesky | solution.py:32
  208.0 11.7 %cholesky.466 = f32[128,128]{1,0:T(8,128)S(1)} custom-call(f32[128,128]{1,0:T(8,128)S(1)} %convolution_subtract_fusion.14), custom_call_target="Cholesky" | custom-call | tf_op jit(solution)/shard_map/while/body/eval_jaxpr/jit(cholesky)/cholesky | solution.py:32
  226.9 19.7 %custom-call.50 = f32[2,128,128]{1,2,0:T(8,128)S(1)} custom-call(f32[2,128,128]{2,1,0:T(8,128)S(1)} %get-tuple-element.594), custom_call_target="InvertDiagBlocksLowerTriangular" | custom-call | tf_op jit(solution)/shard_map/while/body/eval_jaxpr/triangular_solve | solution.py:33
  253.1 11.7 %cholesky.459 = f32[128,128]{1,0:T(8,128)S(1)} custom-call(f32[128,128]{1,0:T(8,128)S(1)} %cholesky.458), custom_call_target="Cholesky" | custom-call | tf_op jit(solution)/shard_map/while/body/eval_jaxpr/jit(cholesky)/cholesky | solution.py:26
  275.1 11.7 %cholesky.461 = f32[128,128]{1,0:T(8,128)S(1)} custom-call(f32[128,128]{1,0:T(8,128)S(1)} %convolution_subtract_fusion.12), custom_call_target="Cholesky" | custom-call | tf_op jit(solution)/shard_map/while/body/eval_jaxpr/jit(cholesky)/cholesky | solution.py:26
  293.4 19.7 %custom-call.48 = f32[2,128,128]{1,2,0:T(8,128)S(1)} custom-call(f32[2,128,128]{2,1,0:T(8,128)S(1)} %get-tuple-element.591), custom_call_target="InvertDiagBlocksLowerTriangular" | custom-call | tf_op jit(solution)/shard_map/while/body/eval_jaxpr/triangular_solve | solution.py:27
  317.0 11.7 %cholesky.464 = f32[128,128]{1,0:T(8,128)S(1)} custom-call(f32[128,128]{1,0:T(8,128)S(1)} %cholesky.463), custom_call_target="Cholesky" | custom-call | tf_op jit(solution)/shard_map/while/body/eval_jaxpr/jit(cholesky)/cholesky | solution.py:32
  339.0 11.7 %cholesky.466 = f32[128,128]{1,0:T(8,128)S(1)} custom-call(f32[128,128]{1,0:T(8,128)S(1)} %convolution_subtract_fusion.14), custom_call_target="Cholesky" | custom-call | tf_op jit(solution)/shard_map/while/body/eval_jaxpr/jit(cholesky)/cholesky | solution.py:32
  357.9 19.7 %custom-call.50 = f32[2,128,128]{1,2,0:T(8,128)S(1)} custom-call(f32[2,128,128]{2,1,0:T(8,128)S(1)} %get-tuple-element.594), custom_call_target="InvertDiagBlocksLowerTriangular" | custom-call | tf_op jit(solution)/shard_map/while/body/eval_jaxpr/triangular_solve | solution.py:33
  384.1 11.7 %cholesky.459 = f32[128,128]{1,0:T(8,128)S(1)} custom-call(f32[128,128]{1,0:T(8,128)S(1)} %cholesky.458), custom_call_target="Cholesky" | custom-call | tf_op jit(solution)/shard_map/while/body/eval_jaxpr/jit(cholesky)/cholesky | solution.py:26
  406.1 11.7 %cholesky.461 = f32[128,128]{1,0:T(8,128)S(1)} custom-call(f32[128,128]{1,0:T(8,128)S(1)} %convolution_subtract_fusion.12), custom_call_target="Cholesky" | custom-call | tf_op jit(solution)/shard_map/while/body/eval_jaxpr/jit(cholesky)/cholesky | solution.py:26
  424.4 19.7 %custom-call.48 = f32[2,128,128]{1,2,0:T(8,128)S(1)} custom-call(f32[2,128,128]{2,1,0:T(8,128)S(1)} %get-tuple-element.591), custom_call_target="InvertDiagBlocksLowerTriangular" | custom-call | tf_op jit(solution)/shard_map/while/body/eval_jaxpr/triangular_solve | solution.py:27
  470.0 11.7 %cholesky.466 = f32[128,128]{1,0:T(8,128)S(1)} custom-call(f32[128,128]{1,0:T(8,128)S(1)} %convolution_subtract_fusion.14), custom_call_target="Cholesky" | custom-call | tf_op jit(solution)/shard_map/while/body/eval_jaxpr/jit(cholesky)/cholesky | solution.py:32
  488.9 19.7 %custom-call.50 = f32[2,128,128]{1,2,0:T(8,128)S(1)} custom-call(f32[2,128,128]{2,1,0:T(8,128)S(1)} %get-tuple-element.594), custom_call_target="InvertDiagBlocksLowerTriangular" | custom-call | tf_op jit(solution)/shard_map/while/body/eval_jaxpr/triangular_solve | solution.py:33
  537.1 11.7 %cholesky.461 = f32[128,128]{1,0:T(8,128)S(1)} custom-call(f32[128,128]{1,0:T(8,128)S(1)} %convolution_subtract_fusion.12), custom_call_target="Cholesky" | custom-call | tf_op jit(solution)/shard_map/while/body/eval_jaxpr/jit(cholesky)/cholesky | solution.py:26
  555.4 19.7 %custom-call.48 = f32[2,128,128]{1,2,0:T(8,128)S(1)} custom-call(f32[2,128,128]{2,1,0:T(8,128)S(1)} %get-tuple-element.591), custom_call_target="InvertDiagBlocksLowerTriangular" | custom-call | tf_op jit(solution)/shard_map/while/body/eval_jaxpr/triangular_solve | solution.py:27
  601.0 11.7 %cholesky.466 = f32[128,128]{1,0:T(8,128)S(1)} custom-call(f32[128,128]{1,0:T(8,128)S(1)} %convolution_subtract_fusion.14), custom_call_target="Cholesky" | custom-call | tf_op jit(solution)/shard_map/while/body/eval_jaxpr/jit(cholesky)/cholesky | solution.py:32
  619.9 19.7 %custom-call.50 = f32[2,128,128]{1,2,0:T(8,128)S(1)} custom-call(f32[2,128,128]{2,1,0:T(8,128)S(1)} %get-tuple-element.594), custom_call_target="InvertDiagBlocksLowerTriangular" | custom-call | tf_op jit(solution)/shard_map/while/body/eval_jaxpr/triangular_solve | solution.py:33
  (420 shorter events, 252.5 us)
Async XLA Ops:
  6.5 55.0 %all-gather.3.cloned.1.call-start = ((), (), s32[]{:S(2)}) async-start(), calls=%async_computation | async-start | bytes 2359296 | tf_op jit(solution)/shard_map/all_gather | solution.py:84
  7.3 88.5 %all-gather.5.cloned.1.call-start = ((), (), s32[]{:S(2)}) async-start(), calls=%async_computation.1 | async-start | bytes 3932160 | tf_op jit(solution)/shard_map/all_gather | solution.py:93
  61.5 4.6 copy-start.4
  61.5 4.6 copy-start.6
  65.7 1.3 copy-start.5
  120.5 62.9 %copy-start.1 = (f32[4,256,256]{2,1,0:T(8,128)}, f32[4,256,256]{2,1,0:T(8,128)S(1)}, u32[]{:S(2)}) copy-start(f32[4,256,256]{2,1,0:T(8,128)S(1)} %get-tuple-element.697) | copy-start | bytes 3145732 | tf_op jit(solution)/shard_map/while
  248.2 2.1 copy-start
  249.2 1.5 copy-start.3
  250.3 1.2 copy-start.2
  251.6 62.9 %copy-start.1 = (f32[4,256,256]{2,1,0:T(8,128)}, f32[4,256,256]{2,1,0:T(8,128)S(1)}, u32[]{:S(2)}) copy-start(f32[4,256,256]{2,1,0:T(8,128)S(1)} %get-tuple-element.697) | copy-start | bytes 3145732 | tf_op jit(solution)/shard_map/while
  379.2 2.1 copy-start
  380.2 1.6 copy-start.3
  381.3 1.2 copy-start.2
  382.5 62.9 %copy-start.1 = (f32[4,256,256]{2,1,0:T(8,128)}, f32[4,256,256]{2,1,0:T(8,128)S(1)}, u32[]{:S(2)}) copy-start(f32[4,256,256]{2,1,0:T(8,128)S(1)} %get-tuple-element.697) | copy-start | bytes 3145732 | tf_op jit(solution)/shard_map/while
  510.2 2.1 copy-start
  511.2 1.5 copy-start.3
  512.3 1.2 copy-start.2
  513.5 62.9 %copy-start.1 = (f32[4,256,256]{2,1,0:T(8,128)}, f32[4,256,256]{2,1,0:T(8,128)S(1)}, u32[]{:S(2)}) copy-start(f32[4,256,256]{2,1,0:T(8,128)S(1)} %get-tuple-element.697) | copy-start | bytes 3145732 | tf_op jit(solution)/shard_map/while
  641.2 2.1 copy-start
  642.2 1.5 copy-start.3
  643.3 1.2 copy-start.2
Sparse Core Ops, SparseCore 0:
  9.5 51.9 all-gather.2
  68.7 27.0 all-gather.4

commit v3 on v2

--- a/solution.py
+++ b/solution.py
@@ -1,6 +1,8 @@
 import jax
 import jax.numpy as jnp
 from jax import lax
+from jax.experimental import pallas as pl
+from jax.experimental.pallas import tpu as pltpu
 from jax.sharding import PartitionSpec as P
 
 BW = 32
@@ -20,19 +22,45 @@
     return 0.5 * (matrix + jnp.swapaxes(matrix, -1, -2))
 
 
+def sweep_kernel(a_ref, o_ref):
+    n = a_ref.shape[0]
+    half = n // 2
+    o_ref[...] = a_ref[...]
+
+    def pivot(k, carry):
+        lanes = lax.broadcasted_iota(jnp.int32, (1, n), 1)
+        half_cols = lax.broadcasted_iota(jnp.int32, (n, half), 1)
+        a = o_ref[...]
+        row = o_ref[pl.ds(k, 1), :]
+        diag = jnp.sum(jnp.where(lanes == k, row, 0.0), axis=1, keepdims=True)
+        inv_d = 1.0 / diag
+        tile = jnp.where(k < half, a[:, :half], a[:, half:])
+        col = jnp.sum(jnp.where(half_cols == lax.rem(k, half), tile, 0.0), axis=1, keepdims=True)
+        scaled = row * inv_d
+        factor = jnp.where(lanes == k, 1.0 - inv_d, scaled)
+        o_ref[...] = a - col * factor
+        o_ref[pl.ds(k, 1), :] = jnp.where(lanes == k, -inv_d, scaled)
+        return carry
+
+    lax.fori_loop(0, n, pivot, 0)
+
+
+def neg_inverse(matrix):
+    n = matrix.shape[-1]
+    return pl.pallas_call(
+        sweep_kernel,
+        out_shape=jax.ShapeDtypeStruct((n, n), jnp.float32),
+        in_specs=[pl.BlockSpec(memory_space=pltpu.VMEM)],
+        out_specs=pl.BlockSpec(memory_space=pltpu.VMEM),
+    )(matrix)
+
+
 def invert_pair(block_re, block_im):
-    orbitals = block_re.shape[-1]
-    eye_mat = jnp.eye(orbitals, dtype=block_re.dtype)
-    first_factor = jnp.linalg.cholesky(block_re)
-    solved = lax.linalg.triangular_solve(
-        first_factor, jnp.concatenate([block_im, eye_mat], axis=1), left_side=True, lower=True
-    )
-    ratio_half, first_inverse = solved[:, :orbitals], solved[:, orbitals:]
-    merged = symmetric(block_re + jnp.dot(ratio_half.T, ratio_half, precision=HI))
-    second_factor = jnp.linalg.cholesky(merged)
-    second_inverse = lax.linalg.triangular_solve(second_factor, eye_mat, left_side=True, lower=True)
-    inv_re = jnp.dot(second_inverse.T, second_inverse, precision=HI)
-    inv_im = jnp.dot(first_inverse.T, jnp.dot(ratio_half, inv_re, precision=HI), precision=HI)
+    first_neg = neg_inverse(block_re)
+    solved_ratio = -jnp.dot(first_neg, block_im, precision=HI)
+    merged = symmetric(block_re + jnp.dot(block_im, solved_ratio, precision=HI))
+    inv_re = -neg_inverse(merged)
+    inv_im = jnp.dot(solved_ratio, inv_re, precision=HI)
     return (inv_re, inv_im)
 
 

time: 658 us -> 414 us (0.63)
  other arithmetic: 439 us -> 20 us
  Pallas kernels: 0 us -> 267 us
  local copies, waits for them, and re-layouts: 56.2 us -> 9.94 us
  loops' own time: 34.1 us -> 0.76 us
  matrix products: 33.1 us -> 24.8 us
    another operation x72 -> x0, other arithmetic: 432 us -> none  [the longest x28 138 us: invert_pair(): second_factor = jnp.linalg.cholesky(merged)]
    pallas_call x0 -> x8, Pallas kernels: none -> 267 us  [neg_inverse(): pl.pallas_call(sweep_kernel, out_shape=jax.ShapeDtypeStruct((n, n), jnp.f...]
    another operation x140 -> x0, local copies, waits for them, and re-layouts: 35.3 us -> none
    another operation x1, loops' own time: 33.4 us -> 0.76 us  [body(): carry = lax.fori_loop(0, slab_total, chain_step, (zero_block,) * 6)]
    another operation x40 -> x0, matrix products: 13.3 us -> none  [the longest x12 5.69 us: invert_pair(): lax.linalg.triangular_solve(first_factor, jnp.concatenate([block_im, eye_...]
    dynamic_slice x16 -> x8, local copies, waits for them, and re-layouts: 9.5 us -> 0.61 us  [chain_step(): link_block = all_link[link_index]]
    add x4, other arithmetic: 0.23 us -> 7.37 us  [chain_step(): all_im[slab] + jnp.where(use_left, left_im, 0.0)]
where the time goes in v3:
time: 414 us; the launch traced here: 413 us
  Pallas kernels  267 us (64%)
  waiting for transfers between devices  73 us (18%)
  matrix products  24.8 us (6%)
  other arithmetic  20 us (5%)
  between operations  18 us (4%)
  local copies, waits for them, and re-layouts  9.94 us (2%)
    pallas_call x8, Pallas kernels, neg_inverse(): pl.pallas_call(sweep_kernel, out_shape=jax.ShapeDtypeStruct((n, n), jnp.f...  267 us
    all_gather x1, waiting for transfers between devices, body(): lax.all_gather(green_prev, 'energy', axis=0, tiled=True).astype(jnp.float32)  45.1 us
    all_gather x1, waiting for transfers between devices, body(): lax.all_gather(jnp.stack([block_re, block_im, coupling]), 'dom', axis=1,...  27.1 us
  transfers between devices with their start and end apart: 2, of which 2 were waited for; matrix products, arithmetic and copies ran while one was open for 1% of the time, Pallas kernels for 0%

profile of v3, /device:TPU:0, one launch (start us, length us, event | category | flops | bytes accessed | tf_op | source)
XLA Modules:
  0.0 413.1 jit_solution(17557938375445740675)
XLA Ops:
  10.5 1.4 constant_dynamic-slice_fusion.2
  16.4 45.1 %all-gather.3.cloned.1.call-done = bf16[8,1,2,256,256]{4,3,2,1,0:T(8,128)(2,1)} async-done(((bf16[1,1,2,256,256]{4,3,2,1,0:T(8,128)(2,1)}), bf16[8,1,2,256,256]{4,3,2,1,0:T(8,128)(2,1)}) %all-gather.3.cloned.1.call-update) | async-done | bytes 2097168 | tf_op jit(solution)/shard_map/all_gather | solution.py:112
  61.5 4.1 %fusion.6 = f32[1,2,256,256]{3,0,2,1:T(1,128)S(1)} fusion(bf16[8,2,256,256]{3,2,1,0:T(8,128)(2,1)} %bitcast.169, s32[8]{0:T(128)} %param.14, s32[]{:T(128)S(6)} %select_n.204, s32[]{:T(128)S(6)} %select_n.203), kind=kOutput, calls=%fused_computation.19 | convolution fusion | flops 12582952 | bytes 2621480 | tf_op jit(solution)/shard_map/n,nsabc->sabc/dot_general | solution.py:109
  68.6 27.1 %all-gather.5.cloned.1.call-done = f32[3,4,256,256]{3,2,1,0:T(8,128)} async-done(((f32[3,1,256,256]{3,2,1,0:T(8,128)}), f32[3,4,256,256]{3,2,1,0:T(8,128)}) %all-gather.5.cloned.1.call-update) | async-done | bytes 3145744 | tf_op jit(solution)/shard_map/all_gather | solution.py:121
  95.8 3.5 slice_bitcast_fusion
  99.2 305.1 %while.27 = (s32[]{:T(128)}, f32[256,256]{1,0:T(8,128)S(1)}, f32[256,256]{1,0:T(8,128)S(1)}, f32[256,256]{1,0:T(8,128)S(1)}, f32[256,256]{1,0:T(8,128)S(1)}, /*i...) while((s32[]{:T(128)}, f32[256,256]{1,0:T(8,128)S(1)}, ...), condition=%wide.region_1.2_spmd.clone.clone, body=%wide.region_0.1_spmd.clone.sunk.clone | while | flops 1411317760 | bytes 17826152 | solution.py:158
  99.2 1.8 fusion.105
  101.1 33.3 %eval_jaxpr.16 = f32[256,256]{1,0:T(8,128)} custom-call(f32[256,256]{1,0:T(8,128)} %get-tuple-element.432.a_ref), custom_call_target="tpu_custom_call" | custom-call | tf_op jit(solution)/shard_map/while/body/eval_jaxpr/pallas_call | solution.py:50
  134.4 1.3 convolution_negate_fusion.3
  135.7 1.3 convolution_add_fusion.3
  138.0 33.3 %eval_jaxpr.17 = f32[256,256]{1,0:T(8,128)} custom-call(f32[256,256]{1,0:T(8,128)} %fusion.106.a_ref), custom_call_target="tpu_custom_call" | custom-call | tf_op jit(solution)/shard_map/while/body/eval_jaxpr/pallas_call | solution.py:50
  175.5 1.8 fusion.105
  177.4 33.3 %eval_jaxpr.16 = f32[256,256]{1,0:T(8,128)} custom-call(f32[256,256]{1,0:T(8,128)} %get-tuple-element.432.a_ref), custom_call_target="tpu_custom_call" | custom-call | tf_op jit(solution)/shard_map/while/body/eval_jaxpr/pallas_call | solution.py:50
  212.0 1.3 convolution_add_fusion.3
  214.2 33.3 %eval_jaxpr.17 = f32[256,256]{1,0:T(8,128)} custom-call(f32[256,256]{1,0:T(8,128)} %fusion.106.a_ref), custom_call_target="tpu_custom_call" | custom-call | tf_op jit(solution)/shard_map/while/body/eval_jaxpr/pallas_call | solution.py:50
  251.8 1.8 fusion.105
  253.7 33.3 %eval_jaxpr.16 = f32[256,256]{1,0:T(8,128)} custom-call(f32[256,256]{1,0:T(8,128)} %get-tuple-element.432.a_ref), custom_call_target="tpu_custom_call" | custom-call | tf_op jit(solution)/shard_map/while/body/eval_jaxpr/pallas_call | solution.py:50
  287.0 1.3 convolution_negate_fusion.3
  288.3 1.3 convolution_add_fusion.3
  290.5 33.3 %eval_jaxpr.17 = f32[256,256]{1,0:T(8,128)} custom-call(f32[256,256]{1,0:T(8,128)} %fusion.106.a_ref), custom_call_target="tpu_custom_call" | custom-call | tf_op jit(solution)/shard_map/while/body/eval_jaxpr/pallas_call | solution.py:50
  328.1 1.8 fusion.105
  329.9 33.3 %eval_jaxpr.16 = f32[256,256]{1,0:T(8,128)} custom-call(f32[256,256]{1,0:T(8,128)} %get-tuple-element.432.a_ref), custom_call_target="tpu_custom_call" | custom-call | tf_op jit(solution)/shard_map/while/body/eval_jaxpr/pallas_call | solution.py:50
  364.6 1.3 convolution_add_fusion.3
  366.8 33.3 %eval_jaxpr.17 = f32[256,256]{1,0:T(8,128)} custom-call(f32[256,256]{1,0:T(8,128)} %fusion.106.a_ref), custom_call_target="tpu_custom_call" | custom-call | tf_op jit(solution)/shard_map/while/body/eval_jaxpr/pallas_call | solution.py:50
  (104 shorter events, 31.0 us)
Async XLA Ops:
  6.5 55.0 %all-gather.3.cloned.1.call-start = ((), (), s32[]{:S(2)}) async-start(), calls=%async_computation | async-start | bytes 2359296 | tf_op jit(solution)/shard_map/all_gather | solution.py:112
  7.3 88.5 %all-gather.5.cloned.1.call-start = ((), (), s32[]{:S(2)}) async-start(), calls=%async_computation.1 | async-start | bytes 3932160 | tf_op jit(solution)/shard_map/all_gather | solution.py:121
  61.5 4.6 %copy-start.2 = (f32[1,256,256]{2,1,0:T(8,128)S(1)}, f32[1,256,256]{2,1,0:T(8,128)}, u32[]{:S(2)}) copy-start(f32[1,256,256]{2,1,0:T(8,128)} %param.9) | copy-start | bytes 786436
  61.5 4.6 %copy-start.4 = (f32[1,256]{1,0:T(1,128)S(1)}, f32[1,256]{1,0:T(1,128)}, u32[]{:S(2)}) copy-start(f32[1,256]{1,0:T(1,128)} %param.11) | copy-start | bytes 3076
  65.7 1.3 copy-start.3
  172.3 1.9 copy-start
  172.7 1.5 copy-start.1
  248.5 1.9 copy-start
  248.9 1.5 copy-start.1
  324.8 1.9 copy-start
  325.2 1.5 copy-start.1
  401.1 1.9 copy-start
  401.5 1.5 copy-start.1
Sparse Core Ops, SparseCore 0:
  9.5 51.9 all-gather.2
  68.7 27.0 all-gather.4

commit v4 on v2

--- a/solution.py
+++ b/solution.py
@@ -1,6 +1,8 @@
 import jax
 import jax.numpy as jnp
 from jax import lax
+from jax.experimental import pallas as pl
+from jax.experimental.pallas import tpu as pltpu
 from jax.sharding import PartitionSpec as P
 
 BW = 32
@@ -20,20 +22,53 @@
     return 0.5 * (matrix + jnp.swapaxes(matrix, -1, -2))
 
 
+def sweep_kernel(ar_ref, ai_ref, or_ref, oi_ref):
+    n = ar_ref.shape[0]
+    half = n // 2
+    or_ref[...] = ar_ref[...]
+    oi_ref[...] = ai_ref[...]
+
+    def pivot(k, carry):
+        lanes = lax.broadcasted_iota(jnp.int32, (1, n), 1)
+        half_cols = lax.broadcasted_iota(jnp.int32, (n, half), 1)
+        kh = lax.rem(k, half)
+        at_k = lanes == k
+        a_re = or_ref[...]
+        a_im = oi_ref[...]
+        row_re = or_ref[pl.ds(k, 1), :]
+        row_im = oi_ref[pl.ds(k, 1), :]
+        d_re = jnp.sum(jnp.where(at_k, row_re, 0.0), axis=1, keepdims=True)
+        d_im = jnp.sum(jnp.where(at_k, row_im, 0.0), axis=1, keepdims=True)
+        tile_re = jnp.where(k < half, a_re[:, :half], a_re[:, half:])
+        tile_im = jnp.where(k < half, a_im[:, :half], a_im[:, half:])
+        col_re = jnp.sum(jnp.where(half_cols == kh, tile_re, 0.0), axis=1, keepdims=True)
+        col_im = jnp.sum(jnp.where(half_cols == kh, tile_im, 0.0), axis=1, keepdims=True)
+        norm = d_re * d_re + d_im * d_im
+        inv_re = d_re / norm
+        inv_im = -d_im / norm
+        s_re = row_re * inv_re - row_im * inv_im
+        s_im = row_re * inv_im + row_im * inv_re
+        f_re = jnp.where(at_k, 1.0 - inv_re, s_re)
+        f_im = jnp.where(at_k, -inv_im, s_im)
+        or_ref[...] = a_re - (col_re * f_re - col_im * f_im)
+        oi_ref[...] = a_im - (col_re * f_im + col_im * f_re)
+        or_ref[pl.ds(k, 1), :] = jnp.where(at_k, -inv_re, s_re)
+        oi_ref[pl.ds(k, 1), :] = jnp.where(at_k, -inv_im, s_im)
+        return carry
+
+    lax.fori_loop(0, n, pivot, 0)
+
+
 def invert_pair(block_re, block_im):
-    orbitals = block_re.shape[-1]
-    eye_mat = jnp.eye(orbitals, dtype=block_re.dtype)
-    first_factor = jnp.linalg.cholesky(block_re)
-    solved = lax.linalg.triangular_solve(
-        first_factor, jnp.concatenate([block_im, eye_mat], axis=1), left_side=True, lower=True
-    )
-    ratio_half, first_inverse = solved[:, :orbitals], solved[:, orbitals:]
-    merged = symmetric(block_re + jnp.dot(ratio_half.T, ratio_half, precision=HI))
-    second_factor = jnp.linalg.cholesky(merged)
-    second_inverse = lax.linalg.triangular_solve(second_factor, eye_mat, left_side=True, lower=True)
-    inv_re = jnp.dot(second_inverse.T, second_inverse, precision=HI)
-    inv_im = jnp.dot(first_inverse.T, jnp.dot(ratio_half, inv_re, precision=HI), precision=HI)
-    return (inv_re, inv_im)
+    n = block_re.shape[-1]
+    spec = pl.BlockSpec(memory_space=pltpu.VMEM)
+    neg_re, neg_im = pl.pallas_call(
+        sweep_kernel,
+        out_shape=(jax.ShapeDtypeStruct((n, n), jnp.float32),) * 2,
+        in_specs=[spec, spec],
+        out_specs=(spec, spec),
+    )(block_re, -block_im)
+    return (-neg_re, -neg_im)
 
 
 def slab_blocks(hamiltonian, coupling, deform, fetched, energy, first_mask, last_mask):

time: 658 us -> 333 us (0.51)
  other arithmetic: 439 us -> 17.5 us
  Pallas kernels: 0 us -> 201 us
  local copies, waits for them, and re-layouts: 56.2 us -> 9.44 us
  loops' own time: 34.1 us -> 0.73 us
  matrix products: 33.1 us -> 12.6 us
    another operation x72 -> x0, other arithmetic: 432 us -> none  [the longest x28 138 us: invert_pair(): second_factor = jnp.linalg.cholesky(merged)]
    pallas_call x0 -> x4, Pallas kernels: none -> 201 us  [invert_pair(): pl.pallas_call(sweep_kernel, out_shape=(jax.ShapeDtypeStruct((n, n), jnp....]
    another operation x140 -> x0, local copies, waits for them, and re-layouts: 35.3 us -> none
    another operation x1, loops' own time: 33.4 us -> 0.73 us  [body(): carry = lax.fori_loop(0, slab_total, chain_step, (zero_block,) * 6)]
    another operation x40 -> x0, matrix products: 13.3 us -> none  [the longest x12 5.69 us: invert_pair(): lax.linalg.triangular_solve(first_factor, jnp.concatenate([block_im, eye_...]
    neg x0 -> x12, other arithmetic: none -> 11.7 us  [the longest x4 7.76 us: invert_pair(): -block_im]
    dynamic_slice x16 -> x8, local copies, waits for them, and re-layouts: 9.5 us -> 0.61 us  [chain_step(): link_block = all_link[link_index]]
    dot_general x16 -> x0, matrix products: 8.66 us -> none  [the longest x4 2.39 us: invert_pair(): jnp.dot(ratio_half.T, ratio_half, precision=HI)]
where the time goes in v4:
time: 333 us
  Pallas kernels  201 us (60%)
  waiting for transfers between devices  73 us (22%)
  between operations  18 us (5%)
  other arithmetic  17.5 us (5%)
  matrix products  12.6 us (4%)
  local copies, waits for them, and re-layouts  9.44 us (3%)
    pallas_call x4, Pallas kernels, invert_pair(): pl.pallas_call(sweep_kernel, out_shape=(jax.ShapeDtypeStruct((n, n), jnp....  201 us
    all_gather x1, waiting for transfers between devices, body(): lax.all_gather(green_prev, 'energy', axis=0, tiled=True).astype(jnp.float32)  45.1 us
    all_gather x1, waiting for transfers between devices, body(): lax.all_gather(jnp.stack([block_re, block_im, coupling]), 'dom', axis=1,...  27.1 us
    neg x4, other arithmetic, invert_pair(): -block_im  7.76 us
  transfers between devices with their start and end apart: 2, of which 2 were waited for; matrix products, arithmetic and copies ran while one was open for 1% of the time, Pallas kernels for 0%

profile of v4, /device:TPU:0, one launch (start us, length us, event | category | flops | bytes accessed | tf_op | source)
XLA Modules:
  0.0 332.6 jit_solution(1338490437250042101)
XLA Ops:
  7.3 1.2 dynamic_slice.42
  10.5 1.4 constant_dynamic-slice_fusion.2
  14.5 1.2 dynamic_slice.43
  16.4 45.1 %all-gather.3.cloned.1.call-done = bf16[8,1,2,256,256]{4,3,2,1,0:T(8,128)(2,1)} async-done(((bf16[1,1,2,256,256]{4,3,2,1,0:T(8,128)(2,1)}), bf16[8,1,2,256,256]{4,3,2,1,0:T(8,128)(2,1)}) %all-gather.3.cloned.1.call-update) | async-done | bytes 2097168 | tf_op jit(solution)/shard_map/all_gather | solution.py:119
  61.5 4.1 %fusion.6 = f32[1,2,256,256]{3,0,2,1:T(1,128)S(1)} fusion(bf16[8,2,256,256]{3,2,1,0:T(8,128)(2,1)} %bitcast.140, s32[8]{0:T(128)} %param.14, s32[]{:T(128)S(6)} %select_n.204, s32[]{:T(128)S(6)} %select_n.203), kind=kOutput, calls=%fused_computation.16 | convolution fusion | flops 12582952 | bytes 2621480 | tf_op jit(solution)/shard_map/n,nsabc->sabc/dot_general | solution.py:116
  66.1 0.8 fusion.16
  67.6 1.0 pad_maximum_fusion
  68.6 27.1 %all-gather.5.cloned.1.call-done = f32[3,4,256,256]{3,2,1,0:T(8,128)} async-done(((f32[3,1,256,256]{3,2,1,0:T(8,128)}), f32[3,4,256,256]{3,2,1,0:T(8,128)}) %all-gather.5.cloned.1.call-update) | async-done | bytes 3145744 | tf_op jit(solution)/shard_map/all_gather | solution.py:128
  95.8 3.5 %slice_bitcast_fusion = (f32[4,256,256]{2,1,0:T(8,128)}, f32[4,256,256]{2,1,0:T(8,128)}, f32[4,256,256]{2,1,0:T(8,128)S(1)}) fusion(f32[3,4,256,256]{3,2,1,0:T(8,128)} %all-gather.5.cloned.1.call-done), kind=kLoop, calls=%fused_computation.21 | loop fusion | bytes 6291456 | tf_op jit(solution)/shard_map/squeeze | solution.py:131
  99.2 224.6 %while.27 = (s32[]{:T(128)}, f32[256,256]{1,0:T(8,128)S(1)}, f32[256,256]{1,0:T(8,128)S(1)}, f32[256,256]{1,0:T(8,128)S(1)}, f32[256,256]{1,0:T(8,128)S(1)}, /*i...) while((s32[]{:T(128)}, f32[256,256]{1,0:T(8,128)S(1)}, ...), condition=%wide.region_1.2_spmd.clone.clone, body=%wide.region_0.1_spmd.clone.sunk.clone | while | flops 807206912 | bytes 15466885 | solution.py:165
  99.2 1.9 fusion.76
  101.2 50.3 %eval_jaxpr.8 = (f32[256,256]{1,0:T(8,128)}, f32[256,256]{1,0:T(8,128)}) custom-call(f32[256,256]{1,0:T(8,128)} %get-tuple-element.440.ar_ref, f32[256,256]{1,0:T(8,128)} %get-tuple-element.441.ai_ref), custom_call_target="tpu_custom_call" | custom-call | tf_op jit(solution)/shard_map/while/body/eval_jaxpr/pallas_call | solution.py:65
  151.5 1.0 neg.64
  155.4 1.9 fusion.76
  157.3 50.3 %eval_jaxpr.8 = (f32[256,256]{1,0:T(8,128)}, f32[256,256]{1,0:T(8,128)}) custom-call(f32[256,256]{1,0:T(8,128)} %get-tuple-element.440.ar_ref, f32[256,256]{1,0:T(8,128)} %get-tuple-element.441.ai_ref), custom_call_target="tpu_custom_call" | custom-call | tf_op jit(solution)/shard_map/while/body/eval_jaxpr/pallas_call | solution.py:65
  207.7 1.0 neg.64
  211.6 1.9 fusion.76
  213.5 50.3 %eval_jaxpr.8 = (f32[256,256]{1,0:T(8,128)}, f32[256,256]{1,0:T(8,128)}) custom-call(f32[256,256]{1,0:T(8,128)} %get-tuple-element.440.ar_ref, f32[256,256]{1,0:T(8,128)} %get-tuple-element.441.ai_ref), custom_call_target="tpu_custom_call" | custom-call | tf_op jit(solution)/shard_map/while/body/eval_jaxpr/pallas_call | solution.py:65
  263.8 1.0 neg.64
  267.7 1.9 fusion.76
  269.7 50.3 %eval_jaxpr.8 = (f32[256,256]{1,0:T(8,128)}, f32[256,256]{1,0:T(8,128)}) custom-call(f32[256,256]{1,0:T(8,128)} %get-tuple-element.440.ar_ref, f32[256,256]{1,0:T(8,128)} %get-tuple-element.441.ai_ref), custom_call_target="tpu_custom_call" | custom-call | tf_op jit(solution)/shard_map/while/body/eval_jaxpr/pallas_call | solution.py:65
  320.0 1.0 neg.64
  323.9 1.1 negate_bitcast_fusion
  324.9 0.8 maximum_bitcast_fusion
  (92 shorter events, 13.5 us)
Async XLA Ops:
  6.5 55.0 %all-gather.3.cloned.1.call-start = ((), (), s32[]{:S(2)}) async-start(), calls=%async_computation | async-start | bytes 2359296 | tf_op jit(solution)/shard_map/all_gather | solution.py:119
  7.3 88.5 %all-gather.5.cloned.1.call-start = ((), (), s32[]{:S(2)}) async-start(), calls=%async_computation.1 | async-start | bytes 3932160 | tf_op jit(solution)/shard_map/all_gather | solution.py:128
  61.5 4.6 %copy-start.3 = (f32[1,256,256]{2,1,0:T(8,128)S(1)}, f32[1,256,256]{2,1,0:T(8,128)}, u32[]{:S(2)}) copy-start(f32[1,256,256]{2,1,0:T(8,128)} %param.9) | copy-start | bytes 786436
  61.5 4.6 %copy-start.5 = (f32[1,256]{1,0:T(1,128)S(1)}, f32[1,256]{1,0:T(1,128)}, u32[]{:S(2)}) copy-start(f32[1,256]{1,0:T(1,128)} %param.11) | copy-start | bytes 3076
  65.7 1.3 copy-start.4
  152.5 1.5 copy-start.1
  152.7 1.3 copy-start.2
  154.1 1.3 copy-start
  208.6 1.5 copy-start.1
  208.8 1.3 copy-start.2
  210.2 1.3 copy-start
  264.8 1.5 copy-start.1
  265.0 1.3 copy-start.2
  266.4 1.3 copy-start
  321.0 1.5 copy-start.1
  321.2 1.3 copy-start.2
  322.6 1.3 copy-start
Sparse Core Ops, SparseCore 0:
  9.5 51.9 all-gather.2
  68.7 27.0 all-gather.4

commit v5 on v4

--- a/solution.py
+++ b/solution.py
@@ -71,7 +71,7 @@
     return (-neg_re, -neg_im)
 
 
-def slab_blocks(hamiltonian, coupling, deform, fetched, energy, first_mask, last_mask):
+def slab_blocks(hamiltonian, deform, fetched, energy, first_mask, last_mask, lead_term):
     orbitals = hamiltonian.shape[-1]
     positions = jnp.arange(orbitals)
     distance = jnp.abs(positions[:, None] - positions[None, :]).astype(hamiltonian.dtype)
@@ -81,13 +81,12 @@
     sigma_re = weight * mixed_part[:, 0]
     sigma_im = weight * mixed_part[:, 1]
     eye_mat = jnp.eye(orbitals, dtype=hamiltonian.dtype)
-    lead_term = lead_scale * jnp.matmul(jnp.swapaxes(coupling, 1, 2), coupling, precision=HI)
     block_re = hamiltonian - energy * eye_mat + sigma_re
     block_im = (
         broaden * eye_mat
         - sigma_im
         + first_mask[:, None, None] * lead_gamma * eye_mat
-        + last_mask[:, None, None] * lead_term
+        + last_mask[:, None, None] * lead_term[None]
     )
     return (block_re, block_im)
 
@@ -100,36 +99,63 @@
     return (lower_level, upper_level)
 
 
+def band_windows(orbitals):
+    rows = BW
+    width = rows + 2 * BW
+    if orbitals % rows or width > orbitals:
+        return None
+    return [(r * rows, min(max(r * rows - BW, 0), orbitals - width)) for r in range(orbitals // rows)], rows, width
+
+
+def pack_band(matrix, windows):
+    spots, rows, width = windows
+    return jnp.stack([matrix[..., r0:r0 + rows, c0:c0 + width] for r0, c0 in spots], axis=-3)
+
+
+def unpack_band(packed, windows, orbitals):
+    spots, rows, width = windows
+    pieces = []
+    for index, (r0, c0) in enumerate(spots):
+        pad = [(0, 0)] * (packed.ndim - 3) + [(0, 0), (c0, orbitals - c0 - width)]
+        pieces.append(jnp.pad(packed[..., index, :, :], pad))
+    return jnp.concatenate(pieces, axis=-2)
+
+
 def body(hamiltonian, coupling, deform, green_prev, energy_grid, slot_energy, phonon_offsets):
     local_slabs = hamiltonian.shape[0]
+    orbitals = hamiltonian.shape[-1]
     level_count = slot_energy.shape[0]
     dom_count = lax.axis_size("dom")
     dom_index = lax.axis_index("dom")
     slab_total = local_slabs * dom_count
+    dense = lax.all_gather(jnp.stack([hamiltonian, coupling]), "dom", axis=1, tiled=True)
+    all_deform = lax.all_gather(deform, "dom", axis=0, tiled=True)
+    windows = band_windows(orbitals)
+    shipped = green_prev if windows is None else pack_band(green_prev, windows)
+    gathered = lax.all_gather(shipped, "energy", axis=0, tiled=True)
     own_slot = lax.axis_index("energy")
     energy_level = slot_energy[own_slot]
     energy = energy_grid[energy_level]
     lower_level, upper_level = partner_levels(energy_level, phonon_offsets, level_count)
-    weights = emission_weight * (slot_energy == lower_level).astype(jnp.float32) + absorb_weight * (
-        slot_energy == upper_level
-    ).astype(jnp.float32)
-    fetched = jnp.einsum(
-        "n,nsabc->sabc",
-        weights,
-        lax.all_gather(green_prev, "energy", axis=0, tiled=True).astype(jnp.float32),
-        precision=HI,
-    )
-    global_index = dom_index * local_slabs + jnp.arange(local_slabs)
+    lower_slot = jnp.argmax(slot_energy == jnp.maximum(lower_level, 0))
+    upper_slot = jnp.argmax(slot_energy == jnp.maximum(upper_level, 0))
+    low_weight = jnp.where(lower_level >= 0, emission_weight, 0.0)
+    high_weight = jnp.where(upper_level >= 0, absorb_weight, 0.0)
+    fetched = low_weight * gathered[lower_slot].astype(jnp.float32) + high_weight * gathered[
+        upper_slot
+    ].astype(jnp.float32)
+    all_fetched = lax.all_gather(fetched, "dom", axis=0, tiled=True)
+    if windows is not None:
+        all_fetched = unpack_band(all_fetched, windows, orbitals)
+    all_link = dense[1]
+    last_link = all_link[slab_total - 1]
+    lead_term = lead_scale * jnp.matmul(last_link.T, last_link, precision=HI)
+    global_index = jnp.arange(slab_total)
     first_mask = (global_index == 0).astype(jnp.float32)
     last_mask = (global_index == slab_total - 1).astype(jnp.float32)
-    block_re, block_im = slab_blocks(
-        hamiltonian, coupling, deform, fetched, energy, first_mask, last_mask
+    all_re, all_im = slab_blocks(
+        dense[0], all_deform, all_fetched, energy, first_mask, last_mask, lead_term
     )
-    gathered = lax.all_gather(
-        jnp.stack([block_re, block_im, coupling]), "dom", axis=1, tiled=True
-    )
-    all_re, all_im, all_link = gathered[0], gathered[1], gathered[2]
-    orbitals = hamiltonian.shape[-1]
     zero_block = jnp.zeros((orbitals, orbitals), jnp.float32)
 
     outputs = []

time: 333 us -> 386 us (1.16)
  blocking collectives: 0 us -> 93 us
  waiting for transfers between devices: 73 us -> 0.02 us
  local copies, waits for them, and re-layouts: 9.44 us -> 29.5 us
  other arithmetic: 17.5 us -> 29 us
    all_gather x0 -> x3, blocking collectives: none -> 93 us  [the longest x1 66.5 us: body(): gathered = lax.all_gather(shipped, 'energy', axis=0, tiled=True)]
    all_gather x2 -> x1, waiting for transfers between devices: 72.2 us -> 0.01 us  [body(): lax.all_gather(jnp.stack([hamiltonian, coupling]), 'dom', axis=1, tiled=T...]
    pad x0 -> x8, local copies, waits for them, and re-layouts: none -> 8.66 us  [unpack_band(): pieces.append(jnp.pad(packed[..., index, :, :], pad))]
    concatenate x0 -> x2, local copies, waits for them, and re-layouts: none -> 7.8 us  [unpack_band(): return jnp.concatenate(pieces, axis=-2)]
    unnamed x6 -> x18, local copies, waits for them, and re-layouts: 0.01 us -> 5.49 us
  transfers between devices with their start and end apart: 2 -> 1, of which waited for: 2 -> 0; matrix products, arithmetic and copies ran while one was open for 1% -> 9% of each run, Pallas kernels for 0% -> 0%
where the time goes in v5:
time: 386 us; the launch traced here: 385 us
  Pallas kernels  201 us (52%)
  blocking collectives  93 us (24%)
  local copies, waits for them, and re-layouts  29.5 us (8%)
  other arithmetic  29 us (8%)
  between operations  21.6 us (6%)
  matrix products  9.6 us (2%)
    pallas_call x4, Pallas kernels, invert_pair(): pl.pallas_call(sweep_kernel, out_shape=(jax.ShapeDtypeStruct((n, n), jnp....  201 us
    all_gather x1, blocking collectives, body(): gathered = lax.all_gather(shipped, 'energy', axis=0, tiled=True)  66.5 us
    all_gather x1, blocking collectives, body(): all_fetched = lax.all_gather(fetched, 'dom', axis=0, tiled=True)  21.5 us
    pad x8, local copies, waits for them, and re-layouts, unpack_band(): pieces.append(jnp.pad(packed[..., index, :, :], pad))  8.66 us
    concatenate x2, local copies, waits for them, and re-layouts, unpack_band(): return jnp.concatenate(pieces, axis=-2)  7.8 us
    neg x4, other arithmetic, invert_pair(): -block_im  7.76 us
  transfers between devices with their start and end apart: 1, of which 0 were waited for; matrix products, arithmetic and copies ran while one was open for 9% of the time, Pallas kernels for 0%

profile of v5, /device:TPU:0, one launch (start us, length us, event | category | flops | bytes accessed | tf_op | source)
XLA Modules:
  0.0 384.8 jit_solution(11790655834280114872)
XLA Ops:
  6.5 1.9 pad_maximum_fusion
  8.4 1.3 dynamic_slice.48
  11.5 1.4 constant_dynamic-slice_fusion.1
  14.1 1.3 compare_reduce_fusion.1
  17.9 1.3 compare_reduce_fusion
  28.3 66.5 %all_gather.14 = bf16[8,1,2,8,32,96]{4,5,0,2,3,1:T(8,128)(2,1)S(1)} all-gather(bf16[1,1,2,8,32,96]{4,5,0,2,3,1:T(8,128)(2,1)S(1)} %copy.36), channel_id=1, replica_groups=mesh['energy'=8,'dom'=4] {'energy'}, dimensions={0}, use_global_device_ids=true | all-gather | bytes 884736 | tf_op jit(solution)/shard_map/all_gather | solution.py:135
  94.9 21.5 %all-gather = f32[4,1,2,8,32,96]{4,5,0,2,3,1:T(8,128)S(1)} all-gather(f32[1,1,2,8,32,96]{4,5,0,2,3,1:T(8,128)S(1)} %multiply_add_fusion), channel_id=2, replica_groups=mesh['energy'=8,'dom'=4] {'dom'}, dimensions={0}, use_global_device_ids=true | all-gather | bytes 983040 | tf_op jit(solution)/shard_map/all_gather | solution.py:147
  125.3 6.0 %concatenate.3 = f32[4,2,256,256]{2,3,0,1:T(8,128)S(1)} concatenate(f32[4,2,32,256]{2,3,0,1:T(8,128)} %pad.30, f32[4,2,32,256]{2,3,0,1:T(8,128)} %pad.31, f32[4,2,32,256]{2,3,0,1:T(8,128)} %pad.32, f32[4,2,32,256]{2,3,0,1:T(8,128)} %pad.33, f32[4,2,32,256]{2,3,0,1:T(8,128)} %pad.34, f32[4,2,32,256]{2,3,0,1:T(8,128)} %pad.35, f32[4,2,32,256]{2,3,0,1:T(8,128)} %pad.36, ...), dimensions={2} | concatenate | bytes 4194304 | tf_op jit(solution)/shard_map/concatenate | solution.py:121
  131.4 1.8 copy.37
  133.8 5.1 %all-gather.1 = f32[4,1,256]{2,1,0:T(1,128)S(1)} all-gather(f32[1,1,256]{2,1,0:T(1,128)S(1)} %bitcast.167), channel_id=1, replica_groups=mesh['energy'=8,'dom'=4] {'dom'}, dimensions={0}, use_global_device_ids=true | all-gather | bytes 5120 | tf_op jit(solution)/shard_map/all_gather | solution.py:132
  138.9 1.3 fusion.16
  141.1 3.2 fusion.6
  144.3 1.8 convolution_multiply_fusion
  146.0 1.3 slice_bitcast_fusion.3
  147.4 3.1 fusion.10
  150.5 224.7 %while.27 = (s32[]{:T(128)}, f32[256,256]{1,0:T(8,128)S(1)}, f32[256,256]{1,0:T(8,128)S(1)}, f32[256,256]{1,0:T(8,128)S(1)}, f32[256,256]{1,0:T(8,128)S(1)}, /*i...) while((s32[]{:T(128)}, f32[256,256]{1,0:T(8,128)S(1)}, ...), condition=%wide.region_3.4_spmd.clone.clone, body=%wide.region_2.3_spmd.clone.sunk.clone | while | flops 807206912 | bytes 15466885 | solution.py:191
  150.5 1.9 fusion.63
  152.4 50.3 %eval_jaxpr.8 = (f32[256,256]{1,0:T(8,128)}, f32[256,256]{1,0:T(8,128)}) custom-call(f32[256,256]{1,0:T(8,128)} %get-tuple-element.451.ar_ref, f32[256,256]{1,0:T(8,128)} %get-tuple-element.452.ai_ref), custom_call_target="tpu_custom_call" | custom-call | tf_op jit(solution)/shard_map/while/body/eval_jaxpr/pallas_call | solution.py:65
  206.7 1.9 fusion.63
  208.6 50.3 %eval_jaxpr.8 = (f32[256,256]{1,0:T(8,128)}, f32[256,256]{1,0:T(8,128)}) custom-call(f32[256,256]{1,0:T(8,128)} %get-tuple-element.451.ar_ref, f32[256,256]{1,0:T(8,128)} %get-tuple-element.452.ai_ref), custom_call_target="tpu_custom_call" | custom-call | tf_op jit(solution)/shard_map/while/body/eval_jaxpr/pallas_call | solution.py:65
  262.9 1.9 fusion.63
  264.8 50.3 %eval_jaxpr.8 = (f32[256,256]{1,0:T(8,128)}, f32[256,256]{1,0:T(8,128)}) custom-call(f32[256,256]{1,0:T(8,128)} %get-tuple-element.451.ar_ref, f32[256,256]{1,0:T(8,128)} %get-tuple-element.452.ai_ref), custom_call_target="tpu_custom_call" | custom-call | tf_op jit(solution)/shard_map/while/body/eval_jaxpr/pallas_call | solution.py:65
  319.0 1.9 fusion.63
  321.0 50.3 %eval_jaxpr.8 = (f32[256,256]{1,0:T(8,128)}, f32[256,256]{1,0:T(8,128)}) custom-call(f32[256,256]{1,0:T(8,128)} %get-tuple-element.451.ar_ref, f32[256,256]{1,0:T(8,128)} %get-tuple-element.452.ai_ref), custom_call_target="tpu_custom_call" | custom-call | tf_op jit(solution)/shard_map/while/body/eval_jaxpr/pallas_call | solution.py:65
  (124 shorter events, 34.7 us)
Async XLA Ops:
  6.5 137.7 %all-gather.4.cloned.1.call-start = ((), (), s32[]{:S(2)}) async-start(), calls=%async_computation | async-start | bytes 2621440 | tf_op jit(solution)/shard_map/all_gather | solution.py:131
  131.3 1.9 copy-start.7
  131.3 2.4 copy-start.6
  144.3 3.1 copy-start.4
  144.3 3.1 copy-start.5
  144.3 3.1 copy-start.2
  203.8 1.5 copy-start.1
  204.0 1.4 copy-start.3
  205.3 1.3 copy-start
  259.9 1.5 copy-start.1
  260.1 1.3 copy-start.3
  261.5 1.3 copy-start
  316.1 1.5 copy-start.1
  316.3 1.3 copy-start.3
  317.7 1.3 copy-start
  372.3 1.5 copy-start.1
  372.5 1.3 copy-start.3
  373.9 1.3 copy-start
Sparse Core Ops, SparseCore 0:
  8.9 25.2 all-gather.3

commit v6 on v4

--- a/solution.py
+++ b/solution.py
@@ -92,6 +92,17 @@
     return (block_re, block_im)
 
 
+def gathered_over_dom(array):
+    peers = lax.axis_size("dom")
+    pieces = [array]
+    for shift in range(1, peers):
+        pairs = [(i, (i + shift) % peers) for i in range(peers)]
+        pieces.append(lax.ppermute(array, "dom", pairs))
+    order = (lax.axis_index("dom") - jnp.arange(peers)) % peers
+    stacked = jnp.stack(pieces)[order]
+    return stacked.reshape((peers * array.shape[0],) + array.shape[1:])
+
+
 def partner_levels(energy_level, phonon_offsets, level_count):
     lower_level = energy_level - phonon_offsets[0, energy_level]
     upper_level = energy_level + phonon_offsets[1, energy_level]
@@ -102,34 +113,32 @@
 
 def body(hamiltonian, coupling, deform, green_prev, energy_grid, slot_energy, phonon_offsets):
     local_slabs = hamiltonian.shape[0]
+    orbitals = hamiltonian.shape[-1]
     level_count = slot_energy.shape[0]
     dom_count = lax.axis_size("dom")
     dom_index = lax.axis_index("dom")
     slab_total = local_slabs * dom_count
+    all_link = gathered_over_dom(coupling)
+    gathered = lax.all_gather(green_prev, "energy", axis=0, tiled=True)
     own_slot = lax.axis_index("energy")
     energy_level = slot_energy[own_slot]
     energy = energy_grid[energy_level]
     lower_level, upper_level = partner_levels(energy_level, phonon_offsets, level_count)
-    weights = emission_weight * (slot_energy == lower_level).astype(jnp.float32) + absorb_weight * (
-        slot_energy == upper_level
-    ).astype(jnp.float32)
-    fetched = jnp.einsum(
-        "n,nsabc->sabc",
-        weights,
-        lax.all_gather(green_prev, "energy", axis=0, tiled=True).astype(jnp.float32),
-        precision=HI,
-    )
+    lower_slot = jnp.argmax(slot_energy == jnp.maximum(lower_level, 0))
+    upper_slot = jnp.argmax(slot_energy == jnp.maximum(upper_level, 0))
+    low_weight = jnp.where(lower_level >= 0, emission_weight, 0.0)
+    high_weight = jnp.where(upper_level >= 0, absorb_weight, 0.0)
+    fetched = low_weight * gathered[lower_slot].astype(jnp.float32) + high_weight * gathered[
+        upper_slot
+    ].astype(jnp.float32)
     global_index = dom_index * local_slabs + jnp.arange(local_slabs)
     first_mask = (global_index == 0).astype(jnp.float32)
     last_mask = (global_index == slab_total - 1).astype(jnp.float32)
     block_re, block_im = slab_blocks(
         hamiltonian, coupling, deform, fetched, energy, first_mask, last_mask
     )
-    gathered = lax.all_gather(
-        jnp.stack([block_re, block_im, coupling]), "dom", axis=1, tiled=True
-    )
-    all_re, all_im, all_link = gathered[0], gathered[1], gathered[2]
-    orbitals = hamiltonian.shape[-1]
+    blocks = lax.all_gather(jnp.stack([block_re, block_im]), "dom", axis=1, tiled=True)
+    all_re, all_im = blocks[0], blocks[1]
     zero_block = jnp.zeros((orbitals, orbitals), jnp.float32)
 
     outputs = []

time: 333 us -> 330 us (level)
  waiting for transfers between devices: 73 us -> 63 us
  matrix products: 12.6 us -> 8.47 us
  between operations: 18 us -> 21.5 us
    all_gather x2, waiting for transfers between devices: 72.2 us -> 44.6 us  [the longest x1 39 us: body(): gathered = lax.all_gather(green_prev, 'energy', axis=0, tiled=True)]
    ppermute x0 -> x3, waiting for transfers between devices: none -> 17.7 us  [gathered_over_dom(): pieces.append(lax.ppermute(array, 'dom', pairs))]
    dot_general x1 -> x0, matrix products: 4.14 us -> none  [body(): jnp.einsum('n,nsabc->sabc', weights, lax.all_gather(green_prev, 'energy',...]
  transfers between devices with their start and end apart: 2 -> 5, of which waited for: 2 -> 5; matrix products, arithmetic and copies ran while one was open for 1% -> 2% of each run, Pallas kernels for 0% -> 0%
where the time goes in v6:
time: 330 us; the launch traced here: 329 us
  Pallas kernels  201 us (61%)
  waiting for transfers between devices  63 us (19%)
  between operations  21.5 us (7%)
  other arithmetic  20.2 us (6%)
  local copies, waits for them, and re-layouts  11.1 us (3%)
  matrix products  8.47 us (3%)
    pallas_call x4, Pallas kernels, invert_pair(): pl.pallas_call(sweep_kernel, out_shape=(jax.ShapeDtypeStruct((n, n), jnp....  201 us
    all_gather x1, waiting for transfers between devices, body(): gathered = lax.all_gather(green_prev, 'energy', axis=0, tiled=True)  39 us
    ppermute x3, waiting for transfers between devices, gathered_over_dom(): pieces.append(lax.ppermute(array, 'dom', pairs))  17.7 us
    neg x4, other arithmetic, invert_pair(): -block_im  7.75 us
  transfers between devices with their start and end apart: 5, of which 5 were waited for; matrix products, arithmetic and copies ran while one was open for 2% of the time, Pallas kernels for 0%

profile of v6, /device:TPU:0, one launch (start us, length us, event | category | flops | bytes accessed | tf_op | source)
XLA Modules:
  0.0 329.4 jit_solution(716152311875702693)
XLA Ops:
  7.3 1.2 dynamic_slice.48
  10.5 1.4 constant_dynamic-slice_fusion.3
  13.2 1.4 compare_reduce_fusion.1
  17.0 1.3 compare_reduce_fusion
  19.4 1.2 dynamic_slice.49
  22.5 39.0 %all-gather.3.cloned.1.call-done = bf16[8,1,2,256,256]{4,3,2,1,0:T(8,128)(2,1)} async-done(((bf16[1,1,2,256,256]{4,3,2,1,0:T(8,128)(2,1)}), bf16[8,1,2,256,256]{4,3,2,1,0:T(8,128)(2,1)}) %all-gather.3.cloned.1.call-update) | async-done | bytes 2097168 | tf_op jit(solution)/shard_map/all_gather | solution.py:122
  61.5 1.1 constant_dynamic-slice_fusion.2
  66.1 1.5 collective-permute-start.1
  67.6 1.4 collective-permute-start.2
  69.0 5.0 %collective-permute-done = f32[1,256,256]{2,1,0:T(8,128)S(1)} collective-permute-done((f32[1,256,256]{2,1,0:T(8,128)S(1)}, f32[1,256,256]{2,1,0:T(8,128)S(1)}, u32[]{:S(2)}, u32[]{:S(2)}) %collective-permute-start) | collective-permute-done | bytes 262176 | tf_op jit(solution)/shard_map/ppermute | solution.py:100
  74.0 2.0 collective-permute-done.1
  76.1 10.6 %collective-permute-done.2 = f32[1,256,256]{2,1,0:T(8,128)S(1)} collective-permute-done((f32[1,256,256]{2,1,0:T(8,128)S(1)}, f32[1,256,256]{2,1,0:T(8,128)S(1)}, u32[]{:S(2)}, u32[]{:S(2)}) %collective-permute-start.2) | collective-permute-done | bytes 262176 | tf_op jit(solution)/shard_map/ppermute | solution.py:100
  87.4 5.6 %all-gather.5.cloned.1.call-done = f32[2,4,256,256]{3,2,1,0:T(8,128)} async-done(((f32[2,1,256,256]{3,2,1,0:T(8,128)}), f32[2,4,256,256]{3,2,1,0:T(8,128)}) %all-gather.5.cloned.1.call-update) | async-done | bytes 2097168 | tf_op jit(solution)/shard_map/all_gather | solution.py:140
  93.0 3.0 slice_bitcast_fusion
  96.0 224.6 %while.27 = (s32[]{:T(128)}, f32[256,256]{1,0:T(8,128)S(1)}, f32[256,256]{1,0:T(8,128)S(1)}, f32[256,256]{1,0:T(8,128)S(1)}, f32[256,256]{1,0:T(8,128)S(1)}, /*i...) while((s32[]{:T(128)}, f32[256,256]{1,0:T(8,128)S(1)}, ...), condition=%wide.region_3.4_spmd.clone.clone, body=%wide.region_2.3_spmd.clone.sunk.clone | while | flops 807206912 | bytes 15466885 | solution.py:174
  96.0 1.9 fusion.66
  97.9 50.3 %eval_jaxpr.8 = (f32[256,256]{1,0:T(8,128)}, f32[256,256]{1,0:T(8,128)}) custom-call(f32[256,256]{1,0:T(8,128)} %get-tuple-element.445.ar_ref, f32[256,256]{1,0:T(8,128)} %get-tuple-element.446.ai_ref), custom_call_target="tpu_custom_call" | custom-call | tf_op jit(solution)/shard_map/while/body/eval_jaxpr/pallas_call | solution.py:65
  152.2 1.9 fusion.66
  154.1 50.3 %eval_jaxpr.8 = (f32[256,256]{1,0:T(8,128)}, f32[256,256]{1,0:T(8,128)}) custom-call(f32[256,256]{1,0:T(8,128)} %get-tuple-element.445.ar_ref, f32[256,256]{1,0:T(8,128)} %get-tuple-element.446.ai_ref), custom_call_target="tpu_custom_call" | custom-call | tf_op jit(solution)/shard_map/while/body/eval_jaxpr/pallas_call | solution.py:65
  208.3 1.9 fusion.66
  210.3 50.3 %eval_jaxpr.8 = (f32[256,256]{1,0:T(8,128)}, f32[256,256]{1,0:T(8,128)}) custom-call(f32[256,256]{1,0:T(8,128)} %get-tuple-element.445.ar_ref, f32[256,256]{1,0:T(8,128)} %get-tuple-element.446.ai_ref), custom_call_target="tpu_custom_call" | custom-call | tf_op jit(solution)/shard_map/while/body/eval_jaxpr/pallas_call | solution.py:65
  264.5 1.9 fusion.66
  266.4 50.3 %eval_jaxpr.8 = (f32[256,256]{1,0:T(8,128)}, f32[256,256]{1,0:T(8,128)}) custom-call(f32[256,256]{1,0:T(8,128)} %get-tuple-element.445.ar_ref, f32[256,256]{1,0:T(8,128)} %get-tuple-element.446.ai_ref), custom_call_target="tpu_custom_call" | custom-call | tf_op jit(solution)/shard_map/while/body/eval_jaxpr/pallas_call | solution.py:65
  320.6 1.1 negate_bitcast_fusion
  (107 shorter events, 21.2 us)
Async XLA Ops:
  6.5 55.0 %all-gather.3.cloned.1.call-start = ((), (), s32[]{:S(2)}) async-start(), calls=%async_computation | async-start | bytes 2359296 | tf_op jit(solution)/shard_map/all_gather | solution.py:122
  7.3 85.8 %all-gather.5.cloned.1.call-start = ((), (), s32[]{:S(2)}) async-start(), calls=%async_computation.1 | async-start | bytes 2621440 | tf_op jit(solution)/shard_map/all_gather | solution.py:140
  62.7 1.0 copy-start.3
  62.7 0.9 copy-start.5
  62.9 1.6 copy-start.4
  66.0 8.0 %collective-permute-start = (f32[1,256,256]{2,1,0:T(8,128)S(1)}, f32[1,256,256]{2,1,0:T(8,128)S(1)}, u32[]{:S(2)}, u32[]{:S(2)}) collective-permute-start(f32[1,256,256]{2,1,0:T(8,128)S(1)} %copy-done.4), channel_id=1, source_target_pairs={{0,1},{1,2},{2,3},{3,0},{4,5},{5,6},{6,7},{7,4},{8,9},{9,10},{10,1... | collective-permute-start | bytes 786440 | tf_op jit(solution)/shard_map/ppermute | solution.py:100
  66.1 10.0 %collective-permute-start.1 = (f32[1,256,256]{2,1,0:T(8,128)S(1)}, f32[1,256,256]{2,1,0:T(8,128)S(1)}, u32[]{:S(2)}, u32[]{:S(2)}) collective-permute-start(f32[1,256,256]{2,1,0:T(8,128)S(1)} %copy-done.4), channel_id=1, source_target_pairs={{0,2},{1,3},{2,0},{3,1},{4,6},{5,7},{6,4},{7,5},{8,10},{9,11},{10,... | collective-permute-start | bytes 786440 | tf_op jit(solution)/shard_map/ppermute | solution.py:100
  67.6 19.1 %collective-permute-start.2 = (f32[1,256,256]{2,1,0:T(8,128)S(1)}, f32[1,256,256]{2,1,0:T(8,128)S(1)}, u32[]{:S(2)}, u32[]{:S(2)}) collective-permute-start(f32[1,256,256]{2,1,0:T(8,128)S(1)} %copy-done.4), channel_id=1, source_target_pairs={{0,3},{1,0},{2,1},{3,2},{4,7},{5,4},{6,5},{7,6},{8,11},{9,8},{10,9... | collective-permute-start | bytes 786440 | tf_op jit(solution)/shard_map/ppermute | solution.py:100
  149.2 1.5 copy-start.1
  149.4 1.3 copy-start.2
  150.8 1.3 copy-start
  205.4 1.5 copy-start.1
  205.6 1.3 copy-start.2
  207.0 1.3 copy-start
  261.6 1.5 copy-start.1
  261.8 1.4 copy-start.2
  263.1 1.3 copy-start
  317.7 1.5 copy-start.1
  317.9 1.4 copy-start.2
  319.3 1.3 copy-start
Sparse Core Ops, SparseCore 0:
  9.5 51.9 all-gather.2
  66.1 26.8 all-gather.4

commit v7 on v6

--- a/solution.py
+++ b/solution.py
@@ -22,11 +22,23 @@
     return 0.5 * (matrix + jnp.swapaxes(matrix, -1, -2))
 
 
-def sweep_kernel(ar_ref, ai_ref, or_ref, oi_ref):
-    n = ar_ref.shape[0]
+def sweep_kernel(
+    scalars, blk_re_ref, blk_im_ref, lre_ref, lim_ref, rre_ref, rim_ref, or_ref, oi_ref
+):
+    n = or_ref.shape[0]
     half = n // 2
-    or_ref[...] = ar_ref[...]
-    oi_ref[...] = ai_ref[...]
+    use_left = scalars[1] == 1
+    use_right = scalars[2] == 1
+    or_ref[...] = (
+        blk_re_ref[...]
+        + jnp.where(use_left, lre_ref[...], 0.0)
+        + jnp.where(use_right, rre_ref[...], 0.0)
+    )
+    oi_ref[...] = -(
+        blk_im_ref[...]
+        + jnp.where(use_left, lim_ref[...], 0.0)
+        + jnp.where(use_right, rim_ref[...], 0.0)
+    )
 
     def pivot(k, carry):
         lanes = lax.broadcasted_iota(jnp.int32, (1, n), 1)
@@ -59,16 +71,21 @@
     lax.fori_loop(0, n, pivot, 0)
 
 
-def invert_pair(block_re, block_im):
-    n = block_re.shape[-1]
-    spec = pl.BlockSpec(memory_space=pltpu.VMEM)
-    neg_re, neg_im = pl.pallas_call(
+def neg_inverse_step(scalars, all_re, all_im, left_re, left_im, right_re, right_im):
+    n = all_re.shape[-1]
+    slab_spec = pl.BlockSpec((None, n, n), lambda i, sc: (sc[0], 0, 0))
+    full_spec = pl.BlockSpec((n, n), lambda i, sc: (0, 0))
+    grid_spec = pltpu.PrefetchScalarGridSpec(
+        num_scalar_prefetch=1,
+        grid=(1,),
+        in_specs=[slab_spec, slab_spec, full_spec, full_spec, full_spec, full_spec],
+        out_specs=[full_spec, full_spec],
+    )
+    return pl.pallas_call(
         sweep_kernel,
         out_shape=(jax.ShapeDtypeStruct((n, n), jnp.float32),) * 2,
-        in_specs=[spec, spec],
-        out_specs=(spec, spec),
-    )(block_re, -block_im)
-    return (-neg_re, -neg_im)
+        grid_spec=grid_spec,
+    )(scalars, all_re, all_im, left_re, left_im, right_re, right_im)
 
 
 def slab_blocks(hamiltonian, coupling, deform, fetched, energy, first_mask, last_mask):
@@ -152,27 +169,28 @@
             slab = jnp.where(is_left, step, slab_total - 1 - step + own)
             use_left = jnp.logical_or(is_left, is_final)
             use_right = jnp.logical_not(is_left)
-            in_re = all_re[slab] + jnp.where(use_left, left_re, 0.0) + jnp.where(use_right, right_re, 0.0)
-            in_im = all_im[slab] + jnp.where(use_left, left_im, 0.0) + jnp.where(use_right, right_im, 0.0)
-            inv_re, inv_im = invert_pair(in_re, in_im)
+            scalars = jnp.stack([slab, use_left, use_right]).astype(jnp.int32)
+            neg_re, neg_im = neg_inverse_step(
+                scalars, all_re, all_im, left_re, left_im, right_re, right_im
+            )
             link_index = jnp.where(is_left, step, jnp.maximum(slab - 1, 0))
             link_block = all_link[link_index]
             link_block = jnp.where(is_left, link_block, link_block.T)
-            next_re = -symmetric(
-                jnp.dot(link_block.T, jnp.dot(inv_re, link_block, precision=HI), precision=HI)
+            next_re = symmetric(
+                jnp.dot(link_block.T, jnp.dot(neg_re, link_block, precision=HI), precision=HI)
             )
-            next_im = symmetric(
-                jnp.dot(link_block.T, jnp.dot(inv_im, link_block, precision=HI), precision=HI)
+            next_im = -symmetric(
+                jnp.dot(link_block.T, jnp.dot(neg_im, link_block, precision=HI), precision=HI)
             )
             left_re = jnp.where(is_left, next_re, left_re)
             left_im = jnp.where(is_left, next_im, left_im)
             keep_right = jnp.logical_or(is_left, is_final)
             right_re = jnp.where(keep_right, right_re, next_re)
             right_im = jnp.where(keep_right, right_im, next_im)
-            return (left_re, left_im, right_re, right_im, inv_re, inv_im)
+            return (left_re, left_im, right_re, right_im, neg_re, neg_im)
 
         carry = lax.fori_loop(0, slab_total, chain_step, (zero_block,) * 6)
-        outputs.append(jnp.stack([-carry[4], -carry[5]]))
+        outputs.append(jnp.stack([carry[4], carry[5]]))
     return jnp.stack(outputs)[None]
 
 

time: 330 us -> 348 us (1.055)
  other arithmetic: 20.2 us -> 33.2 us
  local copies, waits for them, and re-layouts: 11.1 us -> 16.5 us
    while x0 -> x8, other arithmetic: none -> 12.8 us
    neg x12 -> x0, other arithmetic: 11.7 us -> none  [the longest x4 7.75 us: invert_pair(): -block_im]
    dynamic_slice x8, local copies, waits for them, and re-layouts: 0.61 us -> 5.23 us  [chain_step(): link_block = all_link[link_index]]
    select_n x4, other arithmetic: 0.14 us -> 3.96 us  [chain_step(): link_block = jnp.where(is_left, link_block, link_block.T)]
  transfers between devices with their start and end apart: 5 -> 5, of which waited for: 5 -> 5; matrix products, arithmetic and copies ran while one was open for 2% -> 3% of each run, Pallas kernels for 0% -> 0%
where the time goes in v7:
time: 348 us; the launch traced here: 347 us
  Pallas kernels  201 us (58%)
  waiting for transfers between devices  61.9 us (18%)
  other arithmetic  33.2 us (10%)
  between operations  21.8 us (6%)
  local copies, waits for them, and re-layouts  16.5 us (5%)
  matrix products  8.45 us (2%)
    pallas_call x4, Pallas kernels, neg_inverse_step(): pl.pallas_call(sweep_kernel, out_shape=(jax.ShapeDtypeStruct((n, n), jnp....  201 us
    all_gather x1, waiting for transfers between devices, body(): gathered = lax.all_gather(green_prev, 'energy', axis=0, tiled=True)  38.9 us
    ppermute x3, waiting for transfers between devices, gathered_over_dom(): pieces.append(lax.ppermute(array, 'dom', pairs))  17.7 us
    while x8, other arithmetic  12.8 us
  transfers between devices with their start and end apart: 5, of which 5 were waited for; matrix products, arithmetic and copies ran while one was open for 3% of the time, Pallas kernels for 0%

profile of v7, /device:TPU:0, one launch (start us, length us, event | category | flops | bytes accessed | tf_op | source)
XLA Modules:
  0.0 346.9 jit_solution(5388830394514552544)
XLA Ops:
  10.5 1.4 constant_dynamic-slice_fusion.3
  13.2 1.4 compare_reduce_fusion.1
  17.2 1.3 compare_reduce_fusion
  22.8 38.9 %all-gather.3.cloned.1.call-done = bf16[8,1,2,256,256]{4,3,2,1,0:T(8,128)(2,1)} async-done(((bf16[1,1,2,256,256]{4,3,2,1,0:T(8,128)(2,1)}), bf16[8,1,2,256,256]{4,3,2,1,0:T(8,128)(2,1)}) %all-gather.3.cloned.1.call-update) | async-done | bytes 2097168 | tf_op jit(solution)/shard_map/all_gather | solution.py:139
  66.2 1.5 collective-permute-start.1
  67.8 1.4 collective-permute-start.2
  69.2 5.0 %collective-permute-done = f32[1,256,256]{2,1,0:T(8,128)S(1)} collective-permute-done((f32[1,256,256]{2,1,0:T(8,128)S(1)}, f32[1,256,256]{2,1,0:T(8,128)S(1)}, u32[]{:S(2)}, u32[]{:S(2)}) %collective-permute-start) | collective-permute-done | bytes 262176 | tf_op jit(solution)/shard_map/ppermute | solution.py:117
  74.2 2.0 collective-permute-done.1
  76.3 10.6 %collective-permute-done.2 = f32[1,256,256]{2,1,0:T(8,128)S(1)} collective-permute-done((f32[1,256,256]{2,1,0:T(8,128)S(1)}, f32[1,256,256]{2,1,0:T(8,128)S(1)}, u32[]{:S(2)}, u32[]{:S(2)}) %collective-permute-start.2) | collective-permute-done | bytes 262176 | tf_op jit(solution)/shard_map/ppermute | solution.py:117
  87.0 1.6 gather_fusion
  88.6 4.6 %all-gather.5.cloned.1.call-done = f32[2,4,256,256]{3,2,1,0:T(8,128)} async-done(((f32[2,1,256,256]{3,2,1,0:T(8,128)}), f32[2,4,256,256]{3,2,1,0:T(8,128)}) %all-gather.5.cloned.1.call-update) | async-done | bytes 2097168 | tf_op jit(solution)/shard_map/all_gather | solution.py:157
  93.2 2.7 slice_bitcast_fusion
  95.9 242.2 %while.27 = (s32[]{:T(128)}, f32[256,256]{1,0:T(8,128)}, f32[256,256]{1,0:T(8,128)}, f32[256,256]{1,0:T(8,128)}, f32[256,256]{1,0:T(8,128)}, /*index=5*/f32[256,...) while((s32[]{:T(128)}, f32[256,256]{1,0:T(8,128)}, ...), condition=%wide.region_3.4_spmd.clone.clone, body=%wide.region_2.3_spmd.clone.sunk.clone | while | flops 806223872 | bytes 17564112 | solution.py:192
  98.2 50.3 %eval_jaxpr.8 = (f32[256,256]{1,0:T(8,128)S(1)}, f32[256,256]{1,0:T(8,128)S(1)}) custom-call(s32[3]{0:T(128)} %pad_add_fusion.3.scalars, f32[4,256,256]{2,1,0:T(8,128)} %get-tuple-element.500.blk_re_ref, f32[4,256,256]{2,1,0:T(8,128)S(1)} %get-tuple-element.501.blk_im_ref, f32[256,256]{1,0:T(8,128)} %get-tuple-element.444.lre_ref, ...), custom_call_target="tpu_custom_call" | custom-call | tf_op jit(solution)/shard_map/while/body/eval_jaxpr/pallas_call | solution.py:84
  155.5 1.8 broadcast_select_fusion.16
  157.4 1.9 broadcast_select_fusion.17
  159.3 50.3 %eval_jaxpr.8 = (f32[256,256]{1,0:T(8,128)S(1)}, f32[256,256]{1,0:T(8,128)S(1)}) custom-call(s32[3]{0:T(128)} %pad_add_fusion.3.scalars, f32[4,256,256]{2,1,0:T(8,128)} %get-tuple-element.500.blk_re_ref, f32[4,256,256]{2,1,0:T(8,128)S(1)} %get-tuple-element.501.blk_im_ref, f32[256,256]{1,0:T(8,128)} %get-tuple-element.444.lre_ref, ...), custom_call_target="tpu_custom_call" | custom-call | tf_op jit(solution)/shard_map/while/body/eval_jaxpr/pallas_call | solution.py:84
  216.6 1.8 broadcast_select_fusion.16
  218.5 1.9 broadcast_select_fusion.17
  220.3 50.3 %eval_jaxpr.8 = (f32[256,256]{1,0:T(8,128)S(1)}, f32[256,256]{1,0:T(8,128)S(1)}) custom-call(s32[3]{0:T(128)} %pad_add_fusion.3.scalars, f32[4,256,256]{2,1,0:T(8,128)} %get-tuple-element.500.blk_re_ref, f32[4,256,256]{2,1,0:T(8,128)S(1)} %get-tuple-element.501.blk_im_ref, f32[256,256]{1,0:T(8,128)} %get-tuple-element.444.lre_ref, ...), custom_call_target="tpu_custom_call" | custom-call | tf_op jit(solution)/shard_map/while/body/eval_jaxpr/pallas_call | solution.py:84
  277.7 1.8 broadcast_select_fusion.16
  279.5 1.9 broadcast_select_fusion.17
  281.4 50.3 %eval_jaxpr.8 = (f32[256,256]{1,0:T(8,128)S(1)}, f32[256,256]{1,0:T(8,128)S(1)}) custom-call(s32[3]{0:T(128)} %pad_add_fusion.3.scalars, f32[4,256,256]{2,1,0:T(8,128)} %get-tuple-element.500.blk_re_ref, f32[4,256,256]{2,1,0:T(8,128)S(1)} %get-tuple-element.501.blk_im_ref, f32[256,256]{1,0:T(8,128)} %get-tuple-element.444.lre_ref, ...), custom_call_target="tpu_custom_call" | custom-call | tf_op jit(solution)/shard_map/while/body/eval_jaxpr/pallas_call | solution.py:84
  338.2 1.9 maximum_bitcast_fusion.1
  (130 shorter events, 37.5 us)
Async XLA Ops:
  6.5 55.1 %all-gather.3.cloned.1.call-start = ((), (), s32[]{:S(2)}) async-start(), calls=%async_computation | async-start | bytes 2359296 | tf_op jit(solution)/shard_map/all_gather | solution.py:139
  7.3 86.0 %all-gather.5.cloned.1.call-start = ((), (), s32[]{:S(2)}) async-start(), calls=%async_computation.1 | async-start | bytes 2621440 | tf_op jit(solution)/shard_map/all_gather | solution.py:157
  66.2 8.0 %collective-permute-start = (f32[1,256,256]{2,1,0:T(8,128)S(1)}, f32[1,256,256]{2,1,0:T(8,128)S(1)}, u32[]{:S(2)}, u32[]{:S(2)}) collective-permute-start(f32[1,256,256]{2,1,0:T(8,128)S(1)} %copy-done.7), channel_id=1, source_target_pairs={{0,1},{1,2},{2,3},{3,0},{4,5},{5,6},{6,7},{7,4},{8,9},{9,10},{10,1... | collective-permute-start | bytes 786440 | tf_op jit(solution)/shard_map/ppermute | solution.py:117
  66.2 10.0 %collective-permute-start.1 = (f32[1,256,256]{2,1,0:T(8,128)S(1)}, f32[1,256,256]{2,1,0:T(8,128)S(1)}, u32[]{:S(2)}, u32[]{:S(2)}) collective-permute-start(f32[1,256,256]{2,1,0:T(8,128)S(1)} %copy-done.7), channel_id=1, source_target_pairs={{0,2},{1,3},{2,0},{3,1},{4,6},{5,7},{6,4},{7,5},{8,10},{9,11},{10,... | collective-permute-start | bytes 786440 | tf_op jit(solution)/shard_map/ppermute | solution.py:117
  67.8 19.1 %collective-permute-start.2 = (f32[1,256,256]{2,1,0:T(8,128)S(1)}, f32[1,256,256]{2,1,0:T(8,128)S(1)}, u32[]{:S(2)}, u32[]{:S(2)}) collective-permute-start(f32[1,256,256]{2,1,0:T(8,128)S(1)} %copy-done.7), channel_id=1, source_target_pairs={{0,3},{1,0},{2,1},{3,2},{4,7},{5,4},{6,5},{7,6},{8,11},{9,8},{10,9... | collective-permute-start | bytes 786440 | tf_op jit(solution)/shard_map/ppermute | solution.py:117
  148.5 4.4 %copy-start.5 = (f32[256,256]{1,0:T(8,128)}, f32[256,256]{1,0:T(8,128)S(1)}, u32[]{:S(2)}) copy-start(f32[256,256]{1,0:T(8,128)S(1)} %get-tuple-element.497) | copy-start | bytes 786436 | tf_op jit(solution)/shard_map/while
  148.6 4.4 %copy-start.4 = (f32[256,256]{1,0:T(8,128)}, f32[256,256]{1,0:T(8,128)S(1)}, u32[]{:S(2)}) copy-start(f32[256,256]{1,0:T(8,128)S(1)} %get-tuple-element.496) | copy-start | bytes 786436 | tf_op jit(solution)/shard_map/while
  148.6 3.5 %copy-start.2 = (f32[256,256]{1,0:T(8,128)S(1)}, f32[256,256]{1,0:T(8,128)}, u32[]{:S(2)}) copy-start(f32[256,256]{1,0:T(8,128)} %get-tuple-element.446.rim_ref) | copy-start | bytes 786436 | tf_op jit(solution)/shard_map/while
  148.6 3.5 %copy-start.3 = (f32[256,256]{1,0:T(8,128)S(1)}, f32[256,256]{1,0:T(8,128)}, u32[]{:S(2)}) copy-start(f32[256,256]{1,0:T(8,128)} %get-tuple-element.445.lim_ref) | copy-start | bytes 786436 | tf_op jit(solution)/shard_map/while
  151.9 2.2 copy-start
  151.9 2.2 copy-start.1
  209.6 4.4 %copy-start.5 = (f32[256,256]{1,0:T(8,128)}, f32[256,256]{1,0:T(8,128)S(1)}, u32[]{:S(2)}) copy-start(f32[256,256]{1,0:T(8,128)S(1)} %get-tuple-element.497) | copy-start | bytes 786436 | tf_op jit(solution)/shard_map/while
  209.6 4.4 %copy-start.4 = (f32[256,256]{1,0:T(8,128)}, f32[256,256]{1,0:T(8,128)S(1)}, u32[]{:S(2)}) copy-start(f32[256,256]{1,0:T(8,128)S(1)} %get-tuple-element.496) | copy-start | bytes 786436 | tf_op jit(solution)/shard_map/while
  209.6 3.5 %copy-start.2 = (f32[256,256]{1,0:T(8,128)S(1)}, f32[256,256]{1,0:T(8,128)}, u32[]{:S(2)}) copy-start(f32[256,256]{1,0:T(8,128)} %get-tuple-element.446.rim_ref) | copy-start | bytes 786436 | tf_op jit(solution)/shard_map/while
  209.7 3.5 %copy-start.3 = (f32[256,256]{1,0:T(8,128)S(1)}, f32[256,256]{1,0:T(8,128)}, u32[]{:S(2)}) copy-start(f32[256,256]{1,0:T(8,128)} %get-tuple-element.445.lim_ref) | copy-start | bytes 786436 | tf_op jit(solution)/shard_map/while
  270.7 4.4 %copy-start.5 = (f32[256,256]{1,0:T(8,128)}, f32[256,256]{1,0:T(8,128)S(1)}, u32[]{:S(2)}) copy-start(f32[256,256]{1,0:T(8,128)S(1)} %get-tuple-element.497) | copy-start | bytes 786436 | tf_op jit(solution)/shard_map/while
  270.7 4.4 %copy-start.4 = (f32[256,256]{1,0:T(8,128)}, f32[256,256]{1,0:T(8,128)S(1)}, u32[]{:S(2)}) copy-start(f32[256,256]{1,0:T(8,128)S(1)} %get-tuple-element.496) | copy-start | bytes 786436 | tf_op jit(solution)/shard_map/while
  270.7 3.5 %copy-start.2 = (f32[256,256]{1,0:T(8,128)S(1)}, f32[256,256]{1,0:T(8,128)}, u32[]{:S(2)}) copy-start(f32[256,256]{1,0:T(8,128)} %get-tuple-element.446.rim_ref) | copy-start | bytes 786436 | tf_op jit(solution)/shard_map/while
  270.7 3.5 %copy-start.3 = (f32[256,256]{1,0:T(8,128)S(1)}, f32[256,256]{1,0:T(8,128)}, u32[]{:S(2)}) copy-start(f32[256,256]{1,0:T(8,128)} %get-tuple-element.445.lim_ref) | copy-start | bytes 786436 | tf_op jit(solution)/shard_map/while
  274.0 2.2 copy-start
  331.8 4.4 %copy-start.5 = (f32[256,256]{1,0:T(8,128)}, f32[256,256]{1,0:T(8,128)S(1)}, u32[]{:S(2)}) copy-start(f32[256,256]{1,0:T(8,128)S(1)} %get-tuple-element.497) | copy-start | bytes 786436 | tf_op jit(solution)/shard_map/while
  331.8 4.4 %copy-start.4 = (f32[256,256]{1,0:T(8,128)}, f32[256,256]{1,0:T(8,128)S(1)}, u32[]{:S(2)}) copy-start(f32[256,256]{1,0:T(8,128)S(1)} %get-tuple-element.496) | copy-start | bytes 786436 | tf_op jit(solution)/shard_map/while
  331.8 3.5 %copy-start.2 = (f32[256,256]{1,0:T(8,128)S(1)}, f32[256,256]{1,0:T(8,128)}, u32[]{:S(2)}) copy-start(f32[256,256]{1,0:T(8,128)} %get-tuple-element.446.rim_ref) | copy-start | bytes 786436 | tf_op jit(solution)/shard_map/while
  331.8 3.5 %copy-start.3 = (f32[256,256]{1,0:T(8,128)S(1)}, f32[256,256]{1,0:T(8,128)}, u32[]{:S(2)}) copy-start(f32[256,256]{1,0:T(8,128)} %get-tuple-element.445.lim_ref) | copy-start | bytes 786436 | tf_op jit(solution)/shard_map/while
  (8 other events, 14.4 us)
Sparse Core Ops, SparseCore 0:
  9.5 52.1 all-gather.2
  66.3 26.8 all-gather.4

commit v8 on v6

--- a/solution.py
+++ b/solution.py
@@ -59,7 +59,7 @@
     lax.fori_loop(0, n, pivot, 0)
 
 
-def invert_pair(block_re, block_im):
+def neg_invert_pair(block_re, block_im):
     n = block_re.shape[-1]
     spec = pl.BlockSpec(memory_space=pltpu.VMEM)
     neg_re, neg_im = pl.pallas_call(
@@ -68,7 +68,7 @@
         in_specs=[spec, spec],
         out_specs=(spec, spec),
     )(block_re, -block_im)
-    return (-neg_re, -neg_im)
+    return (neg_re, neg_im)
 
 
 def slab_blocks(hamiltonian, coupling, deform, fetched, energy, first_mask, last_mask):
@@ -138,7 +138,6 @@
         hamiltonian, coupling, deform, fetched, energy, first_mask, last_mask
     )
     blocks = lax.all_gather(jnp.stack([block_re, block_im]), "dom", axis=1, tiled=True)
-    all_re, all_im = blocks[0], blocks[1]
     zero_block = jnp.zeros((orbitals, orbitals), jnp.float32)
 
     outputs = []
@@ -152,27 +151,27 @@
             slab = jnp.where(is_left, step, slab_total - 1 - step + own)
             use_left = jnp.logical_or(is_left, is_final)
             use_right = jnp.logical_not(is_left)
-            in_re = all_re[slab] + jnp.where(use_left, left_re, 0.0) + jnp.where(use_right, right_re, 0.0)
-            in_im = all_im[slab] + jnp.where(use_left, left_im, 0.0) + jnp.where(use_right, right_im, 0.0)
-            inv_re, inv_im = invert_pair(in_re, in_im)
+            in_re = blocks[0, slab] + jnp.where(use_left, left_re, 0.0) + jnp.where(use_right, right_re, 0.0)
+            in_im = blocks[1, slab] + jnp.where(use_left, left_im, 0.0) + jnp.where(use_right, right_im, 0.0)
+            neg_re, neg_im = neg_invert_pair(in_re, in_im)
             link_index = jnp.where(is_left, step, jnp.maximum(slab - 1, 0))
             link_block = all_link[link_index]
             link_block = jnp.where(is_left, link_block, link_block.T)
-            next_re = -symmetric(
-                jnp.dot(link_block.T, jnp.dot(inv_re, link_block, precision=HI), precision=HI)
+            next_re = symmetric(
+                jnp.dot(link_block.T, jnp.dot(neg_re, link_block, precision=HI), precision=HI)
             )
-            next_im = symmetric(
-                jnp.dot(link_block.T, jnp.dot(inv_im, link_block, precision=HI), precision=HI)
+            next_im = -symmetric(
+                jnp.dot(link_block.T, jnp.dot(neg_im, link_block, precision=HI), precision=HI)
             )
             left_re = jnp.where(is_left, next_re, left_re)
             left_im = jnp.where(is_left, next_im, left_im)
             keep_right = jnp.logical_or(is_left, is_final)
             right_re = jnp.where(keep_right, right_re, next_re)
             right_im = jnp.where(keep_right, right_im, next_im)
-            return (left_re, left_im, right_re, right_im, inv_re, inv_im)
+            return (left_re, left_im, right_re, right_im, neg_re, neg_im)
 
         carry = lax.fori_loop(0, slab_total, chain_step, (zero_block,) * 6)
-        outputs.append(jnp.stack([-carry[4], -carry[5]]))
+        outputs.append(jnp.stack([carry[4], carry[5]]))
     return jnp.stack(outputs)[None]
 
 

time: 330 us -> 317 us (0.961)
  other arithmetic: 20.2 us -> 16 us
    neg x12 -> x4, other arithmetic: 11.7 us -> 7.77 us  [neg_invert_pair(): -block_im]
    pallas_call x4, Pallas kernels: 201 us -> 198 us  [neg_invert_pair(): pl.pallas_call(sweep_kernel, out_shape=(jax.ShapeDtypeStruct((n, n), jnp....]
  transfers between devices with their start and end apart: 5 -> 5, of which waited for: 5 -> 5; matrix products, arithmetic and copies ran while one was open for 2% -> 3% of each run, Pallas kernels for 0% -> 0%
where the time goes in v8:
time: 317 us
  Pallas kernels  198 us (62%)
  waiting for transfers between devices  60.9 us (19%)
  between operations  21.7 us (7%)
  other arithmetic  16 us (5%)
  matrix products  8.47 us (3%)
  local copies, waits for them, and re-layouts  8.03 us (3%)
  starting transfers between devices  3.33 us (1%)
    pallas_call x4, Pallas kernels, neg_invert_pair(): pl.pallas_call(sweep_kernel, out_shape=(jax.ShapeDtypeStruct((n, n), jnp....  198 us
    all_gather x1, waiting for transfers between devices, body(): gathered = lax.all_gather(green_prev, 'energy', axis=0, tiled=True)  38.8 us
    ppermute x3, waiting for transfers between devices, gathered_over_dom(): pieces.append(lax.ppermute(array, 'dom', pairs))  15.8 us
    neg x4, other arithmetic, neg_invert_pair(): -block_im  7.77 us
  transfers between devices with their start and end apart: 5, of which 5 were waited for; matrix products, arithmetic and copies ran while one was open for 3% of the time, Pallas kernels for 0%

profile of v8, /device:TPU:0, one launch (start us, length us, event | category | flops | bytes accessed | tf_op | source)
XLA Modules:
  0.0 316.7 jit_solution(15480187846420145314)
XLA Ops:
  7.3 1.2 dynamic_slice.48
  10.5 1.4 constant_dynamic-slice_fusion.3
  14.4 1.3 compare_reduce_fusion.1
  17.0 1.3 compare_reduce_fusion
  19.5 1.2 dynamic_slice.49
  22.7 38.8 %all-gather.3.cloned.1.call-done = bf16[8,1,2,256,256]{4,3,2,1,0:T(8,128)(2,1)} async-done(((bf16[1,1,2,256,256]{4,3,2,1,0:T(8,128)(2,1)}), bf16[8,1,2,256,256]{4,3,2,1,0:T(8,128)(2,1)}) %all-gather.3.cloned.1.call-update) | async-done | bytes 2097168 | tf_op jit(solution)/shard_map/all_gather | solution.py:122
  61.5 1.1 constant_dynamic-slice_fusion.2
  65.1 0.8 pad_maximum_fusion
  66.0 1.5 collective-permute-start.1
  67.5 1.7 collective-permute-start.2
  69.3 6.8 %collective-permute-done.1 = f32[1,256,256]{2,1,0:T(8,128)S(1)} collective-permute-done((f32[1,256,256]{2,1,0:T(8,128)S(1)}, f32[1,256,256]{2,1,0:T(8,128)S(1)}, u32[]{:S(2)}, u32[]{:S(2)}) %collective-permute-start.1) | collective-permute-done | bytes 262176 | tf_op jit(solution)/shard_map/ppermute | solution.py:100
  76.2 1.9 collective-permute-done
  78.0 7.1 %collective-permute-done.2 = f32[1,256,256]{2,1,0:T(8,128)S(1)} collective-permute-done((f32[1,256,256]{2,1,0:T(8,128)S(1)}, f32[1,256,256]{2,1,0:T(8,128)S(1)}, u32[]{:S(2)}, u32[]{:S(2)}) %collective-permute-start.2) | collective-permute-done | bytes 262176 | tf_op jit(solution)/shard_map/ppermute | solution.py:100
  85.8 5.6 %all-gather.5.cloned.1.call-done = f32[2,4,256,256]{3,2,1,0:T(8,128)} async-done(((f32[2,1,256,256]{3,2,1,0:T(8,128)}), f32[2,4,256,256]{3,2,1,0:T(8,128)}) %all-gather.5.cloned.1.call-update) | async-done | bytes 2097168 | tf_op jit(solution)/shard_map/all_gather | solution.py:140
  91.4 216.6 %while.27 = (s32[]{:T(128)}, f32[256,256]{1,0:T(8,128)S(1)}, f32[256,256]{1,0:T(8,128)S(1)}, f32[256,256]{1,0:T(8,128)S(1)}, f32[256,256]{1,0:T(8,128)S(1)}, /*i...) while((s32[]{:T(128)}, f32[256,256]{1,0:T(8,128)S(1)}, ...), condition=%wide.region_3.4_spmd.clone.clone, body=%wide.region_2.3_spmd.clone.sunk.clone | while | flops 807075840 | bytes 13369702 | solution.py:173
  91.6 1.9 fusion.66
  93.5 49.4 %eval_jaxpr.8 = (f32[256,256]{1,0:T(8,128)S(1)}, f32[256,256]{1,0:T(8,128)S(1)}) custom-call(f32[256,256]{1,0:T(8,128)} %get-tuple-element.417.ar_ref, f32[256,256]{1,0:T(8,128)} %get-tuple-element.418.ai_ref), custom_call_target="tpu_custom_call" | custom-call | tf_op jit(solution)/shard_map/while/body/eval_jaxpr/pallas_call | solution.py:65
  145.7 1.9 fusion.66
  147.7 49.4 %eval_jaxpr.8 = (f32[256,256]{1,0:T(8,128)S(1)}, f32[256,256]{1,0:T(8,128)S(1)}) custom-call(f32[256,256]{1,0:T(8,128)} %get-tuple-element.417.ar_ref, f32[256,256]{1,0:T(8,128)} %get-tuple-element.418.ai_ref), custom_call_target="tpu_custom_call" | custom-call | tf_op jit(solution)/shard_map/while/body/eval_jaxpr/pallas_call | solution.py:65
  199.9 1.9 fusion.66
  201.8 49.4 %eval_jaxpr.8 = (f32[256,256]{1,0:T(8,128)S(1)}, f32[256,256]{1,0:T(8,128)S(1)}) custom-call(f32[256,256]{1,0:T(8,128)} %get-tuple-element.417.ar_ref, f32[256,256]{1,0:T(8,128)} %get-tuple-element.418.ai_ref), custom_call_target="tpu_custom_call" | custom-call | tf_op jit(solution)/shard_map/while/body/eval_jaxpr/pallas_call | solution.py:65
  254.1 1.9 fusion.66
  256.0 49.4 %eval_jaxpr.8 = (f32[256,256]{1,0:T(8,128)S(1)}, f32[256,256]{1,0:T(8,128)S(1)}) custom-call(f32[256,256]{1,0:T(8,128)} %get-tuple-element.417.ar_ref, f32[256,256]{1,0:T(8,128)} %get-tuple-element.418.ai_ref), custom_call_target="tpu_custom_call" | custom-call | tf_op jit(solution)/shard_map/while/body/eval_jaxpr/pallas_call | solution.py:65
  308.0 1.9 maximum_bitcast_fusion.1
  (85 shorter events, 15.3 us)
Async XLA Ops:
  6.5 55.0 %all-gather.3.cloned.1.call-start = ((), (), s32[]{:S(2)}) async-start(), calls=%async_computation | async-start | bytes 2359296 | tf_op jit(solution)/shard_map/all_gather | solution.py:122
  7.3 84.1 %all-gather.5.cloned.1.call-start = ((), (), s32[]{:S(2)}) async-start(), calls=%async_computation.1 | async-start | bytes 2621440 | tf_op jit(solution)/shard_map/all_gather | solution.py:140
  62.7 1.0 copy-start.2
  62.7 0.9 copy-start.4
  62.9 1.6 copy-start.3
  66.0 10.2 %collective-permute-start.1 = (f32[1,256,256]{2,1,0:T(8,128)S(1)}, f32[1,256,256]{2,1,0:T(8,128)S(1)}, u32[]{:S(2)}, u32[]{:S(2)}) collective-permute-start(f32[1,256,256]{2,1,0:T(8,128)S(1)} %copy-done.3), channel_id=1, source_target_pairs={{0,2},{1,3},{2,0},{3,1},{4,6},{5,7},{6,4},{7,5},{8,10},{9,11},{10,... | collective-permute-start | bytes 786440 | tf_op jit(solution)/shard_map/ppermute | solution.py:100
  67.5 10.5 %collective-permute-start = (f32[1,256,256]{2,1,0:T(8,128)S(1)}, f32[1,256,256]{2,1,0:T(8,128)S(1)}, u32[]{:S(2)}, u32[]{:S(2)}) collective-permute-start(f32[1,256,256]{2,1,0:T(8,128)S(1)} %copy-done.3), channel_id=1, source_target_pairs={{0,1},{1,2},{2,3},{3,0},{4,5},{5,6},{6,7},{7,4},{8,9},{9,10},{10,1... | collective-permute-start | bytes 786440 | tf_op jit(solution)/shard_map/ppermute | solution.py:100
  67.5 17.6 %collective-permute-start.2 = (f32[1,256,256]{2,1,0:T(8,128)S(1)}, f32[1,256,256]{2,1,0:T(8,128)S(1)}, u32[]{:S(2)}, u32[]{:S(2)}) collective-permute-start(f32[1,256,256]{2,1,0:T(8,128)S(1)} %copy-done.3), channel_id=1, source_target_pairs={{0,3},{1,0},{2,1},{3,2},{4,7},{5,4},{6,5},{7,6},{8,11},{9,8},{10,9... | collective-permute-start | bytes 786440 | tf_op jit(solution)/shard_map/ppermute | solution.py:100
  142.9 1.2 copy-start.1
  142.9 2.3 copy-start
  197.1 1.1 copy-start.1
  197.1 2.3 copy-start
  251.2 1.1 copy-start.1
  251.3 2.3 copy-start
  305.4 1.1 copy-start.1
  305.4 2.3 copy-start
Sparse Core Ops, SparseCore 0:
  9.5 51.9 all-gather.2
  66.1 25.2 all-gather.4

commit v9 on v8

--- a/solution.py
+++ b/solution.py
@@ -92,17 +92,6 @@
     return (block_re, block_im)
 
 
-def gathered_over_dom(array):
-    peers = lax.axis_size("dom")
-    pieces = [array]
-    for shift in range(1, peers):
-        pairs = [(i, (i + shift) % peers) for i in range(peers)]
-        pieces.append(lax.ppermute(array, "dom", pairs))
-    order = (lax.axis_index("dom") - jnp.arange(peers)) % peers
-    stacked = jnp.stack(pieces)[order]
-    return stacked.reshape((peers * array.shape[0],) + array.shape[1:])
-
-
 def partner_levels(energy_level, phonon_offsets, level_count):
     lower_level = energy_level - phonon_offsets[0, energy_level]
     upper_level = energy_level + phonon_offsets[1, energy_level]
@@ -118,7 +107,8 @@
     dom_count = lax.axis_size("dom")
     dom_index = lax.axis_index("dom")
     slab_total = local_slabs * dom_count
-    all_link = gathered_over_dom(coupling)
+    all_link = lax.all_gather(coupling, "dom", axis=0, tiled=True)
+    all_link, green_prev = lax.optimization_barrier((all_link, green_prev))
     gathered = lax.all_gather(green_prev, "energy", axis=0, tiled=True)
     own_slot = lax.axis_index("energy")
     energy_level = slot_energy[own_slot]

time: 317 us -> 339 us (1.069)
  waiting for transfers between devices: 60.9 us -> 79.3 us
  other arithmetic: 16 us -> 19.7 us
    all_gather x0 -> x1, waiting for transfers between devices: none -> 21.1 us  [body(): all_link = lax.all_gather(coupling, 'dom', axis=0, tiled=True)]
    ppermute x3 -> x0, waiting for transfers between devices: 15.8 us -> none  [gathered_over_dom(): pieces.append(lax.ppermute(array, 'dom', pairs))]
    all_gather x1, waiting for transfers between devices: 5.57 us -> 21.2 us  [body(): lax.all_gather(jnp.stack([block_re, block_im]), 'dom', axis=1, tiled=True)]
    select_n x4, other arithmetic: 0.14 us -> 3.96 us  [chain_step(): link_block = jnp.where(is_left, link_block, link_block.T)]
    dynamic_slice x8, local copies, waits for them, and re-layouts: 0.6 us -> 4.4 us  [chain_step(): link_block = all_link[link_index]]
  transfers between devices with their start and end apart: 5 -> 3, of which waited for: 5 -> 3; matrix products, arithmetic and copies ran while one was open for 3% -> 2% of each run, Pallas kernels for 0% -> 0%
where the time goes in v9:
time: 339 us; the launch traced here: 338 us
  Pallas kernels  198 us (58%)
  waiting for transfers between devices  79.3 us (23%)
  between operations  21.2 us (6%)
  other arithmetic  19.7 us (6%)
  local copies, waits for them, and re-layouts  11.2 us (3%)
  matrix products  8.47 us (2%)
    pallas_call x4, Pallas kernels, neg_invert_pair(): pl.pallas_call(sweep_kernel, out_shape=(jax.ShapeDtypeStruct((n, n), jnp....  198 us
    all_gather x1, waiting for transfers between devices, body(): gathered = lax.all_gather(green_prev, 'energy', axis=0, tiled=True)  36.3 us
    all_gather x1, waiting for transfers between devices, body(): lax.all_gather(jnp.stack([block_re, block_im]), 'dom', axis=1, tiled=True)  21.2 us
    all_gather x1, waiting for transfers between devices, body(): all_link = lax.all_gather(coupling, 'dom', axis=0, tiled=True)  21.1 us
    neg x4, other arithmetic, neg_invert_pair(): -block_im  7.77 us
  transfers between devices with their start and end apart: 3, of which 3 were waited for; matrix products, arithmetic and copies ran while one was open for 2% of the time, Pallas kernels for 0%

profile of v9, /device:TPU:0, one launch (start us, length us, event | category | flops | bytes accessed | tf_op | source)
XLA Modules:
  0.0 338.1 jit_solution(14241774730794040778)
XLA Ops:
  7.3 21.1 %all-gather.4.cloned.1.call-done = f32[4,256,256]{2,1,0:T(8,128)} async-done(((f32[1,256,256]{2,1,0:T(8,128)}), f32[4,256,256]{2,1,0:T(8,128)}) %all-gather.4.cloned.1.call-update) | async-done | bytes 1048592 | tf_op jit(solution)/shard_map/all_gather | solution.py:110
  28.5 1.2 dynamic_slice.48
  31.6 1.4 constant_dynamic-slice_fusion.3
  35.5 1.3 compare_reduce_fusion.1
  37.9 1.3 compare_reduce_fusion
  40.4 1.2 dynamic_slice.49
  43.5 36.3 %all-gather.6.cloned.1.call-done = bf16[8,1,2,256,256]{4,3,2,1,0:T(8,128)(2,1)} async-done(((bf16[1,1,2,256,256]{4,3,2,1,0:T(8,128)(2,1)}), bf16[8,1,2,256,256]{4,3,2,1,0:T(8,128)(2,1)}) %all-gather.6.cloned.1.call-update) | async-done | bytes 2097168 | tf_op jit(solution)/shard_map/all_gather | solution.py:112
  79.8 1.1 constant_dynamic-slice_fusion.2
  84.4 21.2 %all-gather.8.cloned.1.call-done = f32[2,4,256,256]{3,2,1,0:T(8,128)} async-done(((f32[2,1,256,256]{3,2,1,0:T(8,128)}), f32[2,4,256,256]{3,2,1,0:T(8,128)}) %all-gather.8.cloned.1.call-update) | async-done | bytes 2097168 | tf_op jit(solution)/shard_map/all_gather | solution.py:130
  105.5 224.1 %while.27 = (s32[]{:T(128)}, f32[256,256]{1,0:T(8,128)S(1)}, f32[256,256]{1,0:T(8,128)S(1)}, f32[256,256]{1,0:T(8,128)S(1)}, f32[256,256]{1,0:T(8,128)S(1)}, /*i...) while((s32[]{:T(128)}, f32[256,256]{1,0:T(8,128)S(1)}, ...), condition=%wide.region_3.4_spmd.clone.clone, body=%wide.region_2.3_spmd.clone.sunk.clone | while | flops 807075840 | bytes 13369702 | solution.py:163
  106.7 1.0 bitcast_select_fusion.3
  107.6 1.9 fusion.64
  109.6 49.4 %eval_jaxpr.8 = (f32[256,256]{1,0:T(8,128)S(1)}, f32[256,256]{1,0:T(8,128)S(1)}) custom-call(f32[256,256]{1,0:T(8,128)} %get-tuple-element.411.ar_ref, f32[256,256]{1,0:T(8,128)} %get-tuple-element.412.ai_ref), custom_call_target="tpu_custom_call" | custom-call | tf_op jit(solution)/shard_map/while/body/eval_jaxpr/pallas_call | solution.py:65
  161.6 1.0 constant_dynamic-slice_fusion.7
  162.7 1.0 bitcast_select_fusion.3
  163.7 1.9 fusion.64
  165.6 49.4 %eval_jaxpr.8 = (f32[256,256]{1,0:T(8,128)S(1)}, f32[256,256]{1,0:T(8,128)S(1)}) custom-call(f32[256,256]{1,0:T(8,128)} %get-tuple-element.411.ar_ref, f32[256,256]{1,0:T(8,128)} %get-tuple-element.412.ai_ref), custom_call_target="tpu_custom_call" | custom-call | tf_op jit(solution)/shard_map/while/body/eval_jaxpr/pallas_call | solution.py:65
  218.8 1.0 bitcast_select_fusion.3
  219.7 1.9 fusion.64
  221.7 49.4 %eval_jaxpr.8 = (f32[256,256]{1,0:T(8,128)S(1)}, f32[256,256]{1,0:T(8,128)S(1)}) custom-call(f32[256,256]{1,0:T(8,128)} %get-tuple-element.411.ar_ref, f32[256,256]{1,0:T(8,128)} %get-tuple-element.412.ai_ref), custom_call_target="tpu_custom_call" | custom-call | tf_op jit(solution)/shard_map/while/body/eval_jaxpr/pallas_call | solution.py:65
  274.8 1.0 bitcast_select_fusion.3
  275.8 1.9 fusion.64
  277.7 49.4 %eval_jaxpr.8 = (f32[256,256]{1,0:T(8,128)S(1)}, f32[256,256]{1,0:T(8,128)S(1)}) custom-call(f32[256,256]{1,0:T(8,128)} %get-tuple-element.411.ar_ref, f32[256,256]{1,0:T(8,128)} %get-tuple-element.412.ai_ref), custom_call_target="tpu_custom_call" | custom-call | tf_op jit(solution)/shard_map/while/body/eval_jaxpr/pallas_call | solution.py:65
  329.7 1.9 maximum_bitcast_fusion
  (78 shorter events, 18.1 us)
Async XLA Ops:
  6.5 21.8 %all-gather.4.cloned.1.call-start = ((), (), s32[]{:S(2)}) async-start(), calls=%async_computation | async-start | bytes 1310720 | tf_op jit(solution)/shard_map/all_gather | solution.py:110
  7.3 72.6 %all-gather.6.cloned.1.call-start = ((), (), s32[]{:S(2)}) async-start(), calls=%async_computation.1 | async-start | bytes 2359296 | tf_op jit(solution)/shard_map/all_gather | solution.py:112
  28.4 77.1 %all-gather.8.cloned.1.call-start = ((), (), s32[]{:S(2)}) async-start(), calls=%async_computation.2 | async-start | bytes 2621440 | tf_op jit(solution)/shard_map/all_gather | solution.py:130
  81.0 1.0 copy-start.2
  81.0 0.9 copy-start.4
  81.3 1.4 copy-start.3
  159.0 2.3 copy-start
  159.0 2.3 copy-start.1
  215.0 2.3 copy-start
  215.1 2.3 copy-start.1
  271.1 2.3 copy-start
  271.1 2.3 copy-start.1
  327.1 2.3 copy-start
  327.2 2.3 copy-start.1
Sparse Core Ops, SparseCore 0:
  8.9 19.4 all-gather.3
  30.5 49.2 all-gather.5
  84.4 21.0 all-gather.7

commit v10 on v8

--- a/solution.py
+++ b/solution.py
@@ -118,7 +118,6 @@
     dom_count = lax.axis_size("dom")
     dom_index = lax.axis_index("dom")
     slab_total = local_slabs * dom_count
-    all_link = gathered_over_dom(coupling)
     gathered = lax.all_gather(green_prev, "energy", axis=0, tiled=True)
     own_slot = lax.axis_index("energy")
     energy_level = slot_energy[own_slot]
@@ -137,7 +136,8 @@
     block_re, block_im = slab_blocks(
         hamiltonian, coupling, deform, fetched, energy, first_mask, last_mask
     )
-    blocks = lax.all_gather(jnp.stack([block_re, block_im]), "dom", axis=1, tiled=True)
+    blocks = gathered_over_dom(jnp.stack([block_re, block_im, coupling], axis=1))
+    all_link = blocks[:, 2]
     zero_block = jnp.zeros((orbitals, orbitals), jnp.float32)
 
     outputs = []
@@ -151,8 +151,8 @@
             slab = jnp.where(is_left, step, slab_total - 1 - step + own)
             use_left = jnp.logical_or(is_left, is_final)
             use_right = jnp.logical_not(is_left)
-            in_re = blocks[0, slab] + jnp.where(use_left, left_re, 0.0) + jnp.where(use_right, right_re, 0.0)
-            in_im = blocks[1, slab] + jnp.where(use_left, left_im, 0.0) + jnp.where(use_right, right_im, 0.0)
+            in_re = blocks[slab, 0] + jnp.where(use_left, left_re, 0.0) + jnp.where(use_right, right_re, 0.0)
+            in_im = blocks[slab, 1] + jnp.where(use_left, left_im, 0.0) + jnp.where(use_right, right_im, 0.0)
             neg_re, neg_im = neg_invert_pair(in_re, in_im)
             link_index = jnp.where(is_left, step, jnp.maximum(slab - 1, 0))
             link_block = all_link[link_index]

time: 317 us -> 337 us (1.063)
  waiting for transfers between devices: 60.9 us -> 72.6 us
  local copies, waits for them, and re-layouts: 8.03 us -> 12.7 us
    ppermute x3, waiting for transfers between devices: 15.8 us -> 33 us  [gathered_over_dom(): pieces.append(lax.ppermute(array, 'dom', pairs))]
    all_gather x1 -> x0, waiting for transfers between devices: 5.57 us -> none  [body(): lax.all_gather(jnp.stack([block_re, block_im]), 'dom', axis=1, tiled=True)]
    another operation x1 -> x2, other arithmetic: 0.08 us -> 4.22 us  [gathered_over_dom(): stacked = jnp.stack(pieces)[order]]
    gather x1, local copies, waits for them, and re-layouts: 0.62 us -> 4.3 us  [gathered_over_dom(): stacked = jnp.stack(pieces)[order]]
  transfers between devices with their start and end apart: 5 -> 4, of which waited for: 5 -> 4; matrix products, arithmetic and copies ran while one was open for 3% -> 2% of each run, Pallas kernels for 0% -> 0%
where the time goes in v10:
time: 337 us; the launch traced here: 336 us
  Pallas kernels  198 us (59%)
  waiting for transfers between devices  72.6 us (22%)
  between operations  21.7 us (6%)
  other arithmetic  19.3 us (6%)
  local copies, waits for them, and re-layouts  12.7 us (4%)
  matrix products  8.47 us (3%)
    pallas_call x4, Pallas kernels, neg_invert_pair(): pl.pallas_call(sweep_kernel, out_shape=(jax.ShapeDtypeStruct((n, n), jnp....  198 us
    all_gather x1, waiting for transfers between devices, body(): gathered = lax.all_gather(green_prev, 'energy', axis=0, tiled=True)  38.9 us
    ppermute x3, waiting for transfers between devices, gathered_over_dom(): pieces.append(lax.ppermute(array, 'dom', pairs))  33 us
    neg x4, other arithmetic, neg_invert_pair(): -block_im  7.76 us
  transfers between devices with their start and end apart: 4, of which 4 were waited for; matrix products, arithmetic and copies ran while one was open for 2% of the time, Pallas kernels for 0%

profile of v10, /device:TPU:0, one launch (start us, length us, event | category | flops | bytes accessed | tf_op | source)
XLA Modules:
  0.0 336.0 jit_solution(7101115815947261795)
XLA Ops:
  7.3 1.2 dynamic_slice.48
  10.5 1.4 constant_dynamic-slice_fusion.3
  13.1 1.3 compare_reduce_fusion.1
  16.9 1.3 compare_reduce_fusion
  19.5 1.2 dynamic_slice.49
  22.7 38.9 %all-gather.2.cloned.1.call-done = bf16[8,1,2,256,256]{4,3,2,1,0:T(8,128)(2,1)} async-done(((bf16[1,1,2,256,256]{4,3,2,1,0:T(8,128)(2,1)}), bf16[8,1,2,256,256]{4,3,2,1,0:T(8,128)(2,1)}) %all-gather.2.cloned.1.call-update) | async-done | bytes 2097168 | tf_op jit(solution)/shard_map/all_gather | solution.py:121
  65.9 1.5 collective-permute-start.1
  67.4 1.4 collective-permute-start.2
  68.8 16.5 %collective-permute-done = f32[1,3,256,256]{3,2,1,0:T(8,128)S(1)} collective-permute-done((f32[1,3,256,256]{3,2,1,0:T(8,128)}, f32[1,3,256,256]{3,2,1,0:T(8,128)S(1)}, u32[]{:S(2)}, u32[]{:S(2)}) %collective-permute-start) | collective-permute-done | bytes 786464 | tf_op jit(solution)/shard_map/ppermute | solution.py:100
  85.4 1.1 collective-permute-done.1
  86.5 15.4 %collective-permute-done.2 = f32[1,3,256,256]{3,2,1,0:T(8,128)} collective-permute-done((f32[1,3,256,256]{3,2,1,0:T(8,128)}, f32[1,3,256,256]{3,2,1,0:T(8,128)}, u32[]{:S(2)}, u32[]{:S(2)}) %collective-permute-start.2) | collective-permute-done | bytes 786464 | tf_op jit(solution)/shard_map/ppermute | solution.py:100
  101.9 3.2 maximum_bitcast_fusion
  105.0 4.3 %gather_fusion = f32[4,3,256,256]{3,2,1,0:T(8,128)} fusion(f32[4,3,256,256]{3,2,1,0:T(8,128)} %maximum_bitcast_fusion, s32[1024]{0:T(1024)S(1)} %pad_clamp_fusion), kind=kCustom, calls=%fused_computation | custom fusion | bytes 6291472 | tf_op jit(solution)/shard_map/gather | solution.py:102
  109.3 1.3 slice_bitcast_fusion
  110.6 216.7 %while.27 = (s32[]{:T(128)}, f32[256,256]{1,0:T(8,128)S(1)}, f32[256,256]{1,0:T(8,128)S(1)}, f32[256,256]{1,0:T(8,128)S(1)}, f32[256,256]{1,0:T(8,128)S(1)}, /*i...) while((s32[]{:T(128)}, f32[256,256]{1,0:T(8,128)S(1)}, ...), condition=%wide.region_3.4_spmd.clone.clone, body=%wide.region_2.3_spmd.clone.sunk.clone | while | flops 807075840 | bytes 13369694 | solution.py:173
  110.7 1.9 fusion.67
  112.6 49.4 %eval_jaxpr.8 = (f32[256,256]{1,0:T(8,128)S(1)}, f32[256,256]{1,0:T(8,128)S(1)}) custom-call(f32[256,256]{1,0:T(8,128)} %get-tuple-element.419.ar_ref, f32[256,256]{1,0:T(8,128)} %get-tuple-element.420.ai_ref), custom_call_target="tpu_custom_call" | custom-call | tf_op jit(solution)/shard_map/while/body/eval_jaxpr/pallas_call | solution.py:65
  164.8 1.9 fusion.67
  166.8 49.4 %eval_jaxpr.8 = (f32[256,256]{1,0:T(8,128)S(1)}, f32[256,256]{1,0:T(8,128)S(1)}) custom-call(f32[256,256]{1,0:T(8,128)} %get-tuple-element.419.ar_ref, f32[256,256]{1,0:T(8,128)} %get-tuple-element.420.ai_ref), custom_call_target="tpu_custom_call" | custom-call | tf_op jit(solution)/shard_map/while/body/eval_jaxpr/pallas_call | solution.py:65
  219.0 1.9 fusion.67
  221.0 49.4 %eval_jaxpr.8 = (f32[256,256]{1,0:T(8,128)S(1)}, f32[256,256]{1,0:T(8,128)S(1)}) custom-call(f32[256,256]{1,0:T(8,128)} %get-tuple-element.419.ar_ref, f32[256,256]{1,0:T(8,128)} %get-tuple-element.420.ai_ref), custom_call_target="tpu_custom_call" | custom-call | tf_op jit(solution)/shard_map/while/body/eval_jaxpr/pallas_call | solution.py:65
  273.2 1.9 fusion.67
  275.1 49.4 %eval_jaxpr.8 = (f32[256,256]{1,0:T(8,128)S(1)}, f32[256,256]{1,0:T(8,128)S(1)}) custom-call(f32[256,256]{1,0:T(8,128)} %get-tuple-element.419.ar_ref, f32[256,256]{1,0:T(8,128)} %get-tuple-element.420.ai_ref), custom_call_target="tpu_custom_call" | custom-call | tf_op jit(solution)/shard_map/while/body/eval_jaxpr/pallas_call | solution.py:65
  327.3 1.9 maximum_bitcast_fusion.1
  (83 shorter events, 16.3 us)
Async XLA Ops:
  6.5 56.8 %copy-start.4 = (f32[1,256]{1,0:T(1,128)S(1)}, f32[1,256]{1,0:T(1,128)}, u32[]{:S(2)}) copy-start(f32[1,256]{1,0:T(1,128)} %param.11) | copy-start | bytes 3076
  6.5 56.8 %copy-start.3 = (f32[1,256,256]{2,1,0:T(8,128)S(1)}, f32[1,256,256]{2,1,0:T(8,128)}, u32[]{:S(2)}) copy-start(f32[1,256,256]{2,1,0:T(8,128)} %param.9) | copy-start | bytes 786436
  6.5 55.0 %all-gather.2.cloned.1.call-start = ((), (), s32[]{:S(2)}) async-start(), calls=%async_computation | async-start | bytes 2359296 | tf_op jit(solution)/shard_map/all_gather | solution.py:121
  22.7 41.5 %copy-start.2 = (f32[1,256,256]{2,1,0:T(8,128)S(1)}, f32[1,256,256]{2,1,0:T(8,128)}, u32[]{:S(2)}) copy-start(f32[1,256,256]{2,1,0:T(8,128)} %param.10) | copy-start | bytes 786436
  65.9 19.5 %collective-permute-start = (f32[1,3,256,256]{3,2,1,0:T(8,128)}, f32[1,3,256,256]{3,2,1,0:T(8,128)S(1)}, u32[]{:S(2)}, u32[]{:S(2)}) collective-permute-start(f32[1,3,256,256]{3,2,1,0:T(8,128)} %get-tuple-element.334), channel_id=1, source_target_pairs={{0,1},{1,2},{2,3},{3,0},{4,5},{5,6},{6,7},{7,4},{8,9},{9,10},{10,1... | collective-permute-start | bytes 2359304 | tf_op jit(solution)/shard_map/ppermute | solution.py:100
  65.9 20.6 %collective-permute-start.1 = (f32[1,3,256,256]{3,2,1,0:T(8,128)}, f32[1,3,256,256]{3,2,1,0:T(8,128)S(1)}, u32[]{:S(2)}, u32[]{:S(2)}) collective-permute-start(f32[1,3,256,256]{3,2,1,0:T(8,128)} %get-tuple-element.334), channel_id=1, source_target_pairs={{0,2},{1,3},{2,0},{3,1},{4,6},{5,7},{6,4},{7,5},{8,10},{9,11},{10,... | collective-permute-start | bytes 2359304 | tf_op jit(solution)/shard_map/ppermute | solution.py:100
  67.4 34.5 %collective-permute-start.2 = (f32[1,3,256,256]{3,2,1,0:T(8,128)}, f32[1,3,256,256]{3,2,1,0:T(8,128)}, u32[]{:S(2)}, u32[]{:S(2)}) collective-permute-start(f32[1,3,256,256]{3,2,1,0:T(8,128)} %get-tuple-element.334), channel_id=1, source_target_pairs={{0,3},{1,0},{2,1},{3,2},{4,7},{5,4},{6,5},{7,6},{8,11},{9,8},{10,9... | collective-permute-start | bytes 2359304 | tf_op jit(solution)/shard_map/ppermute | solution.py:100
  162.0 1.4 copy-start.1
  162.0 2.8 copy-start
  216.2 1.4 copy-start.1
  216.2 2.8 copy-start
  270.4 1.4 copy-start.1
  270.4 2.8 copy-start
  324.5 1.4 copy-start.1
  324.5 2.8 copy-start
Sparse Core Ops, SparseCore 0:
  9.5 52.0 all-gather.1

commit v11 on v8

--- a/solution.py
+++ b/solution.py
@@ -39,8 +39,9 @@
         row_im = oi_ref[pl.ds(k, 1), :]
         d_re = jnp.sum(jnp.where(at_k, row_re, 0.0), axis=1, keepdims=True)
         d_im = jnp.sum(jnp.where(at_k, row_im, 0.0), axis=1, keepdims=True)
-        tile_re = jnp.where(k < half, a_re[:, :half], a_re[:, half:])
-        tile_im = jnp.where(k < half, a_im[:, :half], a_im[:, half:])
+        lane_base = pl.multiple_of((k // half) * half, half)
+        tile_re = or_ref[:, pl.ds(lane_base, half)]
+        tile_im = oi_ref[:, pl.ds(lane_base, half)]
         col_re = jnp.sum(jnp.where(half_cols == kh, tile_re, 0.0), axis=1, keepdims=True)
         col_im = jnp.sum(jnp.where(half_cols == kh, tile_im, 0.0), axis=1, keepdims=True)
         norm = d_re * d_re + d_im * d_im

time: 317 us -> 313 us (0.987)
  Pallas kernels: 198 us -> 193 us
    pallas_call x4, Pallas kernels: 198 us -> 193 us  [neg_invert_pair(): pl.pallas_call(sweep_kernel, out_shape=(jax.ShapeDtypeStruct((n, n), jnp....]
where the time goes in v11:
time: 313 us
  Pallas kernels  193 us (62%)
  waiting for transfers between devices  60.9 us (19%)
  between operations  21.7 us (7%)
  other arithmetic  16 us (5%)
  matrix products  8.48 us (3%)
  local copies, waits for them, and re-layouts  8.03 us (3%)
  starting transfers between devices  3.33 us (1%)
    pallas_call x4, Pallas kernels, neg_invert_pair(): pl.pallas_call(sweep_kernel, out_shape=(jax.ShapeDtypeStruct((n, n), jnp....  193 us
    all_gather x1, waiting for transfers between devices, body(): gathered = lax.all_gather(green_prev, 'energy', axis=0, tiled=True)  38.8 us
    ppermute x3, waiting for transfers between devices, gathered_over_dom(): pieces.append(lax.ppermute(array, 'dom', pairs))  15.8 us
    neg x4, other arithmetic, neg_invert_pair(): -block_im  7.77 us
  transfers between devices with their start and end apart: 5, of which 5 were waited for; matrix products, arithmetic and copies ran while one was open for 3% of the time, Pallas kernels for 0%

profile of v11, /device:TPU:0, one launch (start us, length us, event | category | flops | bytes accessed | tf_op | source)
XLA Modules:
  0.0 312.5 jit_solution(11584271828725917185)
XLA Ops:
  7.3 1.2 dynamic_slice.48
  10.5 1.4 constant_dynamic-slice_fusion.3
  14.4 1.3 compare_reduce_fusion.1
  17.0 1.3 compare_reduce_fusion
  19.5 1.2 dynamic_slice.49
  22.7 38.8 %all-gather.3.cloned.1.call-done = bf16[8,1,2,256,256]{4,3,2,1,0:T(8,128)(2,1)} async-done(((bf16[1,1,2,256,256]{4,3,2,1,0:T(8,128)(2,1)}), bf16[8,1,2,256,256]{4,3,2,1,0:T(8,128)(2,1)}) %all-gather.3.cloned.1.call-update) | async-done | bytes 2097168 | tf_op jit(solution)/shard_map/all_gather | solution.py:123
  61.5 1.1 constant_dynamic-slice_fusion.2
  65.1 0.8 pad_maximum_fusion
  66.0 1.5 collective-permute-start.1
  67.5 1.7 collective-permute-start.2
  69.3 6.8 %collective-permute-done.1 = f32[1,256,256]{2,1,0:T(8,128)S(1)} collective-permute-done((f32[1,256,256]{2,1,0:T(8,128)S(1)}, f32[1,256,256]{2,1,0:T(8,128)S(1)}, u32[]{:S(2)}, u32[]{:S(2)}) %collective-permute-start.1) | collective-permute-done | bytes 262176 | tf_op jit(solution)/shard_map/ppermute | solution.py:101
  76.2 1.9 collective-permute-done
  78.0 7.1 %collective-permute-done.2 = f32[1,256,256]{2,1,0:T(8,128)S(1)} collective-permute-done((f32[1,256,256]{2,1,0:T(8,128)S(1)}, f32[1,256,256]{2,1,0:T(8,128)S(1)}, u32[]{:S(2)}, u32[]{:S(2)}) %collective-permute-start.2) | collective-permute-done | bytes 262176 | tf_op jit(solution)/shard_map/ppermute | solution.py:101
  85.8 5.6 %all-gather.5.cloned.1.call-done = f32[2,4,256,256]{3,2,1,0:T(8,128)} async-done(((f32[2,1,256,256]{3,2,1,0:T(8,128)}), f32[2,4,256,256]{3,2,1,0:T(8,128)}) %all-gather.5.cloned.1.call-update) | async-done | bytes 2097168 | tf_op jit(solution)/shard_map/all_gather | solution.py:141
  91.4 212.5 %while.27 = (s32[]{:T(128)}, f32[256,256]{1,0:T(8,128)S(1)}, f32[256,256]{1,0:T(8,128)S(1)}, f32[256,256]{1,0:T(8,128)S(1)}, f32[256,256]{1,0:T(8,128)S(1)}, /*i...) while((s32[]{:T(128)}, f32[256,256]{1,0:T(8,128)S(1)}, ...), condition=%wide.region_3.4_spmd.clone.clone, body=%wide.region_2.3_spmd.clone.sunk.clone | while | flops 807075840 | bytes 13369702 | solution.py:174
  91.6 1.9 fusion.66
  93.5 48.4 %eval_jaxpr.8 = (f32[256,256]{1,0:T(8,128)S(1)}, f32[256,256]{1,0:T(8,128)S(1)}) custom-call(f32[256,256]{1,0:T(8,128)} %get-tuple-element.417.ar_ref, f32[256,256]{1,0:T(8,128)} %get-tuple-element.418.ai_ref), custom_call_target="tpu_custom_call" | custom-call | tf_op jit(solution)/shard_map/while/body/eval_jaxpr/pallas_call | solution.py:66
  144.7 1.9 fusion.66
  146.7 48.4 %eval_jaxpr.8 = (f32[256,256]{1,0:T(8,128)S(1)}, f32[256,256]{1,0:T(8,128)S(1)}) custom-call(f32[256,256]{1,0:T(8,128)} %get-tuple-element.417.ar_ref, f32[256,256]{1,0:T(8,128)} %get-tuple-element.418.ai_ref), custom_call_target="tpu_custom_call" | custom-call | tf_op jit(solution)/shard_map/while/body/eval_jaxpr/pallas_call | solution.py:66
  197.8 1.9 fusion.66
  199.8 48.4 %eval_jaxpr.8 = (f32[256,256]{1,0:T(8,128)S(1)}, f32[256,256]{1,0:T(8,128)S(1)}) custom-call(f32[256,256]{1,0:T(8,128)} %get-tuple-element.417.ar_ref, f32[256,256]{1,0:T(8,128)} %get-tuple-element.418.ai_ref), custom_call_target="tpu_custom_call" | custom-call | tf_op jit(solution)/shard_map/while/body/eval_jaxpr/pallas_call | solution.py:66
  251.0 1.9 fusion.66
  252.9 48.4 %eval_jaxpr.8 = (f32[256,256]{1,0:T(8,128)S(1)}, f32[256,256]{1,0:T(8,128)S(1)}) custom-call(f32[256,256]{1,0:T(8,128)} %get-tuple-element.417.ar_ref, f32[256,256]{1,0:T(8,128)} %get-tuple-element.418.ai_ref), custom_call_target="tpu_custom_call" | custom-call | tf_op jit(solution)/shard_map/while/body/eval_jaxpr/pallas_call | solution.py:66
  303.8 1.9 maximum_bitcast_fusion.1
  (85 shorter events, 15.3 us)
Async XLA Ops:
  6.5 55.0 %all-gather.3.cloned.1.call-start = ((), (), s32[]{:S(2)}) async-start(), calls=%async_computation | async-start | bytes 2359296 | tf_op jit(solution)/shard_map/all_gather | solution.py:123
  7.3 84.1 %all-gather.5.cloned.1.call-start = ((), (), s32[]{:S(2)}) async-start(), calls=%async_computation.1 | async-start | bytes 2621440 | tf_op jit(solution)/shard_map/all_gather | solution.py:141
  62.7 1.0 copy-start.2
  62.7 0.9 copy-start.4
  62.9 1.6 copy-start.3
  66.0 10.2 %collective-permute-start.1 = (f32[1,256,256]{2,1,0:T(8,128)S(1)}, f32[1,256,256]{2,1,0:T(8,128)S(1)}, u32[]{:S(2)}, u32[]{:S(2)}) collective-permute-start(f32[1,256,256]{2,1,0:T(8,128)S(1)} %copy-done.3), channel_id=1, source_target_pairs={{0,2},{1,3},{2,0},{3,1},{4,6},{5,7},{6,4},{7,5},{8,10},{9,11},{10,... | collective-permute-start | bytes 786440 | tf_op jit(solution)/shard_map/ppermute | solution.py:101
  67.5 10.5 %collective-permute-start = (f32[1,256,256]{2,1,0:T(8,128)S(1)}, f32[1,256,256]{2,1,0:T(8,128)S(1)}, u32[]{:S(2)}, u32[]{:S(2)}) collective-permute-start(f32[1,256,256]{2,1,0:T(8,128)S(1)} %copy-done.3), channel_id=1, source_target_pairs={{0,1},{1,2},{2,3},{3,0},{4,5},{5,6},{6,7},{7,4},{8,9},{9,10},{10,1... | collective-permute-start | bytes 786440 | tf_op jit(solution)/shard_map/ppermute | solution.py:101
  67.5 17.6 %collective-permute-start.2 = (f32[1,256,256]{2,1,0:T(8,128)S(1)}, f32[1,256,256]{2,1,0:T(8,128)S(1)}, u32[]{:S(2)}, u32[]{:S(2)}) collective-permute-start(f32[1,256,256]{2,1,0:T(8,128)S(1)} %copy-done.3), channel_id=1, source_target_pairs={{0,3},{1,0},{2,1},{3,2},{4,7},{5,4},{6,5},{7,6},{8,11},{9,8},{10,9... | collective-permute-start | bytes 786440 | tf_op jit(solution)/shard_map/ppermute | solution.py:101
  141.9 1.2 copy-start.1
  141.9 2.3 copy-start
  195.0 1.2 copy-start.1
  195.0 2.3 copy-start
  248.2 1.2 copy-start.1
  248.2 2.3 copy-start
  301.3 1.2 copy-start.1
  301.3 2.3 copy-start
Sparse Core Ops, SparseCore 0:
  9.5 51.9 all-gather.2
  66.1 25.2 all-gather.4

commit v12 on v11

--- a/solution.py
+++ b/solution.py
@@ -146,14 +146,11 @@
         own = dom_index * local_slabs + local
 
         def chain_step(step, carry):
-            left_re, left_im, right_re, right_im, out_re, out_im = carry
+            left_re, left_im, right_re, right_im = carry
             is_left = step < own
-            is_final = step == slab_total - 1
             slab = jnp.where(is_left, step, slab_total - 1 - step + own)
-            use_left = jnp.logical_or(is_left, is_final)
-            use_right = jnp.logical_not(is_left)
-            in_re = blocks[0, slab] + jnp.where(use_left, left_re, 0.0) + jnp.where(use_right, right_re, 0.0)
-            in_im = blocks[1, slab] + jnp.where(use_left, left_im, 0.0) + jnp.where(use_right, right_im, 0.0)
+            in_re = blocks[0, slab] + jnp.where(is_left, left_re, right_re)
+            in_im = blocks[1, slab] + jnp.where(is_left, left_im, right_im)
             neg_re, neg_im = neg_invert_pair(in_re, in_im)
             link_index = jnp.where(is_left, step, jnp.maximum(slab - 1, 0))
             link_block = all_link[link_index]
@@ -166,13 +163,17 @@
             )
             left_re = jnp.where(is_left, next_re, left_re)
             left_im = jnp.where(is_left, next_im, left_im)
-            keep_right = jnp.logical_or(is_left, is_final)
-            right_re = jnp.where(keep_right, right_re, next_re)
-            right_im = jnp.where(keep_right, right_im, next_im)
-            return (left_re, left_im, right_re, right_im, neg_re, neg_im)
+            right_re = jnp.where(is_left, right_re, next_re)
+            right_im = jnp.where(is_left, right_im, next_im)
+            return (left_re, left_im, right_re, right_im)
 
-        carry = lax.fori_loop(0, slab_total, chain_step, (zero_block,) * 6)
-        outputs.append(jnp.stack([carry[4], carry[5]]))
+        left_re, left_im, right_re, right_im = lax.fori_loop(
+            0, slab_total - 1, chain_step, (zero_block,) * 4
+        )
+        neg_re, neg_im = neg_invert_pair(
+            blocks[0, own] + left_re + right_re, blocks[1, own] + left_im + right_im
+        )
+        outputs.append(jnp.stack([neg_re, neg_im]))
     return jnp.stack(outputs)[None]
 
 

time: 313 us -> 318 us (1.016)
  Pallas kernels: 193 us -> 197 us
    pallas_call x4, Pallas kernels: 193 us -> 197 us  [neg_invert_pair(): pl.pallas_call(sweep_kernel, out_shape=(jax.ShapeDtypeStruct((n, n), jnp....]
  transfers between devices with their start and end apart: 5 -> 5, of which waited for: 5 -> 5; matrix products, arithmetic and copies ran while one was open for 3% -> 2% of each run, Pallas kernels for 0% -> 0%
where the time goes in v12:
time: 318 us
  Pallas kernels  197 us (62%)
  waiting for transfers between devices  62.8 us (20%)
  between operations  21.7 us (7%)
  other arithmetic  15.8 us (5%)
  matrix products  9.37 us (3%)
  local copies, waits for them, and re-layouts  7.58 us (2%)
    pallas_call x4, Pallas kernels, neg_invert_pair(): pl.pallas_call(sweep_kernel, out_shape=(jax.ShapeDtypeStruct((n, n), jnp....  197 us
    all_gather x1, waiting for transfers between devices, body(): gathered = lax.all_gather(green_prev, 'energy', axis=0, tiled=True)  38.8 us
    ppermute x3, waiting for transfers between devices, gathered_over_dom(): pieces.append(lax.ppermute(array, 'dom', pairs))  17.7 us
    neg x4, other arithmetic, neg_invert_pair(): -block_im  7.72 us
  transfers between devices with their start and end apart: 5, of which 5 were waited for; matrix products, arithmetic and copies ran while one was open for 2% of the time, Pallas kernels for 0%

profile of v12, /device:TPU:0, one launch (start us, length us, event | category | flops | bytes accessed | tf_op | source)
XLA Modules:
  0.0 317.9 jit_solution(16140301902338043172)
XLA Ops:
  10.5 1.4 constant_dynamic-slice_fusion.3
  13.1 1.3 compare_reduce_fusion.1
  17.0 1.3 compare_reduce_fusion
  19.5 1.2 dynamic_slice.55
  22.7 38.8 %all-gather.3.cloned.1.call-done = bf16[8,1,2,256,256]{4,3,2,1,0:T(8,128)(2,1)} async-done(((bf16[1,1,2,256,256]{4,3,2,1,0:T(8,128)(2,1)}), bf16[8,1,2,256,256]{4,3,2,1,0:T(8,128)(2,1)}) %all-gather.3.cloned.1.call-update) | async-done | bytes 2097168 | tf_op jit(solution)/shard_map/all_gather | solution.py:123
  66.1 1.5 collective-permute-start.1
  67.6 1.4 collective-permute-start.2
  69.0 5.0 %collective-permute-done = f32[1,256,256]{2,1,0:T(8,128)S(1)} collective-permute-done((f32[1,256,256]{2,1,0:T(8,128)S(1)}, f32[1,256,256]{2,1,0:T(8,128)S(1)}, u32[]{:S(2)}, u32[]{:S(2)}) %collective-permute-start) | collective-permute-done | bytes 262176 | tf_op jit(solution)/shard_map/ppermute | solution.py:101
  74.0 2.0 collective-permute-done.1
  76.1 10.6 %collective-permute-done.2 = f32[1,256,256]{2,1,0:T(8,128)S(1)} collective-permute-done((f32[1,256,256]{2,1,0:T(8,128)S(1)}, f32[1,256,256]{2,1,0:T(8,128)S(1)}, u32[]{:S(2)}, u32[]{:S(2)}) %collective-permute-start.2) | collective-permute-done | bytes 262176 | tf_op jit(solution)/shard_map/ppermute | solution.py:101
  87.4 5.6 %all-gather.5.cloned.1.call-done = f32[2,4,256,256]{3,2,1,0:T(8,128)} async-done(((f32[2,1,256,256]{3,2,1,0:T(8,128)}), f32[2,4,256,256]{3,2,1,0:T(8,128)}) %all-gather.5.cloned.1.call-update) | async-done | bytes 2097168 | tf_op jit(solution)/shard_map/all_gather | solution.py:141
  93.0 164.9 %while.22 = (s32[]{:T(128)}, f32[256,256]{1,0:T(8,128)S(1)}, f32[256,256]{1,0:T(8,128)S(1)}, f32[256,256]{1,0:T(8,128)S(1)}, f32[256,256]{1,0:T(8,128)S(1)}, /*i...) while((s32[]{:T(128)}, f32[256,256]{1,0:T(8,128)S(1)}, ...), condition=%wide.region_3.4_spmd.clone, body=%wide.region_2.3_spmd.clone.sunk | while | flops 806813696 | bytes 12321098 | solution.py:170
  93.0 1.9 fusion.54
  95.0 49.3 %eval_jaxpr.8 = (f32[256,256]{1,0:T(8,128)}, f32[256,256]{1,0:T(8,128)}) custom-call(f32[256,256]{1,0:T(8,128)} %get-tuple-element.352.ar_ref, f32[256,256]{1,0:T(8,128)} %get-tuple-element.353.ai_ref), custom_call_target="tpu_custom_call" | custom-call | tf_op jit(solution)/shard_map/while/body/eval_jaxpr/pallas_call | solution.py:66
  144.5 1.3 fusion.57
  148.0 1.9 fusion.54
  149.9 49.3 %eval_jaxpr.8 = (f32[256,256]{1,0:T(8,128)}, f32[256,256]{1,0:T(8,128)}) custom-call(f32[256,256]{1,0:T(8,128)} %get-tuple-element.352.ar_ref, f32[256,256]{1,0:T(8,128)} %get-tuple-element.353.ai_ref), custom_call_target="tpu_custom_call" | custom-call | tf_op jit(solution)/shard_map/while/body/eval_jaxpr/pallas_call | solution.py:66
  199.4 1.3 fusion.57
  203.0 1.9 fusion.54
  204.9 49.3 %eval_jaxpr.8 = (f32[256,256]{1,0:T(8,128)}, f32[256,256]{1,0:T(8,128)}) custom-call(f32[256,256]{1,0:T(8,128)} %get-tuple-element.352.ar_ref, f32[256,256]{1,0:T(8,128)} %get-tuple-element.353.ai_ref), custom_call_target="tpu_custom_call" | custom-call | tf_op jit(solution)/shard_map/while/body/eval_jaxpr/pallas_call | solution.py:66
  254.4 1.3 fusion.57
  257.9 1.9 fusion.16
  259.9 49.3 %shard_map.73 = (f32[256,256]{1,0:T(8,128)}, f32[256,256]{1,0:T(8,128)}) custom-call(f32[256,256]{1,0:T(8,128)} %get-tuple-element.290.ar_ref, f32[256,256]{1,0:T(8,128)} %get-tuple-element.289.ai_ref), custom_call_target="tpu_custom_call" | custom-call | tf_op jit(solution)/shard_map/pallas_call | solution.py:66
  309.2 1.9 maximum_bitcast_fusion.1
  (63 shorter events, 14.7 us)
Async XLA Ops:
  6.5 55.0 %all-gather.3.cloned.1.call-start = ((), (), s32[]{:S(2)}) async-start(), calls=%async_computation | async-start | bytes 2359296 | tf_op jit(solution)/shard_map/all_gather | solution.py:123
  7.3 85.8 %all-gather.5.cloned.1.call-start = ((), (), s32[]{:S(2)}) async-start(), calls=%async_computation.1 | async-start | bytes 2621440 | tf_op jit(solution)/shard_map/all_gather | solution.py:141
  62.7 1.0 copy-start.1
  62.7 0.9 copy-start.3
  62.9 1.6 copy-start.2
  66.0 8.0 %collective-permute-start = (f32[1,256,256]{2,1,0:T(8,128)S(1)}, f32[1,256,256]{2,1,0:T(8,128)S(1)}, u32[]{:S(2)}, u32[]{:S(2)}) collective-permute-start(f32[1,256,256]{2,1,0:T(8,128)S(1)} %copy-done.2), channel_id=1, source_target_pairs={{0,1},{1,2},{2,3},{3,0},{4,5},{5,6},{6,7},{7,4},{8,9},{9,10},{10,1... | collective-permute-start | bytes 786440 | tf_op jit(solution)/shard_map/ppermute | solution.py:101
  66.1 10.0 %collective-permute-start.1 = (f32[1,256,256]{2,1,0:T(8,128)S(1)}, f32[1,256,256]{2,1,0:T(8,128)S(1)}, u32[]{:S(2)}, u32[]{:S(2)}) collective-permute-start(f32[1,256,256]{2,1,0:T(8,128)S(1)} %copy-done.2), channel_id=1, source_target_pairs={{0,2},{1,3},{2,0},{3,1},{4,6},{5,7},{6,4},{7,5},{8,10},{9,11},{10,... | collective-permute-start | bytes 786440 | tf_op jit(solution)/shard_map/ppermute | solution.py:101
  67.6 19.1 %collective-permute-start.2 = (f32[1,256,256]{2,1,0:T(8,128)S(1)}, f32[1,256,256]{2,1,0:T(8,128)S(1)}, u32[]{:S(2)}, u32[]{:S(2)}) collective-permute-start(f32[1,256,256]{2,1,0:T(8,128)S(1)} %copy-done.2), channel_id=1, source_target_pairs={{0,3},{1,0},{2,1},{3,2},{4,7},{5,4},{6,5},{7,6},{8,11},{9,8},{10,9... | collective-permute-start | bytes 786440 | tf_op jit(solution)/shard_map/ppermute | solution.py:101
  144.3 2.3 copy-start
  199.2 2.3 copy-start
  254.2 2.3 copy-start
Sparse Core Ops, SparseCore 0:
  9.5 51.9 all-gather.2
  66.1 26.8 all-gather.4

commit v13 on v11

--- a/solution.py
+++ b/solution.py
@@ -16,6 +16,7 @@
 lead_scale = 0.1
 
 HI = lax.Precision.HIGHEST
+LINK = lax.Precision.HIGH
 
 
 def symmetric(matrix):
@@ -159,10 +160,10 @@
             link_block = all_link[link_index]
             link_block = jnp.where(is_left, link_block, link_block.T)
             next_re = symmetric(
-                jnp.dot(link_block.T, jnp.dot(neg_re, link_block, precision=HI), precision=HI)
+                jnp.dot(link_block.T, jnp.dot(neg_re, link_block, precision=LINK), precision=LINK)
             )
             next_im = -symmetric(
-                jnp.dot(link_block.T, jnp.dot(neg_im, link_block, precision=HI), precision=HI)
+                jnp.dot(link_block.T, jnp.dot(neg_im, link_block, precision=LINK), precision=LINK)
             )
             left_re = jnp.where(is_left, next_re, left_re)
             left_im = jnp.where(is_left, next_im, left_im)

time: 313 us -> 311 us (level)
  no operation moved by 1% of the time
where the time goes in v13:
time: 311 us; the launch traced here: 310 us
  Pallas kernels  193 us (62%)
  waiting for transfers between devices  60.9 us (20%)
  between operations  21.7 us (7%)
  other arithmetic  16 us (5%)
  local copies, waits for them, and re-layouts  8.03 us (3%)
  matrix products  5.93 us (2%)
  starting transfers between devices  3.33 us (1%)
    pallas_call x4, Pallas kernels, neg_invert_pair(): pl.pallas_call(sweep_kernel, out_shape=(jax.ShapeDtypeStruct((n, n), jnp....  193 us
    all_gather x1, waiting for transfers between devices, body(): gathered = lax.all_gather(green_prev, 'energy', axis=0, tiled=True)  38.8 us
    ppermute x3, waiting for transfers between devices, gathered_over_dom(): pieces.append(lax.ppermute(array, 'dom', pairs))  15.8 us
    neg x4, other arithmetic, neg_invert_pair(): -block_im  7.77 us
  transfers between devices with their start and end apart: 5, of which 5 were waited for; matrix products, arithmetic and copies ran while one was open for 3% of the time, Pallas kernels for 0%

profile of v13, /device:TPU:0, one launch (start us, length us, event | category | flops | bytes accessed | tf_op | source)
XLA Modules:
  0.0 310.0 jit_solution(8018549692907036827)
XLA Ops:
  7.3 1.2 dynamic_slice.48
  10.5 1.4 constant_dynamic-slice_fusion.3
  14.4 1.3 compare_reduce_fusion.1
  17.0 1.3 compare_reduce_fusion
  19.5 1.2 dynamic_slice.49
  22.7 38.8 %all-gather.3.cloned.1.call-done = bf16[8,1,2,256,256]{4,3,2,1,0:T(8,128)(2,1)} async-done(((bf16[1,1,2,256,256]{4,3,2,1,0:T(8,128)(2,1)}), bf16[8,1,2,256,256]{4,3,2,1,0:T(8,128)(2,1)}) %all-gather.3.cloned.1.call-update) | async-done | bytes 2097168 | tf_op jit(solution)/shard_map/all_gather | solution.py:124
  61.5 1.1 constant_dynamic-slice_fusion.2
  65.1 0.8 pad_maximum_fusion
  66.0 1.5 collective-permute-start.1
  67.5 1.7 collective-permute-start.2
  69.3 6.8 %collective-permute-done.1 = f32[1,256,256]{2,1,0:T(8,128)S(1)} collective-permute-done((f32[1,256,256]{2,1,0:T(8,128)S(1)}, f32[1,256,256]{2,1,0:T(8,128)S(1)}, u32[]{:S(2)}, u32[]{:S(2)}) %collective-permute-start.1) | collective-permute-done | bytes 262176 | tf_op jit(solution)/shard_map/ppermute | solution.py:102
  76.2 1.9 collective-permute-done
  78.0 7.1 %collective-permute-done.2 = f32[1,256,256]{2,1,0:T(8,128)S(1)} collective-permute-done((f32[1,256,256]{2,1,0:T(8,128)S(1)}, f32[1,256,256]{2,1,0:T(8,128)S(1)}, u32[]{:S(2)}, u32[]{:S(2)}) %collective-permute-start.2) | collective-permute-done | bytes 262176 | tf_op jit(solution)/shard_map/ppermute | solution.py:102
  85.8 5.6 %all-gather.5.cloned.1.call-done = f32[2,4,256,256]{3,2,1,0:T(8,128)} async-done(((f32[2,1,256,256]{3,2,1,0:T(8,128)}), f32[2,4,256,256]{3,2,1,0:T(8,128)}) %all-gather.5.cloned.1.call-update) | async-done | bytes 2097168 | tf_op jit(solution)/shard_map/all_gather | solution.py:142
  91.4 209.9 %while.27 = (s32[]{:T(128)}, f32[256,256]{1,0:T(8,128)S(1)}, f32[256,256]{1,0:T(8,128)S(1)}, f32[256,256]{1,0:T(8,128)S(1)}, f32[256,256]{1,0:T(8,128)S(1)}, /*i...) while((s32[]{:T(128)}, f32[256,256]{1,0:T(8,128)S(1)}, ...), condition=%wide.region_3.4_spmd.clone.clone, body=%wide.region_2.3_spmd.clone.sunk.clone | while | flops 404422656 | bytes 13369702 | solution.py:175
  91.6 1.9 fusion.66
  93.5 48.4 %eval_jaxpr.8 = (f32[256,256]{1,0:T(8,128)S(1)}, f32[256,256]{1,0:T(8,128)S(1)}) custom-call(f32[256,256]{1,0:T(8,128)} %get-tuple-element.417.ar_ref, f32[256,256]{1,0:T(8,128)} %get-tuple-element.418.ai_ref), custom_call_target="tpu_custom_call" | custom-call | tf_op jit(solution)/shard_map/while/body/eval_jaxpr/pallas_call | solution.py:67
  144.1 1.9 fusion.66
  146.0 48.4 %eval_jaxpr.8 = (f32[256,256]{1,0:T(8,128)S(1)}, f32[256,256]{1,0:T(8,128)S(1)}) custom-call(f32[256,256]{1,0:T(8,128)} %get-tuple-element.417.ar_ref, f32[256,256]{1,0:T(8,128)} %get-tuple-element.418.ai_ref), custom_call_target="tpu_custom_call" | custom-call | tf_op jit(solution)/shard_map/while/body/eval_jaxpr/pallas_call | solution.py:67
  196.6 1.9 fusion.66
  198.5 48.4 %eval_jaxpr.8 = (f32[256,256]{1,0:T(8,128)S(1)}, f32[256,256]{1,0:T(8,128)S(1)}) custom-call(f32[256,256]{1,0:T(8,128)} %get-tuple-element.417.ar_ref, f32[256,256]{1,0:T(8,128)} %get-tuple-element.418.ai_ref), custom_call_target="tpu_custom_call" | custom-call | tf_op jit(solution)/shard_map/while/body/eval_jaxpr/pallas_call | solution.py:67
  249.1 1.9 fusion.66
  251.0 48.4 %eval_jaxpr.8 = (f32[256,256]{1,0:T(8,128)S(1)}, f32[256,256]{1,0:T(8,128)S(1)}) custom-call(f32[256,256]{1,0:T(8,128)} %get-tuple-element.417.ar_ref, f32[256,256]{1,0:T(8,128)} %get-tuple-element.418.ai_ref), custom_call_target="tpu_custom_call" | custom-call | tf_op jit(solution)/shard_map/while/body/eval_jaxpr/pallas_call | solution.py:67
  301.3 1.9 maximum_bitcast_fusion.1
  (85 shorter events, 12.7 us)
Async XLA Ops:
  6.5 55.0 %all-gather.3.cloned.1.call-start = ((), (), s32[]{:S(2)}) async-start(), calls=%async_computation | async-start | bytes 2359296 | tf_op jit(solution)/shard_map/all_gather | solution.py:124
  7.3 84.1 %all-gather.5.cloned.1.call-start = ((), (), s32[]{:S(2)}) async-start(), calls=%async_computation.1 | async-start | bytes 2621440 | tf_op jit(solution)/shard_map/all_gather | solution.py:142
  62.7 1.0 copy-start.2
  62.7 0.9 copy-start.4
  62.9 1.6 copy-start.3
  66.0 10.2 %collective-permute-start.1 = (f32[1,256,256]{2,1,0:T(8,128)S(1)}, f32[1,256,256]{2,1,0:T(8,128)S(1)}, u32[]{:S(2)}, u32[]{:S(2)}) collective-permute-start(f32[1,256,256]{2,1,0:T(8,128)S(1)} %copy-done.3), channel_id=1, source_target_pairs={{0,2},{1,3},{2,0},{3,1},{4,6},{5,7},{6,4},{7,5},{8,10},{9,11},{10,... | collective-permute-start | bytes 786440 | tf_op jit(solution)/shard_map/ppermute | solution.py:102
  67.5 10.5 %collective-permute-start = (f32[1,256,256]{2,1,0:T(8,128)S(1)}, f32[1,256,256]{2,1,0:T(8,128)S(1)}, u32[]{:S(2)}, u32[]{:S(2)}) collective-permute-start(f32[1,256,256]{2,1,0:T(8,128)S(1)} %copy-done.3), channel_id=1, source_target_pairs={{0,1},{1,2},{2,3},{3,0},{4,5},{5,6},{6,7},{7,4},{8,9},{9,10},{10,1... | collective-permute-start | bytes 786440 | tf_op jit(solution)/shard_map/ppermute | solution.py:102
  67.5 17.6 %collective-permute-start.2 = (f32[1,256,256]{2,1,0:T(8,128)S(1)}, f32[1,256,256]{2,1,0:T(8,128)S(1)}, u32[]{:S(2)}, u32[]{:S(2)}) collective-permute-start(f32[1,256,256]{2,1,0:T(8,128)S(1)} %copy-done.3), channel_id=1, source_target_pairs={{0,3},{1,0},{2,1},{3,2},{4,7},{5,4},{6,5},{7,6},{8,11},{9,8},{10,9... | collective-permute-start | bytes 786440 | tf_op jit(solution)/shard_map/ppermute | solution.py:102
  141.9 0.8 copy-start.1
  141.9 1.6 copy-start
  194.4 0.8 copy-start.1
  194.4 1.6 copy-start
  246.9 0.8 copy-start.1
  246.9 1.6 copy-start
  299.4 0.8 copy-start.1
  299.4 1.6 copy-start
Sparse Core Ops, SparseCore 0:
  9.5 51.9 all-gather.2
  66.1 25.2 all-gather.4
